TPU v7x, 128 devices: a whole 4x4x4 slice. The times are simulated.
128 devices in a mesh: ctx: 32 (over z, y_hi, x), ch: 4 (over y_lo, core).
Axes of the slice: x: 4, y: 4 (y_hi: 2, y_lo: 2; y = y_hi * 2 + y_lo), z: 4, core: 2. Of those that a mesh axis runs over, the one named last changes fastest.
Arguments:
- q_conv: bfloat16 [7168, 4096], P('ctx', 'ch'), may hold values from -6 to 6
- k_conv: bfloat16 [7168, 4096], P('ctx', 'ch'), may hold values from -6 to 6
- v_conv: bfloat16 [7168, 4096], P('ctx', 'ch'), may hold values from -6 to 6
- conv_filter: bfloat16 [7168, 256], P('ctx', 'ch'), may hold values from -1 to 1
- q_attn: bfloat16 [7168, 4096], P('ctx', 'ch'), may hold values from -5 to 5
- k_attn: bfloat16 [7168, 4096], P('ctx', 'ch'), may hold values from -5 to 5
- v_attn: bfloat16 [7168, 4096], P('ctx', 'ch'), may hold values from -6 to 6
- w_conv_out: bfloat16 [4096, 4096], P('ch'), may hold values from -0.09375 to 0.09375
- w_attn_out: bfloat16 [4096, 4096], P('ch'), may hold values from -0.375 to 0.375
Outputs:
- layer_out: bfloat16 [7168, 4096], P(('ctx', 'ch'))
All inputs are finite; a program needn't handle non-finite values.
Results may differ from a plain program's by a relative error of at most 0.018.
Values may be sent and summed in bfloat16 or wider, within the bound.
No kernel may reach another device: no remote copies, remote signals or barrier semaphores. Data moves between devices by JAX's collectives and lax.ppermute only.
A program may use at most 192 MiB of HBM per device.

v0:
```python
from functools import partial
import math

import jax
import jax.numpy as jnp
from jax import lax
from jax.sharding import PartitionSpec as P

HD = 128


two_pi = 2.0 * math.pi
neg_large = -1e30
highest = lax.Precision.HIGHEST


def angle_table(left_idx, right_idx, period):
    product = left_idx[:, None] * right_idx[None, :] % period
    return product.astype(jnp.float32) * (two_pi / period)


def section_coarse(values, cos_table, sin_table, twiddle):
    real_part = jnp.einsum("kn,nsc->ksc", cos_table, values, precision=highest)
    imag_part = -jnp.einsum("kn,nsc->ksc", sin_table, values, precision=highest)
    cos_twist = jnp.cos(twiddle)[:, :, None]
    sin_twist = jnp.sin(twiddle)[:, :, None]
    return (
        real_part * cos_twist + imag_part * sin_twist,
        imag_part * cos_twist - real_part * sin_twist,
    )


def section_fine(real_part, imag_part, cos_table, sin_table, direction):
    cos_real = jnp.einsum("kn,anc->akc", cos_table, real_part, precision=highest)
    cos_imag = jnp.einsum("kn,anc->akc", cos_table, imag_part, precision=highest)
    sin_real = jnp.einsum("kn,anc->akc", sin_table, real_part, precision=highest)
    sin_imag = jnp.einsum("kn,anc->akc", sin_table, imag_part, precision=highest)
    return (cos_real - direction * sin_imag, cos_imag + direction * sin_real)


def spectral_conv(gated, filters, my_index, tok_rows, count_ctx):
    chans = gated.shape[1]
    groups = filters.shape[1]
    share = chans // groups
    sub_rows = tok_rows // count_ctx
    period = 2 * count_ctx * tok_rows
    got_source, got_filter = (
        lax.all_to_all(
            gated.reshape(1, tok_rows, chans), "ctx", split_axis=1, concat_axis=0, tiled=True
        ),
        lax.all_to_all(
            filters.reshape(1, tok_rows, groups), "ctx", split_axis=1, concat_axis=0, tiled=True
        ),
    )
    coarse_idx = jnp.arange(count_ctx, dtype=jnp.int32)
    coarse_freq = jnp.arange(2 * count_ctx, dtype=jnp.int32)
    coarse_angle = angle_table(coarse_freq, coarse_idx, 2 * count_ctx)
    cos_coarse = jnp.cos(coarse_angle)
    sin_coarse = jnp.sin(coarse_angle)
    fine_global = my_index * sub_rows + jnp.arange(sub_rows, dtype=jnp.int32)
    twist_in = angle_table(coarse_freq, fine_global, period)
    source_re, source_im = section_coarse(
        got_source.astype(jnp.float32), cos_coarse, sin_coarse, twist_in
    )
    filter_re, filter_im = section_coarse(
        got_filter.astype(jnp.float32), cos_coarse, sin_coarse, twist_in
    )
    source_re, source_im, filter_re, filter_im = (
        lax.all_to_all(
            source_re.astype(jnp.bfloat16), "ctx", split_axis=0, concat_axis=1, tiled=True
        ).astype(source_re.dtype),
        lax.all_to_all(
            source_im.astype(jnp.bfloat16), "ctx", split_axis=0, concat_axis=1, tiled=True
        ).astype(source_im.dtype),
        lax.all_to_all(
            filter_re.astype(jnp.bfloat16), "ctx", split_axis=0, concat_axis=1, tiled=True
        ).astype(filter_re.dtype),
        lax.all_to_all(
            filter_im.astype(jnp.bfloat16), "ctx", split_axis=0, concat_axis=1, tiled=True
        ).astype(filter_im.dtype),
    )
    fine_idx = jnp.arange(tok_rows, dtype=jnp.int32)
    fine_angle = angle_table(fine_idx, fine_idx, tok_rows)
    cos_fine = jnp.cos(fine_angle)
    sin_fine = jnp.sin(fine_angle)
    source_re, source_im = section_fine(source_re, source_im, cos_fine, sin_fine, -1.0)
    filter_re, filter_im = section_fine(filter_re, filter_im, cos_fine, sin_fine, -1.0)
    split_re = source_re.reshape(2, tok_rows, groups, share)
    split_im = source_im.reshape(2, tok_rows, groups, share)
    prod_re = split_re * filter_re[..., None] - split_im * filter_im[..., None]
    prod_im = split_re * filter_im[..., None] + split_im * filter_re[..., None]
    back_re, back_im = section_fine(
        prod_re.reshape(2, tok_rows, chans),
        prod_im.reshape(2, tok_rows, chans),
        cos_fine,
        sin_fine,
        1.0,
    )
    pair_freq = my_index * 2 + jnp.arange(2, dtype=jnp.int32)
    twist_out = angle_table(pair_freq, fine_idx, period)
    cos_out = jnp.cos(twist_out)[:, :, None]
    sin_out = jnp.sin(twist_out)[:, :, None]
    turned_re = back_re * cos_out - back_im * sin_out
    turned_im = back_re * sin_out + back_im * cos_out
    turned_re, turned_im = (
        lax.all_to_all(
            turned_re.astype(jnp.bfloat16), "ctx", split_axis=1, concat_axis=0, tiled=True
        ).astype(turned_re.dtype),
        lax.all_to_all(
            turned_im.astype(jnp.bfloat16), "ctx", split_axis=1, concat_axis=0, tiled=True
        ).astype(turned_im.dtype),
    )
    result = jnp.einsum("nk,ksc->nsc", cos_coarse.T, turned_re, precision=highest)
    result = result - jnp.einsum("nk,ksc->nsc", sin_coarse.T, turned_im, precision=highest)
    rounded = (result / period).astype(jnp.bfloat16)
    returned = lax.all_to_all(rounded, "ctx", split_axis=0, concat_axis=1, tiled=True)
    return returned.reshape(tok_rows, chans)


def keep_same(running):
    return running


def attend_block(group_query, group_pos, key_block, value_block, key_pos, score_scale, group_state):
    run_max, run_total, run_accum = group_state
    scores = (
        jnp.einsum("thd,shd->hts", group_query, key_block, preferred_element_type=jnp.float32)
        * score_scale
    )
    allowed = (key_pos[None, :] <= group_pos[:, None])[None]
    block_max = jnp.max(jnp.where(allowed, scores, neg_large), axis=2)
    new_max = jnp.maximum(run_max, block_max)
    factor = jnp.exp(run_max - new_max)
    weights = jnp.where(allowed, jnp.exp(scores - new_max[:, :, None]), 0.0)
    new_total = run_total * factor + jnp.sum(weights, axis=2)
    new_accum = run_accum * factor[:, :, None] + jnp.einsum(
        "hts,shd->htd",
        weights.astype(jnp.bfloat16),
        value_block,
        preferred_element_type=jnp.float32,
    )
    return (new_max, new_total, new_accum)


def attention(q_attn, k_attn, v_attn, my_index, tok_rows):
    heads_local = q_attn.shape[1] // HD
    score_scale = HD ** (-0.5)
    queries = q_attn.reshape(tok_rows, heads_local, HD)
    group_list = [(queries, my_index * tok_rows + jnp.arange(tok_rows, dtype=jnp.int32))]
    initial = tuple(
        (
            (
                jnp.full((heads_local, entry[0].shape[0]), neg_large, jnp.float32),
                jnp.zeros((heads_local, entry[0].shape[0]), jnp.float32),
                jnp.zeros((heads_local, entry[0].shape[0], HD), jnp.float32),
            )
            for entry in group_list
        )
    )
    key_piece = lax.all_gather(k_attn, "ctx", axis=0, tiled=True)
    value_piece = lax.all_gather(v_attn, "ctx", axis=0, tiled=True)
    count_blocks = key_piece.shape[0] // tok_rows
    keys_split = key_piece.reshape(count_blocks, tok_rows, heads_local, HD)
    values_split = value_piece.reshape(count_blocks, tok_rows, heads_local, HD)

    def one_block(carry, item):
        key_block, value_block, block_number = item
        block_first = block_number * tok_rows
        key_pos = block_first + jnp.arange(tok_rows, dtype=jnp.int32)
        updated = []
        for entry, group_state in zip(group_list, carry):
            step_fn = partial(
                attend_block, entry[0], entry[1], key_block, value_block, key_pos, score_scale
            )
            updated.append(lax.cond(block_first <= entry[1][-1], step_fn, keep_same, group_state))
        return (tuple(updated), None)

    new_state, unused = lax.scan(
        one_block, initial, (keys_split, values_split, jnp.arange(count_blocks, dtype=jnp.int32))
    )
    outputs = [
        (state[2] / state[1][:, :, None]).transpose(1, 0, 2).astype(jnp.bfloat16)
        for state in new_state
    ]
    merged = outputs[0]
    return merged.reshape(tok_rows, heads_local * HD)


def local(q_conv, k_conv, v_conv, conv_filter, q_attn, k_attn, v_attn, w_conv_out, w_attn_out):
    count_ctx = lax.axis_size("ctx")
    my_index = lax.axis_index("ctx")
    tok_rows = q_conv.shape[0]
    gated = (k_conv.astype(jnp.float32) * v_conv.astype(jnp.float32)).astype(jnp.bfloat16)
    conv = spectral_conv(gated, conv_filter, my_index, tok_rows, count_ctx)
    mixed = (q_conv.astype(jnp.float32) * conv.astype(jnp.float32)).astype(jnp.bfloat16)
    attended = attention(q_attn, k_attn, v_attn, my_index, tok_rows)
    return lax.psum_scatter(
        (
            jnp.dot(mixed, w_conv_out, preferred_element_type=jnp.float32)
            + jnp.dot(attended, w_attn_out, preferred_element_type=jnp.float32)
        ).astype(jnp.bfloat16),
        "ch",
        scatter_dimension=0,
        tiled=True,
    )


def solution(mesh):
    return jax.shard_map(
        local,
        mesh=mesh,
        in_specs=(
            P("ctx", "ch"),
            P("ctx", "ch"),
            P("ctx", "ch"),
            P("ctx", "ch"),
            P("ctx", "ch"),
            P("ctx", "ch"),
            P("ctx", "ch"),
            P("ch", None),
            P("ch", None),
        ),
        out_specs=P(("ctx", "ch"), None),
        check_vma=False,
    )
```

profile of v0, /device:TPU:1, one launch (start us, length us, event | category | flops | bytes accessed | tf_op | source)
XLA Modules:
  0.0 611.6 jit_solution(7817200553837334792)
XLA Ops:
  11.1 11.3 %all-to-all-start.3 = ((bf16[32,2,224]{2,1,0:T(2,128)(2,1)}), bf16[32,2,224]{2,1,0:T(2,128)(2,1)S(1)}, u32[]{:S(2)}, u32[]{:S(2)}) async-start(bf16[32,2,224]{2,1,0:T(2,128)(2,1)} %reshape.188), calls=%async_computation.3 | async-start | bytes 65536 | tf_op jit(solution)/shard_map/all_to_all | solution.py:51
  31.3 7.0 %all-to-all-start = ((bf16[32,2,3584]{2,1,0:T(2,128)(2,1)}), bf16[32,2,3584]{2,1,0:T(2,128)(2,1)S(1)}, u32[]{:S(2)}, u32[]{:S(2)}) async-start(bf16[32,2,3584]{2,1,0:T(2,128)(2,1)} %reshape.194), calls=%async_computation | async-start | bytes 917504 | tf_op jit(solution)/shard_map/all_to_all | solution.py:48
  41.2 7.5 %all-to-all-done = bf16[32,2,3584]{2,1,0:T(2,128)(2,1)S(1)} async-done(((bf16[32,2,3584]{2,1,0:T(2,128)(2,1)}), bf16[32,2,3584]{2,1,0:T(2,128)(2,1)S(1)}, u32[]{:S(2)}, u32[]{:S(2)}) %all-to-all-start) | async-done | bytes 458784 | tf_op jit(solution)/shard_map/all_to_all | solution.py:48
  48.7 4.4 all-to-all-start.5
  57.7 5.0 all-to-all-done.5
  62.7 4.3 all-to-all-start.4
  71.2 5.3 all-to-all-done.4
  83.0 19.3 %all-to-all-done.1 = bf16[64,7,1024]{2,1,0:T(8,128)(2,1)S(1)} async-done(((bf16[64,7,1024]{2,1,0:T(8,128)(2,1)}), bf16[64,7,1024]{2,1,0:T(8,128)(2,1)S(1)}, u32[]{:S(2)}, u32[]{:S(2)}) %all-to-all-start.1) | async-done | bytes 917536 | tf_op jit(solution)/shard_map/all_to_all | solution.py:69
  102.2 5.0 all-to-all-start.2
  118.6 6.3 %all-to-all-done.2 = bf16[64,7,1024]{2,1,0:T(8,128)(2,1)} async-done(((bf16[64,7,1024]{2,1,0:T(8,128)(2,1)}), bf16[64,7,1024]{2,1,0:T(8,128)(2,1)}, u32[]{:S(2)}, u32[]{:S(2)}) %all-to-all-start.2) | async-done | bytes 917536 | tf_op jit(solution)/shard_map/all_to_all | solution.py:72
  155.4 10.4 %all-to-all-done.7 = bf16[2,224,1024]{2,0,1:T(2,128)(2,1)S(1)} async-done(((bf16[2,224,1024]{2,0,1:T(2,128)(2,1)}), bf16[2,224,1024]{2,0,1:T(2,128)(2,1)S(1)}, u32[]{:S(2)}, u32[]{:S(2)}) %all-to-all-start.7) | async-done | bytes 917536 | tf_op jit(solution)/shard_map/all_to_all | solution.py:109
  165.8 6.0 all-to-all-start.6
  172.7 19.2 %all-to-all-done.6 = bf16[2,224,1024]{2,0,1:T(2,128)(2,1)S(1)} async-done(((bf16[2,224,1024]{2,0,1:T(2,128)(2,1)}), bf16[2,224,1024]{2,0,1:T(2,128)(2,1)S(1)}, u32[]{:S(2)}, u32[]{:S(2)}) %all-to-all-start.6) | async-done | bytes 917536 | tf_op jit(solution)/shard_map/all_to_all | solution.py:106
  195.3 5.5 all-to-all-start.8
  201.0 10.9 %all-to-all-done.8 = bf16[32,7,1024]{2,1,0:T(8,128)(2,1)S(1)} async-done(((bf16[32,7,1024]{2,1,0:T(8,128)(2,1)}), bf16[32,7,1024]{2,1,0:T(8,128)(2,1)S(1)}, u32[]{:S(2)}, u32[]{:S(2)}) %all-to-all-start.8) | async-done | bytes 458784 | tf_op jit(solution)/shard_map/all_to_all | solution.py:116
  212.0 7.3 %fusion.37 = f32[224,4096]{1,0:T(8,128)} fusion(bf16[1024,4096]{1,0:T(8,128)(2,1)} %param.20, f32[224,1024]{1,0:T(8,128)S(1)} %reshape.181, bf16[224,1024]{1,0:T(8,128)(2,1)S(1)} %copy-done.6), kind=kOutput, calls=%fused_computation.63 | convolution fusion | flops 1879736320 | bytes 13434880 | tf_op jit(solution)/shard_map/dot_general | solution.py:199
  219.3 9.2 %copy.126 = bf16[896,8,8,128]{3,2,1,0:T(8,128)(2,1)S(1)} copy(bf16[896,8,8,128]{3,1,2,0:T(8,128)(2,1)} %bitcast.171) | data formatting | bytes 29360128
  228.6 7.3 %copy.117 = bf16[32,224,8,128]{3,1,2,0:T(8,128)(2,1)} copy(bf16[32,224,8,128]{3,2,1,0:T(8,128)(2,1)S(1)} %bitcast.169) | data formatting | bytes 29360128 | tf_op jit(solution)/shard_map/while | solution.py:178
  235.9 97.1 %all-gather.5.cloned.1.call-done = bf16[7168,1024]{1,0:T(8,128)(2,1)} async-done(((bf16[224,1024]{1,0:T(8,128)(2,1)}), bf16[7168,1024]{1,0:T(8,128)(2,1)}) %all-gather.5.cloned.1.call-update) | async-done | bytes 14680080 | tf_op jit(solution)/shard_map/all_gather | solution.py:161
  333.0 9.1 %copy.127 = bf16[896,8,8,128]{3,2,1,0:T(8,128)(2,1)S(1)} copy(bf16[896,8,8,128]{3,1,2,0:T(8,128)(2,1)} %bitcast.172) | data formatting | bytes 29360128
  342.1 7.3 %copy.119 = bf16[32,224,8,128]{3,1,2,0:T(8,128)(2,1)} copy(bf16[32,224,8,128]{3,2,1,0:T(8,128)(2,1)S(1)} %bitcast.170) | data formatting | bytes 29360128 | tf_op jit(solution)/shard_map/while | solution.py:178
  349.5 92.0 %while.14 = (s32[]{:T(128)}, f32[8,224]{1,0:T(8,128)S(1)}, f32[8,224]{1,0:T(8,128)S(1)}, f32[8,224,128]{2,1,0:T(8,128)S(1)}, s32[32]{0:T(128)S(1)}, /*index=5*/s...) while((s32[]{:T(128)}, f32[8,224]{1,0:T(8,128)S(1)}, ...), condition=%wide.region_5.6_spmd, body=%wide.region_0.5_spmd.sunk | while | flops 210449120 | bytes 8349359 | solution.py:178
  441.5 7.9 %fusion.19 = bf16[224,4096]{1,0:T(8,128)(2,1)} fusion(f32[224,4096]{1,0:T(8,128)} %fusion.37, bf16[1024,4096]{1,0:T(8,128)(2,1)} %param.21, f32[8,224,128]{2,1,0:T(8,128)S(1)} %get-tuple-element.145, f32[8,224]{1,0:T(8,128)S(1)} %get-tuple-element.146), kind=kOutput, calls=%fused_computation.26 | convolution fusion | flops 1881341952 | bytes 14818304 | tf_op jit(solution)/shard_map/dot_general | solution.py:200
  449.4 155.4 %reduce-scatter.2.cloned.1.call-done = bf16[56,4096]{1,0:T(8,128)(2,1)} async-done(((bf16[224,4096]{1,0:T(8,128)(2,1)}), bf16[56,4096]{1,0:T(8,128)(2,1)}) %reduce-scatter.2.cloned.1.call-update) | async-done | bytes 458768 | tf_op jit(solution)/shard_map/reduce_scatter | solution.py:197
  (228 shorter events, 128.7 us)
Async XLA Ops:
  6.5 194.3 %copy-start = (bf16[224,1024]{1,0:T(8,128)(2,1)S(1)}, bf16[224,1024]{1,0:T(8,128)(2,1)}, u32[]{:S(2)}) copy-start(bf16[224,1024]{1,0:T(8,128)(2,1)} %param.17) | copy-start | bytes 1376260
  6.5 212.8 %all-gather.3.cloned.1.call-start = ((), (), s32[]{:S(2)}) async-start(), calls=%async_computation.10 | async-start | bytes 15138816 | tf_op jit(solution)/shard_map/all_gather | solution.py:160
  7.3 325.7 %all-gather.5.cloned.1.call-start = ((), (), s32[]{:S(2)}) async-start(), calls=%async_computation.11 | async-start | bytes 15138816 | tf_op jit(solution)/shard_map/all_gather | solution.py:161
  11.1 20.2 %all-to-all-start.3 = ((bf16[32,2,224]{2,1,0:T(2,128)(2,1)}), bf16[32,2,224]{2,1,0:T(2,128)(2,1)S(1)}, u32[]{:S(2)}, u32[]{:S(2)}) async-start(bf16[32,2,224]{2,1,0:T(2,128)(2,1)} %reshape.188), calls=%async_computation.3 | async-start | bytes 65536 | tf_op jit(solution)/shard_map/all_to_all | solution.py:51
  31.3 17.5 %all-to-all-start = ((bf16[32,2,3584]{2,1,0:T(2,128)(2,1)}), bf16[32,2,3584]{2,1,0:T(2,128)(2,1)S(1)}, u32[]{:S(2)}, u32[]{:S(2)}) async-start(bf16[32,2,3584]{2,1,0:T(2,128)(2,1)} %reshape.194), calls=%async_computation | async-start | bytes 917504 | tf_op jit(solution)/shard_map/all_to_all | solution.py:48
  48.7 14.0 %all-to-all-start.5 = ((bf16[32,2,448]{2,1,0:T(2,128)(2,1)}), bf16[32,2,448]{2,1,0:T(2,128)(2,1)S(1)}, u32[]{:S(2)}, u32[]{:S(2)}) async-start(bf16[32,2,448]{2,1,0:T(2,128)(2,1)} %reshape.192), calls=%async_computation.5 | async-start | bytes 131072 | tf_op jit(solution)/shard_map/all_to_all | solution.py:78
  62.7 13.8 %all-to-all-start.4 = ((bf16[32,2,448]{2,1,0:T(2,128)(2,1)}), bf16[32,2,448]{2,1,0:T(2,128)(2,1)S(1)}, u32[]{:S(2)}, u32[]{:S(2)}) async-start(bf16[32,2,448]{2,1,0:T(2,128)(2,1)} %reshape.190), calls=%async_computation.4 | async-start | bytes 131072 | tf_op jit(solution)/shard_map/all_to_all | solution.py:75
  71.2 10.2 %copy-start.5 = (bf16[64,7,1024]{2,0,1:T(8,128)(2,1)S(1)}, bf16[64,7,1024]{2,0,1:T(8,128)(2,1)}, u32[]{:S(2)}) copy-start(bf16[64,7,1024]{2,0,1:T(8,128)(2,1)} %get-tuple-element.199) | copy-start | bytes 2752516
  76.5 25.7 %all-to-all-start.1 = ((bf16[64,7,1024]{2,1,0:T(8,128)(2,1)}), bf16[64,7,1024]{2,1,0:T(8,128)(2,1)S(1)}, u32[]{:S(2)}, u32[]{:S(2)}) async-start(bf16[64,7,1024]{2,1,0:T(8,128)(2,1)} %copy.89), calls=%async_computation.1 | async-start | bytes 2097152 | tf_op jit(solution)/shard_map/all_to_all | solution.py:69
  102.2 6.2 %copy-start.4 = (bf16[64,7,1024]{2,1,0:T(8,128)(2,1)}, bf16[64,7,1024]{2,1,0:T(8,128)(2,1)S(1)}, u32[]{:S(2)}) copy-start(bf16[64,7,1024]{2,1,0:T(8,128)(2,1)S(1)} %all-to-all-done.1) | copy-start | bytes 2752516
  102.2 22.6 %all-to-all-start.2 = ((bf16[64,7,1024]{2,1,0:T(8,128)(2,1)}), bf16[64,7,1024]{2,1,0:T(8,128)(2,1)}, u32[]{:S(2)}, u32[]{:S(2)}) async-start(bf16[64,7,1024]{2,1,0:T(8,128)(2,1)} %copy.92), calls=%async_computation.2 | async-start | bytes 2097152 | tf_op jit(solution)/shard_map/all_to_all | solution.py:72
  130.8 2.0 copy-start.2
  130.8 2.0 copy-start.3
  149.3 16.5 %all-to-all-start.7 = ((bf16[2,224,1024]{2,0,1:T(2,128)(2,1)}), bf16[2,224,1024]{2,0,1:T(2,128)(2,1)S(1)}, u32[]{:S(2)}, u32[]{:S(2)}) async-start(bf16[2,224,1024]{2,0,1:T(2,128)(2,1)} %copy.114), calls=%async_computation.7 | async-start | bytes 1835008 | tf_op jit(solution)/shard_map/all_to_all | solution.py:109
  165.8 26.2 %all-to-all-start.6 = ((bf16[2,224,1024]{2,0,1:T(2,128)(2,1)}), bf16[2,224,1024]{2,0,1:T(2,128)(2,1)S(1)}, u32[]{:S(2)}, u32[]{:S(2)}) async-start(bf16[2,224,1024]{2,0,1:T(2,128)(2,1)} %copy.112), calls=%async_computation.6 | async-start | bytes 1835008 | tf_op jit(solution)/shard_map/all_to_all | solution.py:106
  195.3 16.7 %copy-start.6 = (bf16[224,1024]{1,0:T(8,128)(2,1)S(1)}, bf16[224,1024]{1,0:T(8,128)(2,1)}, u32[]{:S(2)}) copy-start(bf16[224,1024]{1,0:T(8,128)(2,1)} %param.13) | copy-start | bytes 1376260
  195.3 16.6 %all-to-all-start.8 = ((bf16[32,7,1024]{2,1,0:T(8,128)(2,1)}), bf16[32,7,1024]{2,1,0:T(8,128)(2,1)S(1)}, u32[]{:S(2)}, u32[]{:S(2)}) async-start(bf16[32,7,1024]{2,1,0:T(8,128)(2,1)} %copy.116), calls=%async_computation.8 | async-start | bytes 1048576 | tf_op jit(solution)/shard_map/all_to_all | solution.py:116
  200.8 404.0 %reduce-scatter.2.cloned.1.call-start = ((), (), s32[]{:S(2)}) async-start(), calls=%async_computation.12 | async-start | bytes 2293760 | tf_op jit(solution)/shard_map/reduce_scatter | solution.py:197
  441.5 163.3 %copy-start.1 = (bf16[224,1024]{1,0:T(8,128)(2,1)S(1)}, bf16[224,1024]{1,0:T(8,128)(2,1)}, u32[]{:S(2)}) copy-start(bf16[224,1024]{1,0:T(8,128)(2,1)} %param.17) | copy-start | bytes 1376260
Sparse Core Ops, SparseCore 0:
  10.4 179.5 all-gather.2
  193.1 139.8 all-gather.4
  449.5 155.2 reduce-scatter.1
where the time goes:
time: 622 us; the launch traced here: 612 us
  waiting for transfers between devices  340 us (55%)
  local copies, waits for them, and re-layouts  104 us (17%)
  starting transfers between devices  51.9 us (8%)
  matrix products  49.7 us (8%)
  loops' own time  45.7 us (7%)
  between operations  13.9 us (2%)
  other arithmetic  6.44 us (1%)
    reduce_scatter x1, waiting for transfers between devices, local(): lax.psum_scatter((jnp.dot(mixed, w_conv_out, preferred_element_type=jnp.f...  155 us
    all_gather x1, waiting for transfers between devices, attention(): value_piece = lax.all_gather(v_attn, 'ctx', axis=0, tiled=True)  97.1 us
    another operation x1, loops' own time, attention(): lax.scan(one_block, initial, (keys_split, values_split, jnp.arange(count_...  45.1 us
    unnamed x25, local copies, waits for them, and re-layouts  23 us
    dynamic_slice x32, local copies, waits for them, and re-layouts, attention(): lax.scan(one_block, initial, (keys_split, values_split, jnp.arange(count_...  21.2 us
    slice x32, local copies, waits for them, and re-layouts, one_block(): entry[1][-1]  20.8 us
    all_to_all x1, waiting for transfers between devices, spectral_conv(): lax.all_to_all(source_re.astype(jnp.bfloat16), 'ctx', split_axis=0, conca...  19.3 us
    all_to_all x1, waiting for transfers between devices, spectral_conv(): lax.all_to_all(turned_re.astype(jnp.bfloat16), 'ctx', split_axis=1, conca...  19.2 us
  transfers between devices with their start and end apart: 12, of which 11 were waited for; matrix products, arithmetic and copies ran while one was open for 14% of the time, Pallas kernels for 0%

commit v1 on v0

--- a/solution.py
+++ b/solution.py
@@ -5,6 +5,8 @@
 import jax.numpy as jnp
 from jax import lax
 from jax.sharding import PartitionSpec as P
+from jax.experimental import pallas as pl
+from jax.experimental.pallas import tpu as pltpu
 
 HD = 128
 
@@ -117,73 +119,110 @@
     return returned.reshape(tok_rows, chans)
 
 
-def keep_same(running):
-    return running
-
-
-def attend_block(group_query, group_pos, key_block, value_block, key_pos, score_scale, group_state):
-    run_max, run_total, run_accum = group_state
-    scores = (
-        jnp.einsum("thd,shd->hts", group_query, key_block, preferred_element_type=jnp.float32)
-        * score_scale
-    )
-    allowed = (key_pos[None, :] <= group_pos[:, None])[None]
-    block_max = jnp.max(jnp.where(allowed, scores, neg_large), axis=2)
-    new_max = jnp.maximum(run_max, block_max)
-    factor = jnp.exp(run_max - new_max)
-    weights = jnp.where(allowed, jnp.exp(scores - new_max[:, :, None]), 0.0)
-    new_total = run_total * factor + jnp.sum(weights, axis=2)
-    new_accum = run_accum * factor[:, :, None] + jnp.einsum(
-        "hts,shd->htd",
-        weights.astype(jnp.bfloat16),
-        value_block,
-        preferred_element_type=jnp.float32,
-    )
-    return (new_max, new_total, new_accum)
+KEY_BLOCK = 1024
+
+
+def flash_kernel(info_ref, q_ref, k_ref, v_ref, o_ref, m_sc, l_sc, acc_sc, *, heads, tok_rows, key_block, scale):
+    j = pl.program_id(0)
+    q_first = info_ref[0] * tok_rows
+    last_block = info_ref[1] - 1
+    key_first = j * key_block
+
+    @pl.when(j == 0)
+    def _():
+        m_sc[...] = jnp.full_like(m_sc, neg_large)
+        l_sc[...] = jnp.zeros_like(l_sc)
+        acc_sc[...] = jnp.zeros_like(acc_sc)
+
+    def step(masked):
+        if masked:
+            query_pos = q_first + lax.broadcasted_iota(jnp.int32, (tok_rows, key_block), 0)
+            key_pos = key_first + lax.broadcasted_iota(jnp.int32, (tok_rows, key_block), 1)
+            allowed = key_pos <= query_pos
+        for h in range(heads):
+            cols = slice(h * HD, (h + 1) * HD)
+            scores = lax.dot_general(
+                q_ref[:, cols], k_ref[:, cols], (((1,), (1,)), ((), ())),
+                preferred_element_type=jnp.float32,
+            ) * scale
+            if masked:
+                scores = jnp.where(allowed, scores, neg_large)
+            m_prev = m_sc[h]
+            m_new = jnp.maximum(m_prev, jnp.max(scores, axis=1, keepdims=True))
+            weights = jnp.exp(scores - m_new)
+            if masked:
+                weights = jnp.where(allowed, weights, 0.0)
+            factor = jnp.exp(m_prev - m_new)
+            l_sc[h] = l_sc[h] * factor + jnp.sum(weights, axis=1, keepdims=True)
+            acc_sc[:, cols] = acc_sc[:, cols] * factor + jnp.dot(
+                weights.astype(jnp.bfloat16), v_ref[:, cols], preferred_element_type=jnp.float32
+            )
+            m_sc[h] = m_new
+
+    full = key_first + key_block <= q_first
+
+    @pl.when(jnp.logical_and(j <= last_block, full))
+    def _():
+        step(False)
+
+    @pl.when(jnp.logical_and(j <= last_block, jnp.logical_not(full)))
+    def _():
+        step(True)
+
+    @pl.when(j == last_block)
+    def _():
+        for h in range(heads):
+            cols = slice(h * HD, (h + 1) * HD)
+            o_ref[:, cols] = (acc_sc[:, cols] / l_sc[h]).astype(o_ref.dtype)
 
 
 def attention(q_attn, k_attn, v_attn, my_index, tok_rows):
-    heads_local = q_attn.shape[1] // HD
-    score_scale = HD ** (-0.5)
-    queries = q_attn.reshape(tok_rows, heads_local, HD)
-    group_list = [(queries, my_index * tok_rows + jnp.arange(tok_rows, dtype=jnp.int32))]
-    initial = tuple(
-        (
-            (
-                jnp.full((heads_local, entry[0].shape[0]), neg_large, jnp.float32),
-                jnp.zeros((heads_local, entry[0].shape[0]), jnp.float32),
-                jnp.zeros((heads_local, entry[0].shape[0], HD), jnp.float32),
-            )
-            for entry in group_list
-        )
-    )
+    width = q_attn.shape[1]
+    heads_local = width // HD
     key_piece = lax.all_gather(k_attn, "ctx", axis=0, tiled=True)
     value_piece = lax.all_gather(v_attn, "ctx", axis=0, tiled=True)
-    count_blocks = key_piece.shape[0] // tok_rows
-    keys_split = key_piece.reshape(count_blocks, tok_rows, heads_local, HD)
-    values_split = value_piece.reshape(count_blocks, tok_rows, heads_local, HD)
-
-    def one_block(carry, item):
-        key_block, value_block, block_number = item
-        block_first = block_number * tok_rows
-        key_pos = block_first + jnp.arange(tok_rows, dtype=jnp.int32)
-        updated = []
-        for entry, group_state in zip(group_list, carry):
-            step_fn = partial(
-                attend_block, entry[0], entry[1], key_block, value_block, key_pos, score_scale
-            )
-            updated.append(lax.cond(block_first <= entry[1][-1], step_fn, keep_same, group_state))
-        return (tuple(updated), None)
-
-    new_state, unused = lax.scan(
-        one_block, initial, (keys_split, values_split, jnp.arange(count_blocks, dtype=jnp.int32))
-    )
-    outputs = [
-        (state[2] / state[1][:, :, None]).transpose(1, 0, 2).astype(jnp.bfloat16)
-        for state in new_state
-    ]
-    merged = outputs[0]
-    return merged.reshape(tok_rows, heads_local * HD)
+    return attention_core(q_attn, key_piece, value_piece, my_index, tok_rows)
+
+
+def attention_core(q_attn, key_piece, value_piece, my_index, tok_rows):
+    width = q_attn.shape[1]
+    heads_local = width // HD
+    total_rows = key_piece.shape[0]
+    key_block = KEY_BLOCK if total_rows % KEY_BLOCK == 0 else tok_rows
+    count_blocks = total_rows // key_block
+    needed = ((my_index + 1) * tok_rows + key_block - 1) // key_block
+    info = jnp.stack([my_index, needed]).astype(jnp.int32)
+    kernel = partial(
+        flash_kernel, heads=heads_local, tok_rows=tok_rows, key_block=key_block, scale=HD ** (-0.5)
+    )
+    kv_spec = pl.BlockSpec((key_block, width), lambda j, info: (jnp.minimum(j, info[1] - 1), 0))
+    return pl.pallas_call(
+        kernel,
+        out_shape=jax.ShapeDtypeStruct((tok_rows, width), jnp.bfloat16),
+        grid_spec=pltpu.PrefetchScalarGridSpec(
+            num_scalar_prefetch=1,
+            grid=(count_blocks,),
+            in_specs=[
+                pl.BlockSpec((tok_rows, width), lambda j, info: (0, 0)),
+                kv_spec,
+                kv_spec,
+            ],
+            out_specs=pl.BlockSpec((tok_rows, width), lambda j, info: (0, 0)),
+            scratch_shapes=[
+                pltpu.VMEM((heads_local, tok_rows, 1), jnp.float32),
+                pltpu.VMEM((heads_local, tok_rows, 1), jnp.float32),
+                pltpu.VMEM((tok_rows, width), jnp.float32),
+            ],
+        ),
+        compiler_params=pltpu.CompilerParams(
+            dimension_semantics=("arbitrary",), vmem_limit_bytes=48 * 1024 * 1024
+        ),
+        cost_estimate=pl.CostEstimate(
+            flops=4 * tok_rows * total_rows * width,
+            transcendentals=heads_local * tok_rows * total_rows,
+            bytes_accessed=2 * total_rows * width * 2 + 2 * tok_rows * width * 2,
+        ),
+    )(info, q_attn, key_piece, value_piece)
 
 
 def local(q_conv, k_conv, v_conv, conv_filter, q_attn, k_attn, v_attn, w_conv_out, w_attn_out):

time: 622 us -> 416 us (0.67)
  waiting for transfers between devices: 340 us -> 256 us
  local copies, waits for them, and re-layouts: 104 us -> 27.6 us
  loops' own time: 45.7 us -> 0 us
  Pallas kernels: 0 us -> 9.3 us
    reduce_scatter x1, waiting for transfers between devices: 155 us -> 53.3 us  [local(): lax.psum_scatter((jnp.dot(mixed, w_conv_out, preferred_element_type=jnp.f...]
    another operation x33 -> x0, loops' own time: 45.7 us -> none  [the longest x1 45.1 us: attention(): lax.scan(one_block, initial, (keys_split, values_split, jnp.arange(count_...]
    dynamic_slice x32 -> x0, local copies, waits for them, and re-layouts: 21.2 us -> none  [attention(): lax.scan(one_block, initial, (keys_split, values_split, jnp.arange(count_...]
    slice x32 -> x0, local copies, waits for them, and re-layouts: 20.8 us -> none  [one_block(): entry[1][-1]]
    unnamed x25 -> x21, local copies, waits for them, and re-layouts: 23 us -> 4.64 us
    all_gather x1, waiting for transfers between devices: 97.1 us -> 114 us  [attention(): value_piece = lax.all_gather(v_attn, 'ctx', axis=0, tiled=True)]
    while x3 -> x0, local copies, waits for them, and re-layouts: 14.7 us -> none  [attention(): lax.scan(one_block, initial, (keys_split, values_split, jnp.arange(count_...]
    pallas_call x0 -> x1, Pallas kernels: none -> 9.3 us  [attention_core(): pl.pallas_call(kernel, out_shape=jax.ShapeDtypeStruct((tok_rows, width),...]
  transfers between devices with their start and end apart: 12 -> 12, of which waited for: 11 -> 11; matrix products, arithmetic and copies ran while one was open for 14% -> 17% of each run, Pallas kernels for 0% -> 0%
where the time goes in v1:
time: 416 us; the launch traced here: 409 us
  waiting for transfers between devices  256 us (62%)
  starting transfers between devices  51.7 us (12%)
  matrix products  45 us (11%)
  local copies, waits for them, and re-layouts  27.6 us (7%)
  between operations  14 us (3%)
  Pallas kernels  9.3 us (2%)
  other arithmetic  5.97 us (1%)
    all_gather x1, waiting for transfers between devices, attention(): value_piece = lax.all_gather(v_attn, 'ctx', axis=0, tiled=True)  114 us
    reduce_scatter x1, waiting for transfers between devices, local(): lax.psum_scatter((jnp.dot(mixed, w_conv_out, preferred_element_type=jnp.f...  53.3 us
    all_to_all x1, waiting for transfers between devices, spectral_conv(): lax.all_to_all(source_re.astype(jnp.bfloat16), 'ctx', split_axis=0, conca...  19.6 us
    all_to_all x1, waiting for transfers between devices, spectral_conv(): lax.all_to_all(turned_re.astype(jnp.bfloat16), 'ctx', split_axis=1, conca...  19.4 us
    all_to_all x1, starting transfers between devices, spectral_conv(): lax.all_to_all(filters.reshape(1, tok_rows, groups), 'ctx', split_axis=1,...  11.3 us
    all_to_all x1, waiting for transfers between devices, spectral_conv(): lax.all_to_all(rounded, 'ctx', split_axis=0, concat_axis=1, tiled=True)  10.7 us
    all_to_all x1, waiting for transfers between devices, spectral_conv(): lax.all_to_all(turned_im.astype(jnp.bfloat16), 'ctx', split_axis=1, conca...  10.3 us
    pallas_call x1, Pallas kernels, attention_core(): pl.pallas_call(kernel, out_shape=jax.ShapeDtypeStruct((tok_rows, width),...  9.3 us
  transfers between devices with their start and end apart: 12, of which 11 were waited for; matrix products, arithmetic and copies ran while one was open for 17% of the time, Pallas kernels for 0%

profile of v1, /device:TPU:1, one launch (start us, length us, event | category | flops | bytes accessed | tf_op | source)
XLA Modules:
  0.0 409.4 jit_solution(12655066574745567346)
XLA Ops:
  11.1 11.3 %all-to-all-start.3 = ((bf16[32,2,224]{2,1,0:T(2,128)(2,1)}), bf16[32,2,224]{2,1,0:T(2,128)(2,1)S(1)}, u32[]{:S(2)}, u32[]{:S(2)}) async-start(bf16[32,2,224]{2,1,0:T(2,128)(2,1)} %reshape.140), calls=%async_computation.3 | async-start | bytes 65536 | tf_op jit(solution)/shard_map/all_to_all | solution.py:53
  24.6 3.3 reduce.5
  31.3 7.0 %all-to-all-start = ((bf16[32,2,3584]{2,1,0:T(2,128)(2,1)}), bf16[32,2,3584]{2,1,0:T(2,128)(2,1)S(1)}, u32[]{:S(2)}, u32[]{:S(2)}) async-start(bf16[32,2,3584]{2,1,0:T(2,128)(2,1)} %reshape.146), calls=%async_computation | async-start | bytes 917504 | tf_op jit(solution)/shard_map/all_to_all | solution.py:50
  41.2 7.5 %all-to-all-done = bf16[32,2,3584]{2,1,0:T(2,128)(2,1)S(1)} async-done(((bf16[32,2,3584]{2,1,0:T(2,128)(2,1)}), bf16[32,2,3584]{2,1,0:T(2,128)(2,1)S(1)}, u32[]{:S(2)}, u32[]{:S(2)}) %all-to-all-start) | async-done | bytes 458784 | tf_op jit(solution)/shard_map/all_to_all | solution.py:50
  48.7 4.5 %all-to-all-start.5 = ((bf16[32,2,448]{2,1,0:T(2,128)(2,1)}), bf16[32,2,448]{2,1,0:T(2,128)(2,1)S(1)}, u32[]{:S(2)}, u32[]{:S(2)}) async-start(bf16[32,2,448]{2,1,0:T(2,128)(2,1)} %reshape.144), calls=%async_computation.5 | async-start | bytes 131072 | tf_op jit(solution)/shard_map/all_to_all | solution.py:80
  57.7 5.0 %all-to-all-done.5 = bf16[32,2,448]{2,1,0:T(2,128)(2,1)S(1)} async-done(((bf16[32,2,448]{2,1,0:T(2,128)(2,1)}), bf16[32,2,448]{2,1,0:T(2,128)(2,1)S(1)}, u32[]{:S(2)}, u32[]{:S(2)}) %all-to-all-start.5) | async-done | bytes 57376 | tf_op jit(solution)/shard_map/all_to_all | solution.py:80
  62.7 4.3 %all-to-all-start.4 = ((bf16[32,2,448]{2,1,0:T(2,128)(2,1)}), bf16[32,2,448]{2,1,0:T(2,128)(2,1)S(1)}, u32[]{:S(2)}, u32[]{:S(2)}) async-start(bf16[32,2,448]{2,1,0:T(2,128)(2,1)} %reshape.142), calls=%async_computation.4 | async-start | bytes 131072 | tf_op jit(solution)/shard_map/all_to_all | solution.py:77
  71.3 5.1 %all-to-all-done.4 = bf16[32,2,448]{2,1,0:T(2,128)(2,1)S(1)} async-done(((bf16[32,2,448]{2,1,0:T(2,128)(2,1)}), bf16[32,2,448]{2,1,0:T(2,128)(2,1)S(1)}, u32[]{:S(2)}, u32[]{:S(2)}) %all-to-all-start.4) | async-done | bytes 57376 | tf_op jit(solution)/shard_map/all_to_all | solution.py:77
  76.4 4.2 %all-to-all-start.1 = ((bf16[64,7,1024]{2,1,0:T(8,128)(2,1)}), bf16[64,7,1024]{2,1,0:T(8,128)(2,1)S(1)}, u32[]{:S(2)}, u32[]{:S(2)}) async-start(bf16[64,7,1024]{2,1,0:T(8,128)(2,1)} %copy.77), calls=%async_computation.1 | async-start | bytes 2097152 | tf_op jit(solution)/shard_map/all_to_all | solution.py:71
  83.0 19.6 %all-to-all-done.1 = bf16[64,7,1024]{2,1,0:T(8,128)(2,1)S(1)} async-done(((bf16[64,7,1024]{2,1,0:T(8,128)(2,1)}), bf16[64,7,1024]{2,1,0:T(8,128)(2,1)S(1)}, u32[]{:S(2)}, u32[]{:S(2)}) %all-to-all-start.1) | async-done | bytes 917536 | tf_op jit(solution)/shard_map/all_to_all | solution.py:71
  102.6 4.9 %all-to-all-start.2 = ((bf16[64,7,1024]{2,1,0:T(8,128)(2,1)}), bf16[64,7,1024]{2,1,0:T(8,128)(2,1)}, u32[]{:S(2)}, u32[]{:S(2)}) async-start(bf16[64,7,1024]{2,1,0:T(8,128)(2,1)} %copy.80), calls=%async_computation.2 | async-start | bytes 2097152 | tf_op jit(solution)/shard_map/all_to_all | solution.py:74
  117.6 7.2 %all-to-all-done.2 = bf16[64,7,1024]{2,1,0:T(8,128)(2,1)} async-done(((bf16[64,7,1024]{2,1,0:T(8,128)(2,1)}), bf16[64,7,1024]{2,1,0:T(8,128)(2,1)}, u32[]{:S(2)}, u32[]{:S(2)}) %all-to-all-start.2) | async-done | bytes 917536 | tf_op jit(solution)/shard_map/all_to_all | solution.py:74
  143.6 3.8 fusion.10
  149.3 4.2 %all-to-all-start.7 = ((bf16[2,224,1024]{2,0,1:T(2,128)(2,1)}), bf16[2,224,1024]{2,0,1:T(2,128)(2,1)S(1)}, u32[]{:S(2)}, u32[]{:S(2)}) async-start(bf16[2,224,1024]{2,0,1:T(2,128)(2,1)} %copy.102), calls=%async_computation.7 | async-start | bytes 1835008 | tf_op jit(solution)/shard_map/all_to_all | solution.py:111
  155.4 10.3 %all-to-all-done.7 = bf16[2,224,1024]{2,0,1:T(2,128)(2,1)S(1)} async-done(((bf16[2,224,1024]{2,0,1:T(2,128)(2,1)}), bf16[2,224,1024]{2,0,1:T(2,128)(2,1)S(1)}, u32[]{:S(2)}, u32[]{:S(2)}) %all-to-all-start.7) | async-done | bytes 917536 | tf_op jit(solution)/shard_map/all_to_all | solution.py:111
  165.7 5.8 %all-to-all-start.6 = ((bf16[2,224,1024]{2,0,1:T(2,128)(2,1)}), bf16[2,224,1024]{2,0,1:T(2,128)(2,1)S(1)}, u32[]{:S(2)}, u32[]{:S(2)}) async-start(bf16[2,224,1024]{2,0,1:T(2,128)(2,1)} %copy.100), calls=%async_computation.6 | async-start | bytes 1835008 | tf_op jit(solution)/shard_map/all_to_all | solution.py:108
  172.5 19.4 %all-to-all-done.6 = bf16[2,224,1024]{2,0,1:T(2,128)(2,1)S(1)} async-done(((bf16[2,224,1024]{2,0,1:T(2,128)(2,1)}), bf16[2,224,1024]{2,0,1:T(2,128)(2,1)S(1)}, u32[]{:S(2)}, u32[]{:S(2)}) %all-to-all-start.6) | async-done | bytes 917536 | tf_op jit(solution)/shard_map/all_to_all | solution.py:108
  195.3 5.4 %all-to-all-start.8 = ((bf16[32,7,1024]{2,1,0:T(8,128)(2,1)}), bf16[32,7,1024]{2,1,0:T(8,128)(2,1)S(1)}, u32[]{:S(2)}, u32[]{:S(2)}) async-start(bf16[32,7,1024]{2,1,0:T(8,128)(2,1)} %copy.104), calls=%async_computation.8 | async-start | bytes 1048576 | tf_op jit(solution)/shard_map/all_to_all | solution.py:118
  200.9 10.7 %all-to-all-done.8 = bf16[32,7,1024]{2,1,0:T(8,128)(2,1)S(1)} async-done(((bf16[32,7,1024]{2,1,0:T(8,128)(2,1)}), bf16[32,7,1024]{2,1,0:T(8,128)(2,1)S(1)}, u32[]{:S(2)}, u32[]{:S(2)}) %all-to-all-start.8) | async-done | bytes 458784 | tf_op jit(solution)/shard_map/all_to_all | solution.py:118
  211.7 7.4 %fusion.18 = f32[224,4096]{1,0:T(8,128)} fusion(bf16[1024,4096]{1,0:T(8,128)(2,1)} %param.16, f32[224,1024]{1,0:T(8,128)S(1)} %reshape.133, bf16[224,1024]{1,0:T(8,128)(2,1)S(1)} %copy-done.5), kind=kOutput, calls=%fused_computation.37 | convolution fusion | flops 1879736320 | bytes 13434880 | tf_op jit(solution)/shard_map/dot_general | solution.py:238
  219.1 114.0 %all-gather.5.cloned.1.call-done.v_ref = bf16[7168,1024]{1,0:T(8,128)(2,1)} async-done(((bf16[224,1024]{1,0:T(8,128)(2,1)}), bf16[7168,1024]{1,0:T(8,128)(2,1)}) %all-gather.5.cloned.1.call-update) | async-done | bytes 14680080 | tf_op jit(solution)/shard_map/all_gather | solution.py:183
  333.1 9.3 %shard_map.91 = bf16[224,1024]{1,0:T(8,128)(2,1)S(1)} custom-call(s32[2]{0:T(128)S(1)} %pad_add_fusion.info_ref, bf16[224,1024]{1,0:T(8,128)(2,1)S(1)} %copy-done, bf16[7168,1024]{1,0:T(8,128)(2,1)} %all-gather.3.cloned.1.call-done.k_ref, bf16[7168,1024]{1,0:T(8,128)(2,1)} %all-gather.5.cloned.1.call-done.v_ref), custom_call_target="tpu_custom_call" | custom-call | flops 6576668672 | bytes 30277632 | tf_op jit(solution)/shard_map/pallas_call | solution.py:199
  342.5 6.7 %fusion = bf16[224,4096]{1,0:T(8,128)(2,1)} fusion(f32[224,4096]{1,0:T(8,128)S(1)} %copy-done.1, bf16[224,1024]{1,0:T(8,128)(2,1)S(1)} %shard_map.91, bf16[1024,4096]{1,0:T(8,128)(2,1)} %param.17), kind=kOutput, calls=%fused_computation.1 | convolution fusion | flops 1880883200 | bytes 14352384 | tf_op jit(solution)/shard_map/dot_general | solution.py:239
  349.2 53.3 %reduce-scatter.2.cloned.1.call-done = bf16[56,4096]{1,0:T(8,128)(2,1)} async-done(((bf16[224,4096]{1,0:T(8,128)(2,1)}), bf16[56,4096]{1,0:T(8,128)(2,1)}) %reduce-scatter.2.cloned.1.call-update) | async-done | bytes 458768 | tf_op jit(solution)/shard_map/reduce_scatter | solution.py:236
  (81 shorter events, 61.1 us)
Async XLA Ops:
  6.5 212.6 %all-gather.3.cloned.1.call-start = ((), (), s32[]{:S(2)}) async-start(), calls=%async_computation.10 | async-start | bytes 15138816 | tf_op jit(solution)/shard_map/all_gather | solution.py:182
  7.3 325.9 %all-gather.5.cloned.1.call-start = ((), (), s32[]{:S(2)}) async-start(), calls=%async_computation.11 | async-start | bytes 15138816 | tf_op jit(solution)/shard_map/all_gather | solution.py:183
  11.1 20.1 %all-to-all-start.3 = ((bf16[32,2,224]{2,1,0:T(2,128)(2,1)}), bf16[32,2,224]{2,1,0:T(2,128)(2,1)S(1)}, u32[]{:S(2)}, u32[]{:S(2)}) async-start(bf16[32,2,224]{2,1,0:T(2,128)(2,1)} %reshape.140), calls=%async_computation.3 | async-start | bytes 65536 | tf_op jit(solution)/shard_map/all_to_all | solution.py:53
  31.3 17.5 %all-to-all-start = ((bf16[32,2,3584]{2,1,0:T(2,128)(2,1)}), bf16[32,2,3584]{2,1,0:T(2,128)(2,1)S(1)}, u32[]{:S(2)}, u32[]{:S(2)}) async-start(bf16[32,2,3584]{2,1,0:T(2,128)(2,1)} %reshape.146), calls=%async_computation | async-start | bytes 917504 | tf_op jit(solution)/shard_map/all_to_all | solution.py:50
  48.7 14.0 %all-to-all-start.5 = ((bf16[32,2,448]{2,1,0:T(2,128)(2,1)}), bf16[32,2,448]{2,1,0:T(2,128)(2,1)S(1)}, u32[]{:S(2)}, u32[]{:S(2)}) async-start(bf16[32,2,448]{2,1,0:T(2,128)(2,1)} %reshape.144), calls=%async_computation.5 | async-start | bytes 131072 | tf_op jit(solution)/shard_map/all_to_all | solution.py:80
  62.7 13.7 %all-to-all-start.4 = ((bf16[32,2,448]{2,1,0:T(2,128)(2,1)}), bf16[32,2,448]{2,1,0:T(2,128)(2,1)S(1)}, u32[]{:S(2)}, u32[]{:S(2)}) async-start(bf16[32,2,448]{2,1,0:T(2,128)(2,1)} %reshape.142), calls=%async_computation.4 | async-start | bytes 131072 | tf_op jit(solution)/shard_map/all_to_all | solution.py:77
  71.3 10.2 %copy-start.4 = (bf16[64,7,1024]{2,0,1:T(8,128)(2,1)S(1)}, bf16[64,7,1024]{2,0,1:T(8,128)(2,1)}, u32[]{:S(2)}) copy-start(bf16[64,7,1024]{2,0,1:T(8,128)(2,1)} %get-tuple-element.8) | copy-start | bytes 2752516
  76.4 26.2 %all-to-all-start.1 = ((bf16[64,7,1024]{2,1,0:T(8,128)(2,1)}), bf16[64,7,1024]{2,1,0:T(8,128)(2,1)S(1)}, u32[]{:S(2)}, u32[]{:S(2)}) async-start(bf16[64,7,1024]{2,1,0:T(8,128)(2,1)} %copy.77), calls=%async_computation.1 | async-start | bytes 2097152 | tf_op jit(solution)/shard_map/all_to_all | solution.py:71
  102.6 22.3 %all-to-all-start.2 = ((bf16[64,7,1024]{2,1,0:T(8,128)(2,1)}), bf16[64,7,1024]{2,1,0:T(8,128)(2,1)}, u32[]{:S(2)}, u32[]{:S(2)}) async-start(bf16[64,7,1024]{2,1,0:T(8,128)(2,1)} %copy.80), calls=%async_computation.2 | async-start | bytes 2097152 | tf_op jit(solution)/shard_map/all_to_all | solution.py:74
  130.8 2.0 copy-start.2
  130.8 2.0 copy-start.3
  149.3 16.5 %all-to-all-start.7 = ((bf16[2,224,1024]{2,0,1:T(2,128)(2,1)}), bf16[2,224,1024]{2,0,1:T(2,128)(2,1)S(1)}, u32[]{:S(2)}, u32[]{:S(2)}) async-start(bf16[2,224,1024]{2,0,1:T(2,128)(2,1)} %copy.102), calls=%async_computation.7 | async-start | bytes 1835008 | tf_op jit(solution)/shard_map/all_to_all | solution.py:111
  165.7 26.2 %all-to-all-start.6 = ((bf16[2,224,1024]{2,0,1:T(2,128)(2,1)}), bf16[2,224,1024]{2,0,1:T(2,128)(2,1)S(1)}, u32[]{:S(2)}, u32[]{:S(2)}) async-start(bf16[2,224,1024]{2,0,1:T(2,128)(2,1)} %copy.100), calls=%async_computation.6 | async-start | bytes 1835008 | tf_op jit(solution)/shard_map/all_to_all | solution.py:108
  194.2 17.5 %copy-start.5 = (bf16[224,1024]{1,0:T(8,128)(2,1)S(1)}, bf16[224,1024]{1,0:T(8,128)(2,1)}, u32[]{:S(2)}) copy-start(bf16[224,1024]{1,0:T(8,128)(2,1)} %param.9) | copy-start | bytes 1376260
  195.3 16.3 %all-to-all-start.8 = ((bf16[32,7,1024]{2,1,0:T(8,128)(2,1)}), bf16[32,7,1024]{2,1,0:T(8,128)(2,1)S(1)}, u32[]{:S(2)}, u32[]{:S(2)}) async-start(bf16[32,7,1024]{2,1,0:T(8,128)(2,1)} %copy.104), calls=%async_computation.8 | async-start | bytes 1048576 | tf_op jit(solution)/shard_map/all_to_all | solution.py:118
  200.7 201.8 %reduce-scatter.2.cloned.1.call-start = ((), (), s32[]{:S(2)}) async-start(), calls=%async_computation.12 | async-start | bytes 2293760 | tf_op jit(solution)/shard_map/reduce_scatter | solution.py:236
  211.7 121.4 %copy-start = (bf16[224,1024]{1,0:T(8,128)(2,1)S(1)}, bf16[224,1024]{1,0:T(8,128)(2,1)}, u32[]{:S(2)}) copy-start(bf16[224,1024]{1,0:T(8,128)(2,1)} %q_ref.1) | copy-start | bytes 1376260
  333.1 9.3 %copy-start.1 = (f32[224,4096]{1,0:T(8,128)S(1)}, f32[224,4096]{1,0:T(8,128)}, u32[]{:S(2)}) copy-start(f32[224,4096]{1,0:T(8,128)} %fusion.18) | copy-start | bytes 11010052
Sparse Core Ops, SparseCore 0:
  10.4 179.6 all-gather.2
  193.2 139.9 all-gather.4
  349.3 53.1 reduce-scatter.1

commit v2 on v1

--- a/solution.py
+++ b/solution.py
@@ -48,10 +48,10 @@
     period = 2 * count_ctx * tok_rows
     got_source, got_filter = (
         lax.all_to_all(
-            gated.reshape(1, tok_rows, chans), "ctx", split_axis=1, concat_axis=0, tiled=True
-        ),
-        lax.all_to_all(
-            filters.reshape(1, tok_rows, groups), "ctx", split_axis=1, concat_axis=0, tiled=True
+            gated.reshape(1, tok_rows, chans), CTX, split_axis=1, concat_axis=0, tiled=True
+        ),
+        lax.all_to_all(
+            filters.reshape(1, tok_rows, groups), CTX, split_axis=1, concat_axis=0, tiled=True
         ),
     )
     coarse_idx = jnp.arange(count_ctx, dtype=jnp.int32)
@@ -69,16 +69,16 @@
     )
     source_re, source_im, filter_re, filter_im = (
         lax.all_to_all(
-            source_re.astype(jnp.bfloat16), "ctx", split_axis=0, concat_axis=1, tiled=True
+            source_re.astype(jnp.bfloat16), CTX, split_axis=0, concat_axis=1, tiled=True
         ).astype(source_re.dtype),
         lax.all_to_all(
-            source_im.astype(jnp.bfloat16), "ctx", split_axis=0, concat_axis=1, tiled=True
+            source_im.astype(jnp.bfloat16), CTX, split_axis=0, concat_axis=1, tiled=True
         ).astype(source_im.dtype),
         lax.all_to_all(
-            filter_re.astype(jnp.bfloat16), "ctx", split_axis=0, concat_axis=1, tiled=True
+            filter_re.astype(jnp.bfloat16), CTX, split_axis=0, concat_axis=1, tiled=True
         ).astype(filter_re.dtype),
         lax.all_to_all(
-            filter_im.astype(jnp.bfloat16), "ctx", split_axis=0, concat_axis=1, tiled=True
+            filter_im.astype(jnp.bfloat16), CTX, split_axis=0, concat_axis=1, tiled=True
         ).astype(filter_im.dtype),
     )
     fine_idx = jnp.arange(tok_rows, dtype=jnp.int32)
@@ -106,27 +106,28 @@
     turned_im = back_re * sin_out + back_im * cos_out
     turned_re, turned_im = (
         lax.all_to_all(
-            turned_re.astype(jnp.bfloat16), "ctx", split_axis=1, concat_axis=0, tiled=True
+            turned_re.astype(jnp.bfloat16), CTX, split_axis=1, concat_axis=0, tiled=True
         ).astype(turned_re.dtype),
         lax.all_to_all(
-            turned_im.astype(jnp.bfloat16), "ctx", split_axis=1, concat_axis=0, tiled=True
+            turned_im.astype(jnp.bfloat16), CTX, split_axis=1, concat_axis=0, tiled=True
         ).astype(turned_im.dtype),
     )
     result = jnp.einsum("nk,ksc->nsc", cos_coarse.T, turned_re, precision=highest)
     result = result - jnp.einsum("nk,ksc->nsc", sin_coarse.T, turned_im, precision=highest)
     rounded = (result / period).astype(jnp.bfloat16)
-    returned = lax.all_to_all(rounded, "ctx", split_axis=0, concat_axis=1, tiled=True)
+    returned = lax.all_to_all(rounded, CTX, split_axis=0, concat_axis=1, tiled=True)
     return returned.reshape(tok_rows, chans)
 
 
-KEY_BLOCK = 1024
-
-
-def flash_kernel(info_ref, q_ref, k_ref, v_ref, o_ref, m_sc, l_sc, acc_sc, *, heads, tok_rows, key_block, scale):
+CTX = ("z", "yh", "x")
+
+
+def flash_kernel(info_ref, q_ref, k_ref, v_ref, o_ref, m_sc, l_sc, acc_sc, *, heads, tok_rows, x_size, yh_size, scale):
     j = pl.program_id(0)
-    q_first = info_ref[0] * tok_rows
+    my_ctx = info_ref[0]
     last_block = info_ref[1] - 1
-    key_first = j * key_block
+    z = j // x_size
+    x = j % x_size
 
     @pl.when(j == 0)
     def _():
@@ -134,15 +135,15 @@
         l_sc[...] = jnp.zeros_like(l_sc)
         acc_sc[...] = jnp.zeros_like(acc_sc)
 
-    def step(masked):
+    def step(half, masked):
         if masked:
-            query_pos = q_first + lax.broadcasted_iota(jnp.int32, (tok_rows, key_block), 0)
-            key_pos = key_first + lax.broadcasted_iota(jnp.int32, (tok_rows, key_block), 1)
+            query_pos = lax.broadcasted_iota(jnp.int32, (tok_rows, tok_rows), 0)
+            key_pos = lax.broadcasted_iota(jnp.int32, (tok_rows, tok_rows), 1)
             allowed = key_pos <= query_pos
         for h in range(heads):
             cols = slice(h * HD, (h + 1) * HD)
             scores = lax.dot_general(
-                q_ref[:, cols], k_ref[:, cols], (((1,), (1,)), ((), ())),
+                q_ref[:, cols], k_ref[half, :, cols], (((1,), (1,)), ((), ())),
                 preferred_element_type=jnp.float32,
             ) * scale
             if masked:
@@ -155,19 +156,21 @@
             factor = jnp.exp(m_prev - m_new)
             l_sc[h] = l_sc[h] * factor + jnp.sum(weights, axis=1, keepdims=True)
             acc_sc[:, cols] = acc_sc[:, cols] * factor + jnp.dot(
-                weights.astype(jnp.bfloat16), v_ref[:, cols], preferred_element_type=jnp.float32
+                weights.astype(jnp.bfloat16), v_ref[half, :, cols], preferred_element_type=jnp.float32
             )
             m_sc[h] = m_new
 
-    full = key_first + key_block <= q_first
-
-    @pl.when(jnp.logical_and(j <= last_block, full))
-    def _():
-        step(False)
-
-    @pl.when(jnp.logical_and(j <= last_block, jnp.logical_not(full)))
-    def _():
-        step(True)
+    for half in range(yh_size):
+        block_ctx = (z * yh_size + half) * x_size + x
+        active = j <= last_block
+
+        @pl.when(jnp.logical_and(active, block_ctx < my_ctx))
+        def _():
+            step(half, False)
+
+        @pl.when(jnp.logical_and(active, block_ctx == my_ctx))
+        def _():
+            step(half, True)
 
     @pl.when(j == last_block)
     def _():
@@ -176,26 +179,23 @@
             o_ref[:, cols] = (acc_sc[:, cols] / l_sc[h]).astype(o_ref.dtype)
 
 
-def attention(q_attn, k_attn, v_attn, my_index, tok_rows):
+def attention(q_attn, k_attn, v_attn, tok_rows):
     width = q_attn.shape[1]
     heads_local = width // HD
-    key_piece = lax.all_gather(k_attn, "ctx", axis=0, tiled=True)
-    value_piece = lax.all_gather(v_attn, "ctx", axis=0, tiled=True)
-    return attention_core(q_attn, key_piece, value_piece, my_index, tok_rows)
-
-
-def attention_core(q_attn, key_piece, value_piece, my_index, tok_rows):
-    width = q_attn.shape[1]
-    heads_local = width // HD
-    total_rows = key_piece.shape[0]
-    key_block = KEY_BLOCK if total_rows % KEY_BLOCK == 0 else tok_rows
-    count_blocks = total_rows // key_block
-    needed = ((my_index + 1) * tok_rows + key_block - 1) // key_block
-    info = jnp.stack([my_index, needed]).astype(jnp.int32)
+    z_size, yh_size, x_size = (lax.axis_size(name) for name in CTX)
+    z_me, yh_me, x_me = (lax.axis_index(name) for name in CTX)
+    my_ctx = (z_me * yh_size + yh_me) * x_size + x_me
+    both = jnp.stack([k_attn, v_attn])
+    across = lax.all_gather(both, "yh", axis=0)
+    gathered = lax.all_gather(across, ("z", "x"), axis=0)
+    count_blocks = z_size * x_size
+    needed = z_me * x_size + jnp.where(yh_me == 0, x_me + 1, x_size)
+    info = jnp.stack([my_ctx, needed]).astype(jnp.int32)
     kernel = partial(
-        flash_kernel, heads=heads_local, tok_rows=tok_rows, key_block=key_block, scale=HD ** (-0.5)
-    )
-    kv_spec = pl.BlockSpec((key_block, width), lambda j, info: (jnp.minimum(j, info[1] - 1), 0))
+        flash_kernel, heads=heads_local, tok_rows=tok_rows, x_size=x_size, yh_size=yh_size,
+        scale=HD ** (-0.5),
+    )
+    total_rows = count_blocks * yh_size * tok_rows
     return pl.pallas_call(
         kernel,
         out_shape=jax.ShapeDtypeStruct((tok_rows, width), jnp.bfloat16),
@@ -204,8 +204,14 @@
             grid=(count_blocks,),
             in_specs=[
                 pl.BlockSpec((tok_rows, width), lambda j, info: (0, 0)),
-                kv_spec,
-                kv_spec,
+                pl.BlockSpec(
+                    (None, yh_size, None, tok_rows, width),
+                    lambda j, info: (jnp.minimum(j, info[1] - 1), 0, 0, 0, 0),
+                ),
+                pl.BlockSpec(
+                    (None, yh_size, None, tok_rows, width),
+                    lambda j, info: (jnp.minimum(j, info[1] - 1), 0, 1, 0, 0),
+                ),
             ],
             out_specs=pl.BlockSpec((tok_rows, width), lambda j, info: (0, 0)),
             scratch_shapes=[
@@ -222,17 +228,19 @@
             transcendentals=heads_local * tok_rows * total_rows,
             bytes_accessed=2 * total_rows * width * 2 + 2 * tok_rows * width * 2,
         ),
-    )(info, q_attn, key_piece, value_piece)
+    )(info, q_attn, gathered, gathered)
 
 
 def local(q_conv, k_conv, v_conv, conv_filter, q_attn, k_attn, v_attn, w_conv_out, w_attn_out):
-    count_ctx = lax.axis_size("ctx")
-    my_index = lax.axis_index("ctx")
+    z_size, yh_size, x_size = (lax.axis_size(name) for name in CTX)
+    z_me, yh_me, x_me = (lax.axis_index(name) for name in CTX)
+    count_ctx = z_size * yh_size * x_size
+    my_index = (z_me * yh_size + yh_me) * x_size + x_me
     tok_rows = q_conv.shape[0]
     gated = (k_conv.astype(jnp.float32) * v_conv.astype(jnp.float32)).astype(jnp.bfloat16)
     conv = spectral_conv(gated, conv_filter, my_index, tok_rows, count_ctx)
     mixed = (q_conv.astype(jnp.float32) * conv.astype(jnp.float32)).astype(jnp.bfloat16)
-    attended = attention(q_attn, k_attn, v_attn, my_index, tok_rows)
+    attended = attention(q_attn, k_attn, v_attn, tok_rows)
     return lax.psum_scatter(
         (
             jnp.dot(mixed, w_conv_out, preferred_element_type=jnp.float32)
@@ -245,20 +253,18 @@
 
 
 def solution(mesh):
+    ctx_size, ch_size = mesh.devices.shape
+    x_size = 4
+    yh_size = 2
+    z_size = ctx_size // (x_size * yh_size)
+    split_mesh = jax.sharding.Mesh(
+        mesh.devices.reshape(z_size, yh_size, x_size, ch_size), ("z", "yh", "x", "ch")
+    )
+    tokens = P(CTX, "ch")
     return jax.shard_map(
         local,
-        mesh=mesh,
-        in_specs=(
-            P("ctx", "ch"),
-            P("ctx", "ch"),
-            P("ctx", "ch"),
-            P("ctx", "ch"),
-            P("ctx", "ch"),
-            P("ctx", "ch"),
-            P("ctx", "ch"),
-            P("ch", None),
-            P("ch", None),
-        ),
-        out_specs=P(("ctx", "ch"), None),
+        mesh=split_mesh,
+        in_specs=(tokens,) * 7 + (P("ch", None), P("ch", None)),
+        out_specs=P(CTX + ("ch",), None),
         check_vma=False,
     )

time: 416 us -> 468 us (1.12)
  waiting for transfers between devices: 256 us -> 316 us
  starting transfers between devices: 51.7 us -> 44.8 us
    reduce_scatter x1, waiting for transfers between devices: 53.3 us -> 152 us  [local(): lax.psum_scatter((jnp.dot(mixed, w_conv_out, preferred_element_type=jnp.f...]
    all_gather x2, waiting for transfers between devices: 114 us -> 37.4 us  [the longest x1 37.4 us: attention(): across = lax.all_gather(both, 'yh', axis=0)]
    all_to_all x9, waiting for transfers between devices: 87.2 us -> 126 us  [the longest x1 25.9 us: spectral_conv(): lax.all_to_all(source_re.astype(jnp.bfloat16), CTX, split_axis=0, concat_...]
    all_to_all x9, starting transfers between devices: 51.6 us -> 44.7 us  [the longest x1 6.95 us: spectral_conv(): lax.all_to_all(filters.reshape(1, tok_rows, groups), CTX, split_axis=1, c...]
  transfers between devices with their start and end apart: 12 -> 12, of which waited for: 11 -> 11; matrix products, arithmetic and copies ran while one was open for 17% -> 15% of each run, Pallas kernels for 0% -> 0%
where the time goes in v2:
time: 468 us; the launch traced here: 461 us
  waiting for transfers between devices  316 us (68%)
  matrix products  44.9 us (10%)
  starting transfers between devices  44.8 us (10%)
  local copies, waits for them, and re-layouts  26.9 us (6%)
  between operations  14 us (3%)
  Pallas kernels  7.87 us (2%)
  other arithmetic  6.98 us (1%)
    reduce_scatter x1, waiting for transfers between devices, local(): lax.psum_scatter((jnp.dot(mixed, w_conv_out, preferred_element_type=jnp.f...  152 us
    all_gather x1, waiting for transfers between devices, attention(): across = lax.all_gather(both, 'yh', axis=0)  37.4 us
    all_to_all x1, waiting for transfers between devices, spectral_conv(): lax.all_to_all(source_re.astype(jnp.bfloat16), CTX, split_axis=0, concat_...  25.9 us
    all_to_all x1, waiting for transfers between devices, spectral_conv(): lax.all_to_all(turned_re.astype(jnp.bfloat16), CTX, split_axis=1, concat_...  23.2 us
    all_to_all x1, waiting for transfers between devices, spectral_conv(): lax.all_to_all(turned_im.astype(jnp.bfloat16), CTX, split_axis=1, concat_...  22.7 us
    all_to_all x1, waiting for transfers between devices, spectral_conv(): lax.all_to_all(source_im.astype(jnp.bfloat16), CTX, split_axis=0, concat_...  17.8 us
    all_to_all x1, waiting for transfers between devices, spectral_conv(): lax.all_to_all(gated.reshape(1, tok_rows, chans), CTX, split_axis=1, conc...  13.5 us
    all_to_all x1, waiting for transfers between devices, spectral_conv(): lax.all_to_all(rounded, CTX, split_axis=0, concat_axis=1, tiled=True)  10.4 us
  transfers between devices with their start and end apart: 12, of which 11 were waited for; matrix products, arithmetic and copies ran while one was open for 15% of the time, Pallas kernels for 0%

profile of v2, /device:TPU:1, one launch (start us, length us, event | category | flops | bytes accessed | tf_op | source)
XLA Modules:
  0.0 461.4 jit_solution(11952426458774459943)
XLA Ops:
  8.8 37.4 %all-gather.5.cloned.1.call-done = bf16[4,224,1024]{2,1,0:T(8,128)(2,1)} async-done(((bf16[2,224,1024]{2,1,0:T(8,128)(2,1)}), bf16[4,224,1024]{2,1,0:T(8,128)(2,1)}) %all-gather.5.cloned.1.call-update) | async-done | bytes 1835024 | tf_op jit(solution)/shard_map/all_gather | solution.py:189
  48.6 6.9 %all-to-all-start.3 = ((bf16[32,2,224]{2,1,0:T(2,128)(2,1)}), bf16[32,2,224]{2,1,0:T(2,128)(2,1)S(1)}, u32[]{:S(2)}, u32[]{:S(2)}) async-start(bf16[32,2,224]{2,1,0:T(2,128)(2,1)} %reshape.142), calls=%async_computation.3 | async-start | bytes 65536 | tf_op jit(solution)/shard_map/all_to_all | solution.py:53
  61.0 3.4 all-to-all-done.3
  64.4 5.8 %all-to-all-start = ((bf16[32,2,3584]{2,1,0:T(2,128)(2,1)}), bf16[32,2,3584]{2,1,0:T(2,128)(2,1)S(1)}, u32[]{:S(2)}, u32[]{:S(2)}) async-start(bf16[32,2,3584]{2,1,0:T(2,128)(2,1)} %reshape.148), calls=%async_computation | async-start | bytes 917504 | tf_op jit(solution)/shard_map/all_to_all | solution.py:50
  73.2 13.5 %all-to-all-done = bf16[32,2,3584]{2,1,0:T(2,128)(2,1)S(1)} async-done(((bf16[32,2,3584]{2,1,0:T(2,128)(2,1)}), bf16[32,2,3584]{2,1,0:T(2,128)(2,1)S(1)}, u32[]{:S(2)}, u32[]{:S(2)}) %all-to-all-start) | async-done | bytes 458784 | tf_op jit(solution)/shard_map/all_to_all | solution.py:50
  86.7 4.6 all-to-all-start.5
  95.8 4.9 %all-to-all-done.5 = bf16[32,2,448]{2,1,0:T(2,128)(2,1)S(1)} async-done(((bf16[32,2,448]{2,1,0:T(2,128)(2,1)}), bf16[32,2,448]{2,1,0:T(2,128)(2,1)S(1)}, u32[]{:S(2)}, u32[]{:S(2)}) %all-to-all-start.5) | async-done | bytes 57376 | tf_op jit(solution)/shard_map/all_to_all | solution.py:80
  100.7 4.4 all-to-all-start.4
  109.4 4.7 %all-to-all-done.4 = bf16[32,2,448]{2,1,0:T(2,128)(2,1)S(1)} async-done(((bf16[32,2,448]{2,1,0:T(2,128)(2,1)}), bf16[32,2,448]{2,1,0:T(2,128)(2,1)S(1)}, u32[]{:S(2)}, u32[]{:S(2)}) %all-to-all-start.4) | async-done | bytes 57376 | tf_op jit(solution)/shard_map/all_to_all | solution.py:77
  114.0 4.7 %all-to-all-start.1 = ((bf16[64,7,1024]{2,1,0:T(8,128)(2,1)}), bf16[64,7,1024]{2,1,0:T(8,128)(2,1)S(1)}, u32[]{:S(2)}, u32[]{:S(2)}) async-start(bf16[64,7,1024]{2,1,0:T(8,128)(2,1)} %copy.77), calls=%async_computation.1 | async-start | bytes 2097152 | tf_op jit(solution)/shard_map/all_to_all | solution.py:71
  121.1 25.9 %all-to-all-done.1 = bf16[64,7,1024]{2,1,0:T(8,128)(2,1)S(1)} async-done(((bf16[64,7,1024]{2,1,0:T(8,128)(2,1)}), bf16[64,7,1024]{2,1,0:T(8,128)(2,1)S(1)}, u32[]{:S(2)}, u32[]{:S(2)}) %all-to-all-start.1) | async-done | bytes 917536 | tf_op jit(solution)/shard_map/all_to_all | solution.py:71
  147.0 4.7 %all-to-all-start.2 = ((bf16[64,7,1024]{2,1,0:T(8,128)(2,1)}), bf16[64,7,1024]{2,1,0:T(8,128)(2,1)}, u32[]{:S(2)}, u32[]{:S(2)}) async-start(bf16[64,7,1024]{2,1,0:T(8,128)(2,1)} %copy.80), calls=%async_computation.2 | async-start | bytes 2097152 | tf_op jit(solution)/shard_map/all_to_all | solution.py:74
  161.8 17.8 %all-to-all-done.2 = bf16[64,7,1024]{2,1,0:T(8,128)(2,1)} async-done(((bf16[64,7,1024]{2,1,0:T(8,128)(2,1)}), bf16[64,7,1024]{2,1,0:T(8,128)(2,1)}, u32[]{:S(2)}, u32[]{:S(2)}) %all-to-all-start.2) | async-done | bytes 917536 | tf_op jit(solution)/shard_map/all_to_all | solution.py:74
  198.5 3.8 fusion.10
  204.2 4.4 all-to-all-start.7
  210.5 22.7 %all-to-all-done.7 = bf16[2,224,1024]{2,0,1:T(2,128)(2,1)S(1)} async-done(((bf16[2,224,1024]{2,0,1:T(2,128)(2,1)}), bf16[2,224,1024]{2,0,1:T(2,128)(2,1)S(1)}, u32[]{:S(2)}, u32[]{:S(2)}) %all-to-all-start.7) | async-done | bytes 917536 | tf_op jit(solution)/shard_map/all_to_all | solution.py:111
  233.1 4.6 all-to-all-start.6
  238.7 23.2 %all-to-all-done.6 = bf16[2,224,1024]{2,0,1:T(2,128)(2,1)S(1)} async-done(((bf16[2,224,1024]{2,0,1:T(2,128)(2,1)}), bf16[2,224,1024]{2,0,1:T(2,128)(2,1)S(1)}, u32[]{:S(2)}, u32[]{:S(2)}) %all-to-all-start.6) | async-done | bytes 917536 | tf_op jit(solution)/shard_map/all_to_all | solution.py:108
  265.2 4.6 all-to-all-start.8
  270.0 10.4 %all-to-all-done.8 = bf16[32,7,1024]{2,1,0:T(8,128)(2,1)S(1)} async-done(((bf16[32,7,1024]{2,1,0:T(8,128)(2,1)}), bf16[32,7,1024]{2,1,0:T(8,128)(2,1)S(1)}, u32[]{:S(2)}, u32[]{:S(2)}) %all-to-all-start.8) | async-done | bytes 458784 | tf_op jit(solution)/shard_map/all_to_all | solution.py:118
  280.5 7.3 %fusion.18 = f32[224,4096]{1,0:T(8,128)} fusion(bf16[1024,4096]{1,0:T(8,128)(2,1)} %param.16, f32[224,1024]{1,0:T(8,128)S(1)} %reshape.133, bf16[224,1024]{1,0:T(8,128)(2,1)S(1)} %copy-done.5), kind=kOutput, calls=%fused_computation.38 | convolution fusion | flops 1879736320 | bytes 13434880 | tf_op jit(solution)/shard_map/dot_general | solution.py:246
  287.8 7.9 %shard_map.91 = bf16[224,1024]{1,0:T(8,128)(2,1)S(1)} custom-call(s32[2]{0:T(128)S(1)} %pad_add_fusion.info_ref, bf16[224,1024]{1,0:T(8,128)(2,1)S(1)} %copy-done, bf16[16,2,2,224,1024]{4,3,2,1,0:T(8,128)(2,1)} %bitcast.128, bf16[16,2,2,224,1024]{4,3,2,1,0:T(8,128)(2,1)} %bitcast.129), custom_call_target="tpu_custom_call" | custom-call | flops 6576668672 | bytes 30277632 | tf_op jit(solution)/shard_map/pallas_call | solution.py:199
  295.7 6.7 %fusion = bf16[224,4096]{1,0:T(8,128)(2,1)} fusion(f32[224,4096]{1,0:T(8,128)S(1)} %copy-done.1, bf16[224,1024]{1,0:T(8,128)(2,1)S(1)} %shard_map.91, bf16[1024,4096]{1,0:T(8,128)(2,1)} %param.17), kind=kOutput, calls=%fused_computation.1 | convolution fusion | flops 1880883200 | bytes 14352384 | tf_op jit(solution)/shard_map/dot_general | solution.py:247
  302.5 152.0 %reduce-scatter.2.cloned.1.call-done = bf16[56,4096]{1,0:T(8,128)(2,1)} async-done(((bf16[224,4096]{1,0:T(8,128)(2,1)}), bf16[56,4096]{1,0:T(8,128)(2,1)}) %reduce-scatter.2.cloned.1.call-update) | async-done | bytes 458768 | tf_op jit(solution)/shard_map/reduce_scatter | solution.py:244
  (88 shorter events, 61.1 us)
Async XLA Ops:
  6.5 39.7 %all-gather.5.cloned.1.call-start = ((), (), s32[]{:S(2)}) async-start(), calls=%async_computation.11 | async-start | bytes 2752512 | tf_op jit(solution)/shard_map/all_gather | solution.py:189
  8.7 37.6 %copy-start.8 = (bf16[224,64]{0,1:T(8,128)(2,1)S(1)}, bf16[224,64]{0,1:T(8,128)(2,1)}, u32[]{:S(2)}) copy-start(bf16[224,64]{0,1:T(8,128)(2,1)} %param.12) | copy-start | bytes 86020
  8.7 46.9 %copy-start.6 = (bf16[224,1024]{1,0:T(8,128)(2,1)S(1)}, bf16[224,1024]{1,0:T(8,128)(2,1)}, u32[]{:S(2)}) copy-start(bf16[224,1024]{1,0:T(8,128)(2,1)} %param.11) | copy-start | bytes 1376260
  8.7 46.9 %copy-start.7 = (bf16[224,1024]{1,0:T(8,128)(2,1)S(1)}, bf16[224,1024]{1,0:T(8,128)(2,1)}, u32[]{:S(2)}) copy-start(bf16[224,1024]{1,0:T(8,128)(2,1)} %param.10) | copy-start | bytes 1376260
  8.7 279.1 %all-gather.7.cloned.1.call-start = ((), (), s32[]{:S(2)}) async-start(), calls=%async_computation.12 | async-start | bytes 31195136 | tf_op jit(solution)/shard_map/all_gather | solution.py:190
  48.6 15.8 %all-to-all-start.3 = ((bf16[32,2,224]{2,1,0:T(2,128)(2,1)}), bf16[32,2,224]{2,1,0:T(2,128)(2,1)S(1)}, u32[]{:S(2)}, u32[]{:S(2)}) async-start(bf16[32,2,224]{2,1,0:T(2,128)(2,1)} %reshape.142), calls=%async_computation.3 | async-start | bytes 65536 | tf_op jit(solution)/shard_map/all_to_all | solution.py:53
  64.4 22.3 %all-to-all-start = ((bf16[32,2,3584]{2,1,0:T(2,128)(2,1)}), bf16[32,2,3584]{2,1,0:T(2,128)(2,1)S(1)}, u32[]{:S(2)}, u32[]{:S(2)}) async-start(bf16[32,2,3584]{2,1,0:T(2,128)(2,1)} %reshape.148), calls=%async_computation | async-start | bytes 917504 | tf_op jit(solution)/shard_map/all_to_all | solution.py:50
  86.7 14.0 %all-to-all-start.5 = ((bf16[32,2,448]{2,1,0:T(2,128)(2,1)}), bf16[32,2,448]{2,1,0:T(2,128)(2,1)S(1)}, u32[]{:S(2)}, u32[]{:S(2)}) async-start(bf16[32,2,448]{2,1,0:T(2,128)(2,1)} %reshape.146), calls=%async_computation.5 | async-start | bytes 131072 | tf_op jit(solution)/shard_map/all_to_all | solution.py:80
  100.7 13.3 %all-to-all-start.4 = ((bf16[32,2,448]{2,1,0:T(2,128)(2,1)}), bf16[32,2,448]{2,1,0:T(2,128)(2,1)S(1)}, u32[]{:S(2)}, u32[]{:S(2)}) async-start(bf16[32,2,448]{2,1,0:T(2,128)(2,1)} %reshape.144), calls=%async_computation.4 | async-start | bytes 131072 | tf_op jit(solution)/shard_map/all_to_all | solution.py:77
  109.3 10.2 %copy-start.4 = (bf16[64,7,1024]{2,0,1:T(8,128)(2,1)S(1)}, bf16[64,7,1024]{2,0,1:T(8,128)(2,1)}, u32[]{:S(2)}) copy-start(bf16[64,7,1024]{2,0,1:T(8,128)(2,1)} %get-tuple-element.8) | copy-start | bytes 2752516
  114.0 33.0 %all-to-all-start.1 = ((bf16[64,7,1024]{2,1,0:T(8,128)(2,1)}), bf16[64,7,1024]{2,1,0:T(8,128)(2,1)S(1)}, u32[]{:S(2)}, u32[]{:S(2)}) async-start(bf16[64,7,1024]{2,1,0:T(8,128)(2,1)} %copy.77), calls=%async_computation.1 | async-start | bytes 2097152 | tf_op jit(solution)/shard_map/all_to_all | solution.py:71
  147.0 32.6 %all-to-all-start.2 = ((bf16[64,7,1024]{2,1,0:T(8,128)(2,1)}), bf16[64,7,1024]{2,1,0:T(8,128)(2,1)}, u32[]{:S(2)}, u32[]{:S(2)}) async-start(bf16[64,7,1024]{2,1,0:T(8,128)(2,1)} %copy.80), calls=%async_computation.2 | async-start | bytes 2097152 | tf_op jit(solution)/shard_map/all_to_all | solution.py:74
  185.5 2.0 copy-start.2
  185.5 2.2 copy-start.3
  204.2 29.0 %all-to-all-start.7 = ((bf16[2,224,1024]{2,0,1:T(2,128)(2,1)}), bf16[2,224,1024]{2,0,1:T(2,128)(2,1)S(1)}, u32[]{:S(2)}, u32[]{:S(2)}) async-start(bf16[2,224,1024]{2,0,1:T(2,128)(2,1)} %copy.102), calls=%async_computation.7 | async-start | bytes 1835008 | tf_op jit(solution)/shard_map/all_to_all | solution.py:111
  233.1 28.8 %all-to-all-start.6 = ((bf16[2,224,1024]{2,0,1:T(2,128)(2,1)}), bf16[2,224,1024]{2,0,1:T(2,128)(2,1)S(1)}, u32[]{:S(2)}, u32[]{:S(2)}) async-start(bf16[2,224,1024]{2,0,1:T(2,128)(2,1)} %copy.100), calls=%async_computation.6 | async-start | bytes 1835008 | tf_op jit(solution)/shard_map/all_to_all | solution.py:108
  264.1 16.4 %copy-start.5 = (bf16[224,1024]{1,0:T(8,128)(2,1)S(1)}, bf16[224,1024]{1,0:T(8,128)(2,1)}, u32[]{:S(2)}) copy-start(bf16[224,1024]{1,0:T(8,128)(2,1)} %param.9) | copy-start | bytes 1376260
  265.2 15.1 %all-to-all-start.8 = ((bf16[32,7,1024]{2,1,0:T(8,128)(2,1)}), bf16[32,7,1024]{2,1,0:T(8,128)(2,1)S(1)}, u32[]{:S(2)}, u32[]{:S(2)}) async-start(bf16[32,7,1024]{2,1,0:T(8,128)(2,1)} %copy.104), calls=%async_computation.8 | async-start | bytes 1048576 | tf_op jit(solution)/shard_map/all_to_all | solution.py:118
  269.8 184.7 %reduce-scatter.2.cloned.1.call-start = ((), (), s32[]{:S(2)}) async-start(), calls=%async_computation.10 | async-start | bytes 2293760 | tf_op jit(solution)/shard_map/reduce_scatter | solution.py:244
  280.5 7.3 %copy-start = (bf16[224,1024]{1,0:T(8,128)(2,1)S(1)}, bf16[224,1024]{1,0:T(8,128)(2,1)}, u32[]{:S(2)}) copy-start(bf16[224,1024]{1,0:T(8,128)(2,1)} %q_ref.1) | copy-start | bytes 1376260
  287.8 7.9 %copy-start.1 = (f32[224,4096]{1,0:T(8,128)S(1)}, f32[224,4096]{1,0:T(8,128)}, u32[]{:S(2)}) copy-start(f32[224,4096]{1,0:T(8,128)} %fusion.18) | copy-start | bytes 11010052
Sparse Core Ops, SparseCore 0:
  9.0 37.2 all-gather.4
  48.4 223.4 all-gather.6
  302.6 151.8 reduce-scatter.1

commit v3 on v1

--- a/solution.py
+++ b/solution.py
@@ -180,7 +180,11 @@
     width = q_attn.shape[1]
     heads_local = width // HD
     key_piece = lax.all_gather(k_attn, "ctx", axis=0, tiled=True)
-    value_piece = lax.all_gather(v_attn, "ctx", axis=0, tiled=True)
+    count_ctx = lax.axis_size("ctx")
+    copies = jnp.broadcast_to(v_attn[None], (count_ctx,) + v_attn.shape)
+    value_piece = lax.all_to_all(copies, "ctx", split_axis=0, concat_axis=0, tiled=True).reshape(
+        count_ctx * v_attn.shape[0], v_attn.shape[1]
+    )
     return attention_core(q_attn, key_piece, value_piece, my_index, tok_rows)
 
 

time: 416 us -> 524 us (1.26)
  waiting for transfers between devices: 256 us -> 340 us
  blocking collectives: 0 us -> 16.6 us
  local copies, waits for them, and re-layouts: 27.6 us -> 34.5 us
    all_to_all x1, waiting for transfers between devices: 10.7 us -> 189 us  [attention(): lax.all_to_all(copies, 'ctx', split_axis=0, concat_axis=0, tiled=True)]
    all_gather x1 -> x0, waiting for transfers between devices: 114 us -> none  [attention(): value_piece = lax.all_gather(v_attn, 'ctx', axis=0, tiled=True)]
    reduce_scatter x1, waiting for transfers between devices: 53.3 us -> 75.6 us  [local(): lax.psum_scatter((jnp.dot(mixed, w_conv_out, preferred_element_type=jnp.f...]
    all_to_all x0 -> x1, blocking collectives: none -> 16.6 us  [spectral_conv(): lax.all_to_all(rounded, 'ctx', split_axis=0, concat_axis=1, tiled=True)]
    all_to_all x1, waiting for transfers between devices: 19.4 us -> 10.4 us  [spectral_conv(): lax.all_to_all(turned_re.astype(jnp.bfloat16), 'ctx', split_axis=1, conca...]
    all_to_all x1, waiting for transfers between devices: 10.3 us -> 17.8 us  [spectral_conv(): lax.all_to_all(turned_im.astype(jnp.bfloat16), 'ctx', split_axis=1, conca...]
    broadcast_in_dim x0 -> x1, local copies, waits for them, and re-layouts: none -> 7.12 us  [attention(): copies = jnp.broadcast_to(v_attn[None], (count_ctx,) + v_attn.shape)]
  transfers between devices with their start and end apart: 12 -> 11, of which waited for: 11 -> 10; matrix products, arithmetic and copies ran while one was open for 17% -> 15% of each run, Pallas kernels for 0% -> 0%
where the time goes in v3:
time: 524 us; the launch traced here: 517 us
  waiting for transfers between devices  340 us (65%)
  starting transfers between devices  51.6 us (10%)
  matrix products  45.1 us (9%)
  local copies, waits for them, and re-layouts  34.5 us (7%)
  blocking collectives  16.6 us (3%)
  between operations  14.3 us (3%)
  Pallas kernels  9.31 us (2%)
  other arithmetic  5.95 us (1%)
    all_to_all x1, waiting for transfers between devices, attention(): lax.all_to_all(copies, 'ctx', split_axis=0, concat_axis=0, tiled=True)  189 us
    reduce_scatter x1, waiting for transfers between devices, local(): lax.psum_scatter((jnp.dot(mixed, w_conv_out, preferred_element_type=jnp.f...  75.6 us
    all_to_all x1, waiting for transfers between devices, spectral_conv(): lax.all_to_all(turned_im.astype(jnp.bfloat16), 'ctx', split_axis=1, conca...  17.8 us
    all_to_all x1, waiting for transfers between devices, spectral_conv(): lax.all_to_all(source_re.astype(jnp.bfloat16), 'ctx', split_axis=0, conca...  17.4 us
    all_to_all x1, blocking collectives, spectral_conv(): lax.all_to_all(rounded, 'ctx', split_axis=0, concat_axis=1, tiled=True)  16.6 us
    all_to_all x1, starting transfers between devices, spectral_conv(): lax.all_to_all(filters.reshape(1, tok_rows, groups), 'ctx', split_axis=1,...  11.3 us
  transfers between devices with their start and end apart: 11, of which 10 were waited for; matrix products, arithmetic and copies ran while one was open for 15% of the time, Pallas kernels for 0%

profile of v3, /device:TPU:1, one launch (start us, length us, event | category | flops | bytes accessed | tf_op | source)
XLA Modules:
  0.0 517.4 jit_solution(4574657123251013080)
XLA Ops:
  10.4 11.3 %all-to-all-start.3 = ((bf16[32,2,224]{2,1,0:T(2,128)(2,1)}), bf16[32,2,224]{2,1,0:T(2,128)(2,1)S(1)}, u32[]{:S(2)}, u32[]{:S(2)}) async-start(bf16[32,2,224]{2,1,0:T(2,128)(2,1)} %reshape.145), calls=%async_computation.3 | async-start | bytes 65536 | tf_op jit(solution)/shard_map/all_to_all | solution.py:53
  30.4 7.1 %all-to-all-start = ((bf16[32,2,3584]{2,1,0:T(2,128)(2,1)}), bf16[32,2,3584]{2,1,0:T(2,128)(2,1)S(1)}, u32[]{:S(2)}, u32[]{:S(2)}) async-start(bf16[32,2,3584]{2,1,0:T(2,128)(2,1)} %reshape.151), calls=%async_computation | async-start | bytes 917504 | tf_op jit(solution)/shard_map/all_to_all | solution.py:50
  40.5 7.5 %all-to-all-done = bf16[32,2,3584]{2,1,0:T(2,128)(2,1)S(1)} async-done(((bf16[32,2,3584]{2,1,0:T(2,128)(2,1)}), bf16[32,2,3584]{2,1,0:T(2,128)(2,1)S(1)}, u32[]{:S(2)}, u32[]{:S(2)}) %all-to-all-start) | async-done | bytes 458784 | tf_op jit(solution)/shard_map/all_to_all | solution.py:50
  48.0 4.5 all-to-all-start.4
  57.0 4.9 all-to-all-done.4
  61.9 4.4 all-to-all-start.5
  70.5 5.3 %all-to-all-done.5 = bf16[32,2,448]{2,1,0:T(2,128)(2,1)S(1)} async-done(((bf16[32,2,448]{2,1,0:T(2,128)(2,1)}), bf16[32,2,448]{2,1,0:T(2,128)(2,1)S(1)}, u32[]{:S(2)}, u32[]{:S(2)}) %all-to-all-start.5) | async-done | bytes 57376 | tf_op jit(solution)/shard_map/all_to_all | solution.py:80
  75.8 4.1 all-to-all-start.1
  82.3 17.4 %all-to-all-done.1 = bf16[64,7,1024]{2,1,0:T(8,128)(2,1)S(1)} async-done(((bf16[64,7,1024]{2,1,0:T(8,128)(2,1)}), bf16[64,7,1024]{2,1,0:T(8,128)(2,1)S(1)}, u32[]{:S(2)}, u32[]{:S(2)}) %all-to-all-start.1) | async-done | bytes 917536 | tf_op jit(solution)/shard_map/all_to_all | solution.py:71
  99.7 5.1 all-to-all-start.2
  115.0 9.6 %all-to-all-done.2 = bf16[64,7,1024]{2,1,0:T(8,128)(2,1)} async-done(((bf16[64,7,1024]{2,1,0:T(8,128)(2,1)}), bf16[64,7,1024]{2,1,0:T(8,128)(2,1)}, u32[]{:S(2)}, u32[]{:S(2)}) %all-to-all-start.2) | async-done | bytes 917536 | tf_op jit(solution)/shard_map/all_to_all | solution.py:74
  143.3 3.8 fusion.10
  148.9 4.6 all-to-all-start.6
  155.4 10.4 %all-to-all-done.6 = bf16[2,224,1024]{2,0,1:T(2,128)(2,1)S(1)} async-done(((bf16[2,224,1024]{2,0,1:T(2,128)(2,1)}), bf16[2,224,1024]{2,0,1:T(2,128)(2,1)S(1)}, u32[]{:S(2)}, u32[]{:S(2)}) %all-to-all-start.6) | async-done | bytes 917536 | tf_op jit(solution)/shard_map/all_to_all | solution.py:108
  165.8 5.3 %all-to-all-start.7 = ((bf16[2,224,1024]{2,0,1:T(2,128)(2,1)}), bf16[2,224,1024]{2,0,1:T(2,128)(2,1)S(1)}, u32[]{:S(2)}, u32[]{:S(2)}) async-start(bf16[2,224,1024]{2,0,1:T(2,128)(2,1)} %copy.102), calls=%async_computation.7 | async-start | bytes 1835008 | tf_op jit(solution)/shard_map/all_to_all | solution.py:111
  172.1 17.8 %all-to-all-done.7 = bf16[2,224,1024]{2,0,1:T(2,128)(2,1)S(1)} async-done(((bf16[2,224,1024]{2,0,1:T(2,128)(2,1)}), bf16[2,224,1024]{2,0,1:T(2,128)(2,1)S(1)}, u32[]{:S(2)}, u32[]{:S(2)}) %all-to-all-start.7) | async-done | bytes 917536 | tf_op jit(solution)/shard_map/all_to_all | solution.py:111
  192.4 16.6 %all_to_all.146 = bf16[32,7,1024]{2,1,0:T(8,128)(2,1)S(1)} all-to-all(bf16[32,7,1024]{2,1,0:T(8,128)(2,1)S(1)} %copy.104), channel_id=1, replica_groups=mesh['ctx'=32,'ch'=4] {'ctx'}, dimensions={0} | all-to-all | bytes 917504 | tf_op jit(solution)/shard_map/all_to_all | solution.py:118
  209.0 7.1 %broadcast_in_dim.2 = bf16[32,224,1024]{2,1,0:T(8,128)(2,1)} broadcast(bf16[224,1024]{1,0:T(8,128)(2,1)S(1)} %copy-done.6), dimensions={1,2} | broadcast | bytes 15138816 | tf_op jit(solution)/shard_map/broadcast_in_dim | solution.py:184
  216.1 5.1 all-to-all-start.9
  222.3 7.5 %fusion.18 = f32[224,4096]{1,0:T(8,128)} fusion(bf16[1024,4096]{1,0:T(8,128)(2,1)} %param.16, f32[224,1024]{1,0:T(8,128)S(1)} %reshape.138, bf16[224,1024]{1,0:T(8,128)(2,1)S(1)} %copy-done.5), kind=kOutput, calls=%fused_computation.37 | convolution fusion | flops 1879736320 | bytes 13434880 | tf_op jit(solution)/shard_map/dot_general | solution.py:242
  229.7 188.7 %all-to-all-done.9 = bf16[32,224,1024]{2,1,0:T(8,128)(2,1)} async-done(((bf16[32,224,1024]{2,1,0:T(8,128)(2,1)}), bf16[32,224,1024]{2,1,0:T(8,128)(2,1)}, u32[]{:S(2)}, u32[]{:S(2)}) %all-to-all-start.9) | async-done | bytes 14680096 | tf_op jit(solution)/shard_map/all_to_all | solution.py:185
  418.4 9.3 %shard_map.91 = bf16[224,1024]{1,0:T(8,128)(2,1)S(1)} custom-call(s32[2]{0:T(128)S(1)} %pad_add_fusion.info_ref, bf16[224,1024]{1,0:T(8,128)(2,1)S(1)} %copy-done, bf16[7168,1024]{1,0:T(8,128)(2,1)} %all-gather.2.cloned.1.call-done.k_ref, bf16[7168,1024]{1,0:T(8,128)(2,1)} %bitcast.36.v_ref), custom_call_target="tpu_custom_call" | custom-call | flops 6576668672 | bytes 30277632 | tf_op jit(solution)/shard_map/pallas_call | solution.py:203
  427.8 6.7 %fusion = bf16[224,4096]{1,0:T(8,128)(2,1)} fusion(f32[224,4096]{1,0:T(8,128)S(1)} %copy-done.1, bf16[224,1024]{1,0:T(8,128)(2,1)S(1)} %shard_map.91, bf16[1024,4096]{1,0:T(8,128)(2,1)} %param.17), kind=kOutput, calls=%fused_computation.1 | convolution fusion | flops 1880883200 | bytes 14352384 | tf_op jit(solution)/shard_map/dot_general | solution.py:243
  434.5 75.6 %reduce-scatter.2.cloned.1.call-done = bf16[56,4096]{1,0:T(8,128)(2,1)} async-done(((bf16[224,4096]{1,0:T(8,128)(2,1)}), bf16[56,4096]{1,0:T(8,128)(2,1)}) %reduce-scatter.2.cloned.1.call-update) | async-done | bytes 458768 | tf_op jit(solution)/shard_map/reduce_scatter | solution.py:240
  (82 shorter events, 63.3 us)
Async XLA Ops:
  6.5 411.9 %all-gather.2.cloned.1.call-start = ((), (), s32[]{:S(2)}) async-start(), calls=%async_computation.11 | async-start | bytes 15138816 | tf_op jit(solution)/shard_map/all_gather | solution.py:182
  10.4 20.1 %all-to-all-start.3 = ((bf16[32,2,224]{2,1,0:T(2,128)(2,1)}), bf16[32,2,224]{2,1,0:T(2,128)(2,1)S(1)}, u32[]{:S(2)}, u32[]{:S(2)}) async-start(bf16[32,2,224]{2,1,0:T(2,128)(2,1)} %reshape.145), calls=%async_computation.3 | async-start | bytes 65536 | tf_op jit(solution)/shard_map/all_to_all | solution.py:53
  30.4 17.5 %all-to-all-start = ((bf16[32,2,3584]{2,1,0:T(2,128)(2,1)}), bf16[32,2,3584]{2,1,0:T(2,128)(2,1)S(1)}, u32[]{:S(2)}, u32[]{:S(2)}) async-start(bf16[32,2,3584]{2,1,0:T(2,128)(2,1)} %reshape.151), calls=%async_computation | async-start | bytes 917504 | tf_op jit(solution)/shard_map/all_to_all | solution.py:50
  48.0 14.0 %all-to-all-start.4 = ((bf16[32,2,448]{2,1,0:T(2,128)(2,1)}), bf16[32,2,448]{2,1,0:T(2,128)(2,1)S(1)}, u32[]{:S(2)}, u32[]{:S(2)}) async-start(bf16[32,2,448]{2,1,0:T(2,128)(2,1)} %reshape.147), calls=%async_computation.4 | async-start | bytes 131072 | tf_op jit(solution)/shard_map/all_to_all | solution.py:77
  61.9 13.9 %all-to-all-start.5 = ((bf16[32,2,448]{2,1,0:T(2,128)(2,1)}), bf16[32,2,448]{2,1,0:T(2,128)(2,1)S(1)}, u32[]{:S(2)}, u32[]{:S(2)}) async-start(bf16[32,2,448]{2,1,0:T(2,128)(2,1)} %reshape.149), calls=%async_computation.5 | async-start | bytes 131072 | tf_op jit(solution)/shard_map/all_to_all | solution.py:80
  70.5 10.2 %copy-start.4 = (bf16[64,7,1024]{2,0,1:T(8,128)(2,1)S(1)}, bf16[64,7,1024]{2,0,1:T(8,128)(2,1)}, u32[]{:S(2)}) copy-start(bf16[64,7,1024]{2,0,1:T(8,128)(2,1)} %get-tuple-element.8) | copy-start | bytes 2752516
  75.8 23.8 %all-to-all-start.1 = ((bf16[64,7,1024]{2,1,0:T(8,128)(2,1)}), bf16[64,7,1024]{2,1,0:T(8,128)(2,1)S(1)}, u32[]{:S(2)}, u32[]{:S(2)}) async-start(bf16[64,7,1024]{2,1,0:T(8,128)(2,1)} %copy.77), calls=%async_computation.1 | async-start | bytes 2097152 | tf_op jit(solution)/shard_map/all_to_all | solution.py:71
  99.7 24.9 %all-to-all-start.2 = ((bf16[64,7,1024]{2,1,0:T(8,128)(2,1)}), bf16[64,7,1024]{2,1,0:T(8,128)(2,1)}, u32[]{:S(2)}, u32[]{:S(2)}) async-start(bf16[64,7,1024]{2,1,0:T(8,128)(2,1)} %copy.80), calls=%async_computation.2 | async-start | bytes 2097152 | tf_op jit(solution)/shard_map/all_to_all | solution.py:74
  130.5 2.0 copy-start.2
  130.5 2.0 copy-start.3
  148.9 16.9 %all-to-all-start.6 = ((bf16[2,224,1024]{2,0,1:T(2,128)(2,1)}), bf16[2,224,1024]{2,0,1:T(2,128)(2,1)S(1)}, u32[]{:S(2)}, u32[]{:S(2)}) async-start(bf16[2,224,1024]{2,0,1:T(2,128)(2,1)} %copy.100), calls=%async_computation.6 | async-start | bytes 1835008 | tf_op jit(solution)/shard_map/all_to_all | solution.py:108
  165.8 24.1 %all-to-all-start.7 = ((bf16[2,224,1024]{2,0,1:T(2,128)(2,1)}), bf16[2,224,1024]{2,0,1:T(2,128)(2,1)S(1)}, u32[]{:S(2)}, u32[]{:S(2)}) async-start(bf16[2,224,1024]{2,0,1:T(2,128)(2,1)} %copy.102), calls=%async_computation.7 | async-start | bytes 1835008 | tf_op jit(solution)/shard_map/all_to_all | solution.py:111
  191.5 17.5 %copy-start.6 = (bf16[224,1024]{1,0:T(8,128)(2,1)S(1)}, bf16[224,1024]{1,0:T(8,128)(2,1)}, u32[]{:S(2)}) copy-start(bf16[224,1024]{1,0:T(8,128)(2,1)} %param.15) | copy-start | bytes 1376260
  216.1 202.3 %all-to-all-start.9 = ((bf16[32,224,1024]{2,1,0:T(8,128)(2,1)}), bf16[32,224,1024]{2,1,0:T(8,128)(2,1)}, u32[]{:S(2)}, u32[]{:S(2)}) async-start(bf16[32,224,1024]{2,1,0:T(8,128)(2,1)} %broadcast_in_dim.2), calls=%async_computation.9 | async-start | bytes 29360128 | tf_op jit(solution)/shard_map/all_to_all | solution.py:185
  221.3 1.0 copy-start.5
  221.3 288.9 %reduce-scatter.2.cloned.1.call-start = ((), (), s32[]{:S(2)}) async-start(), calls=%async_computation.12 | async-start | bytes 2293760 | tf_op jit(solution)/shard_map/reduce_scatter | solution.py:240
  222.3 196.2 %copy-start = (bf16[224,1024]{1,0:T(8,128)(2,1)S(1)}, bf16[224,1024]{1,0:T(8,128)(2,1)}, u32[]{:S(2)}) copy-start(bf16[224,1024]{1,0:T(8,128)(2,1)} %q_ref.1) | copy-start | bytes 1376260
  418.4 9.3 %copy-start.1 = (f32[224,4096]{1,0:T(8,128)S(1)}, f32[224,4096]{1,0:T(8,128)}, u32[]{:S(2)}) copy-start(f32[224,4096]{1,0:T(8,128)} %fusion.18) | copy-start | bytes 11010052
Sparse Core Ops, SparseCore 0:
  10.4 178.3 all-gather.1
  434.7 75.4 reduce-scatter.1

commit v4 on v2

--- a/solution.py
+++ b/solution.py
@@ -119,123 +119,128 @@
     return returned.reshape(tok_rows, chans)
 
 
-CTX = ("z", "yh", "x")
-
-
-def flash_kernel(info_ref, q_ref, k_ref, v_ref, o_ref, m_sc, l_sc, acc_sc, *, heads, tok_rows, x_size, yh_size, scale):
+CTX = ("zh", "zl", "yh", "x")
+HALF = ("zl", "yh", "x")
+
+
+def flash_kernel(info_ref, q_ref, k_ref, v_ref, acc_ref, m_ref, l_ref, *, heads, tok_rows, key_block, scale):
     j = pl.program_id(0)
-    my_ctx = info_ref[0]
+    q_first = info_ref[0]
     last_block = info_ref[1] - 1
-    z = j // x_size
-    x = j % x_size
+    key_first = j * key_block
 
     @pl.when(j == 0)
     def _():
-        m_sc[...] = jnp.full_like(m_sc, neg_large)
-        l_sc[...] = jnp.zeros_like(l_sc)
-        acc_sc[...] = jnp.zeros_like(acc_sc)
-
-    def step(half, masked):
+        m_ref[...] = jnp.full_like(m_ref, neg_large)
+        l_ref[...] = jnp.zeros_like(l_ref)
+        acc_ref[...] = jnp.zeros_like(acc_ref)
+
+    def step(masked):
         if masked:
-            query_pos = lax.broadcasted_iota(jnp.int32, (tok_rows, tok_rows), 0)
-            key_pos = lax.broadcasted_iota(jnp.int32, (tok_rows, tok_rows), 1)
+            query_pos = q_first + lax.broadcasted_iota(jnp.int32, (tok_rows, key_block), 0)
+            key_pos = key_first + lax.broadcasted_iota(jnp.int32, (tok_rows, key_block), 1)
             allowed = key_pos <= query_pos
         for h in range(heads):
             cols = slice(h * HD, (h + 1) * HD)
             scores = lax.dot_general(
-                q_ref[:, cols], k_ref[half, :, cols], (((1,), (1,)), ((), ())),
+                q_ref[:, cols], k_ref[:, cols], (((1,), (1,)), ((), ())),
                 preferred_element_type=jnp.float32,
             ) * scale
             if masked:
                 scores = jnp.where(allowed, scores, neg_large)
-            m_prev = m_sc[h]
+            m_prev = m_ref[h]
             m_new = jnp.maximum(m_prev, jnp.max(scores, axis=1, keepdims=True))
             weights = jnp.exp(scores - m_new)
             if masked:
                 weights = jnp.where(allowed, weights, 0.0)
             factor = jnp.exp(m_prev - m_new)
-            l_sc[h] = l_sc[h] * factor + jnp.sum(weights, axis=1, keepdims=True)
-            acc_sc[:, cols] = acc_sc[:, cols] * factor + jnp.dot(
-                weights.astype(jnp.bfloat16), v_ref[half, :, cols], preferred_element_type=jnp.float32
+            l_ref[h] = l_ref[h] * factor + jnp.sum(weights, axis=1, keepdims=True)
+            acc_ref[:, cols] = acc_ref[:, cols] * factor + jnp.dot(
+                weights.astype(jnp.bfloat16), v_ref[:, cols], preferred_element_type=jnp.float32
             )
-            m_sc[h] = m_new
-
-    for half in range(yh_size):
-        block_ctx = (z * yh_size + half) * x_size + x
-        active = j <= last_block
-
-        @pl.when(jnp.logical_and(active, block_ctx < my_ctx))
-        def _():
-            step(half, False)
-
-        @pl.when(jnp.logical_and(active, block_ctx == my_ctx))
-        def _():
-            step(half, True)
-
-    @pl.when(j == last_block)
+            m_ref[h] = m_new
+
+    full = key_first + key_block <= q_first
+
+    @pl.when(jnp.logical_and(j <= last_block, full))
     def _():
-        for h in range(heads):
-            cols = slice(h * HD, (h + 1) * HD)
-            o_ref[:, cols] = (acc_sc[:, cols] / l_sc[h]).astype(o_ref.dtype)
+        step(False)
+
+    @pl.when(jnp.logical_and(j <= last_block, jnp.logical_not(full)))
+    def _():
+        step(True)
+
+
+def flash_partial(queries, keys, values, q_first, needed, key_block):
+    tok_rows, width = queries.shape
+    heads = width // HD
+    total_rows = keys.shape[0]
+    info = jnp.stack([q_first, needed]).astype(jnp.int32)
+    kernel = partial(flash_kernel, heads=heads, tok_rows=tok_rows, key_block=key_block, scale=HD ** (-0.5))
+    kv_spec = pl.BlockSpec((key_block, width), lambda j, info: (jnp.minimum(j, info[1] - 1), 0))
+    stat_spec = pl.BlockSpec((heads, tok_rows, 1), lambda j, info: (0, 0, 0))
+    return pl.pallas_call(
+        kernel,
+        out_shape=(
+            jax.ShapeDtypeStruct((tok_rows, width), jnp.float32),
+            jax.ShapeDtypeStruct((heads, tok_rows, 1), jnp.float32),
+            jax.ShapeDtypeStruct((heads, tok_rows, 1), jnp.float32),
+        ),
+        grid_spec=pltpu.PrefetchScalarGridSpec(
+            num_scalar_prefetch=1,
+            grid=(total_rows // key_block,),
+            in_specs=[pl.BlockSpec((tok_rows, width), lambda j, info: (0, 0)), kv_spec, kv_spec],
+            out_specs=[pl.BlockSpec((tok_rows, width), lambda j, info: (0, 0)), stat_spec, stat_spec],
+        ),
+        compiler_params=pltpu.CompilerParams(
+            dimension_semantics=("arbitrary",), vmem_limit_bytes=48 * 1024 * 1024
+        ),
+        cost_estimate=pl.CostEstimate(
+            flops=4 * tok_rows * total_rows * width,
+            transcendentals=heads * tok_rows * total_rows,
+            bytes_accessed=2 * total_rows * width * 2 + tok_rows * width * 6,
+        ),
+    )(info, queries, keys, values)
 
 
 def attention(q_attn, k_attn, v_attn, tok_rows):
     width = q_attn.shape[1]
-    heads_local = width // HD
-    z_size, yh_size, x_size = (lax.axis_size(name) for name in CTX)
-    z_me, yh_me, x_me = (lax.axis_index(name) for name in CTX)
-    my_ctx = (z_me * yh_size + yh_me) * x_size + x_me
-    both = jnp.stack([k_attn, v_attn])
-    across = lax.all_gather(both, "yh", axis=0)
-    gathered = lax.all_gather(across, ("z", "x"), axis=0)
-    count_blocks = z_size * x_size
-    needed = z_me * x_size + jnp.where(yh_me == 0, x_me + 1, x_size)
-    info = jnp.stack([my_ctx, needed]).astype(jnp.int32)
-    kernel = partial(
-        flash_kernel, heads=heads_local, tok_rows=tok_rows, x_size=x_size, yh_size=yh_size,
-        scale=HD ** (-0.5),
-    )
-    total_rows = count_blocks * yh_size * tok_rows
-    return pl.pallas_call(
-        kernel,
-        out_shape=jax.ShapeDtypeStruct((tok_rows, width), jnp.bfloat16),
-        grid_spec=pltpu.PrefetchScalarGridSpec(
-            num_scalar_prefetch=1,
-            grid=(count_blocks,),
-            in_specs=[
-                pl.BlockSpec((tok_rows, width), lambda j, info: (0, 0)),
-                pl.BlockSpec(
-                    (None, yh_size, None, tok_rows, width),
-                    lambda j, info: (jnp.minimum(j, info[1] - 1), 0, 0, 0, 0),
-                ),
-                pl.BlockSpec(
-                    (None, yh_size, None, tok_rows, width),
-                    lambda j, info: (jnp.minimum(j, info[1] - 1), 0, 1, 0, 0),
-                ),
-            ],
-            out_specs=pl.BlockSpec((tok_rows, width), lambda j, info: (0, 0)),
-            scratch_shapes=[
-                pltpu.VMEM((heads_local, tok_rows, 1), jnp.float32),
-                pltpu.VMEM((heads_local, tok_rows, 1), jnp.float32),
-                pltpu.VMEM((tok_rows, width), jnp.float32),
-            ],
-        ),
-        compiler_params=pltpu.CompilerParams(
-            dimension_semantics=("arbitrary",), vmem_limit_bytes=48 * 1024 * 1024
-        ),
-        cost_estimate=pl.CostEstimate(
-            flops=4 * tok_rows * total_rows * width,
-            transcendentals=heads_local * tok_rows * total_rows,
-            bytes_accessed=2 * total_rows * width * 2 + 2 * tok_rows * width * 2,
-        ),
-    )(info, q_attn, gathered, gathered)
+    heads = width // HD
+    upper = lax.axis_index("zh")
+    half_count = 1
+    for name in HALF:
+        half_count = half_count * lax.axis_size(name)
+    my_index = lax.axis_index(CTX)
+    local_index = my_index - upper * half_count
+    key_half = lax.all_gather(k_attn, HALF, axis=0, tiled=True)
+    value_half = lax.all_gather(v_attn, HALF, axis=0, tiled=True)
+    half_rows = key_half.shape[0]
+    key_block = 896 if half_rows % 896 == 0 else tok_rows
+    visiting = lax.ppermute(q_attn, "zh", [(1, 0)])
+    cross = flash_partial(
+        visiting, key_half, value_half, jnp.int32(half_rows), jnp.int32(half_rows // key_block), key_block
+    )
+    cross_acc, cross_max, cross_total = lax.ppermute(cross, "zh", [(0, 1)])
+    needed = ((local_index + 1) * tok_rows + key_block - 1) // key_block
+    own_acc, own_max, own_total = flash_partial(
+        q_attn, key_half, value_half, local_index * tok_rows, needed, key_block
+    )
+    cross_max = jnp.where(upper == 0, neg_large, cross_max)
+    top = jnp.maximum(own_max, cross_max)
+    own_scale = jnp.exp(own_max - top)
+    cross_scale = jnp.exp(cross_max - top)
+    totals = own_total * own_scale + cross_total * cross_scale
+    to_rows = lambda stat: stat.transpose(1, 0, 2)
+    merged = (
+        own_acc.reshape(tok_rows, heads, HD) * to_rows(own_scale)
+        + cross_acc.reshape(tok_rows, heads, HD) * to_rows(cross_scale)
+    ) / to_rows(totals)
+    return merged.reshape(tok_rows, width).astype(jnp.bfloat16)
 
 
 def local(q_conv, k_conv, v_conv, conv_filter, q_attn, k_attn, v_attn, w_conv_out, w_attn_out):
-    z_size, yh_size, x_size = (lax.axis_size(name) for name in CTX)
-    z_me, yh_me, x_me = (lax.axis_index(name) for name in CTX)
-    count_ctx = z_size * yh_size * x_size
-    my_index = (z_me * yh_size + yh_me) * x_size + x_me
+    count_ctx = lax.axis_size(CTX)
+    my_index = lax.axis_index(CTX)
     tok_rows = q_conv.shape[0]
     gated = (k_conv.astype(jnp.float32) * v_conv.astype(jnp.float32)).astype(jnp.bfloat16)
     conv = spectral_conv(gated, conv_filter, my_index, tok_rows, count_ctx)
@@ -254,11 +259,8 @@
 
 def solution(mesh):
     ctx_size, ch_size = mesh.devices.shape
-    x_size = 4
-    yh_size = 2
-    z_size = ctx_size // (x_size * yh_size)
     split_mesh = jax.sharding.Mesh(
-        mesh.devices.reshape(z_size, yh_size, x_size, ch_size), ("z", "yh", "x", "ch")
+        mesh.devices.reshape(2, 2, 2, ctx_size // 8, ch_size), CTX + ("ch",)
     )
     tokens = P(CTX, "ch")
     return jax.shard_map(

time: 468 us -> 402 us (0.86)
  waiting for transfers between devices: 316 us -> 149 us
  starting transfers between devices: 44.8 us -> 104 us
  Pallas kernels: 7.87 us -> 31.6 us
  local copies, waits for them, and re-layouts: 26.9 us -> 41.3 us
    reduce_scatter x1, waiting for transfers between devices: 152 us -> 38.3 us  [local(): lax.psum_scatter((jnp.dot(mixed, w_conv_out, preferred_element_type=jnp.f...]
    all_gather x2, waiting for transfers between devices: 37.4 us -> 0.01 us  [the longest x1 0.01 us: attention(): key_half = lax.all_gather(k_attn, HALF, axis=0, tiled=True)]
    all_to_all x1, starting transfers between devices: 4.58 us -> 38.4 us  [spectral_conv(): lax.all_to_all(filter_im.astype(jnp.bfloat16), CTX, split_axis=0, concat_...]
    pallas_call x1 -> x2, Pallas kernels: 7.87 us -> 31.6 us  [flash_partial(): pl.pallas_call(kernel, out_shape=(jax.ShapeDtypeStruct((tok_rows, width),...]
    all_to_all x1, starting transfers between devices: 4.37 us -> 13.1 us  [spectral_conv(): lax.all_to_all(turned_im.astype(jnp.bfloat16), CTX, split_axis=1, concat_...]
    all_to_all x1, waiting for transfers between devices: 22.7 us -> 14 us  [spectral_conv(): lax.all_to_all(turned_im.astype(jnp.bfloat16), CTX, split_axis=1, concat_...]
    all_to_all x1, waiting for transfers between devices: 23.2 us -> 15.8 us  [spectral_conv(): lax.all_to_all(turned_re.astype(jnp.bfloat16), CTX, split_axis=1, concat_...]
    all_to_all x1, waiting for transfers between devices: 25.9 us -> 19.1 us  [spectral_conv(): lax.all_to_all(source_re.astype(jnp.bfloat16), CTX, split_axis=0, concat_...]
  transfers between devices with their start and end apart: 12 -> 16, of which waited for: 11 -> 11; matrix products, arithmetic and copies ran while one was open for 15% -> 21% of each run, Pallas kernels for 0% -> 2%
where the time goes in v4:
time: 402 us; the launch traced here: 395 us
  waiting for transfers between devices  149 us (37%)
  starting transfers between devices  104 us (26%)
  matrix products  45.6 us (11%)
  local copies, waits for them, and re-layouts  41.3 us (10%)
  Pallas kernels  31.6 us (8%)
  between operations  13.9 us (3%)
  other arithmetic  9.32 us (2%)
    all_to_all x1, starting transfers between devices, spectral_conv(): lax.all_to_all(filter_im.astype(jnp.bfloat16), CTX, split_axis=0, concat_...  38.4 us
    reduce_scatter x1, waiting for transfers between devices, local(): lax.psum_scatter((jnp.dot(mixed, w_conv_out, preferred_element_type=jnp.f...  38.3 us
    pallas_call x2, Pallas kernels, flash_partial(): pl.pallas_call(kernel, out_shape=(jax.ShapeDtypeStruct((tok_rows, width),...  31.6 us
    all_to_all x1, waiting for transfers between devices, spectral_conv(): lax.all_to_all(source_im.astype(jnp.bfloat16), CTX, split_axis=0, concat_...  22.4 us
    all_to_all x1, waiting for transfers between devices, spectral_conv(): lax.all_to_all(source_re.astype(jnp.bfloat16), CTX, split_axis=0, concat_...  19.1 us
    all_to_all x1, waiting for transfers between devices, spectral_conv(): lax.all_to_all(turned_re.astype(jnp.bfloat16), CTX, split_axis=1, concat_...  15.8 us
    all_to_all x1, waiting for transfers between devices, spectral_conv(): lax.all_to_all(turned_im.astype(jnp.bfloat16), CTX, split_axis=1, concat_...  14 us
    all_to_all x1, waiting for transfers between devices, spectral_conv(): lax.all_to_all(gated.reshape(1, tok_rows, chans), CTX, split_axis=1, conc...  13.6 us
  transfers between devices with their start and end apart: 16, of which 11 were waited for; matrix products, arithmetic and copies ran while one was open for 21% of the time, Pallas kernels for 2%

profile of v4, /device:TPU:1, one launch (start us, length us, event | category | flops | bytes accessed | tf_op | source)
XLA Modules:
  0.0 394.8 jit_solution(513891278020764538)
XLA Ops:
  11.1 11.3 %all-to-all-start.3 = ((bf16[32,2,224]{2,1,0:T(2,128)(2,1)}), bf16[32,2,224]{2,1,0:T(2,128)(2,1)S(1)}, u32[]{:S(2)}, u32[]{:S(2)}) async-start(bf16[32,2,224]{2,1,0:T(2,128)(2,1)} %reshape.146), calls=%async_computation.3 | async-start | bytes 65536 | tf_op jit(solution)/shard_map/all_to_all | solution.py:53
  31.4 6.9 %all-to-all-start = ((bf16[32,2,3584]{2,1,0:T(2,128)(2,1)}), bf16[32,2,3584]{2,1,0:T(2,128)(2,1)S(1)}, u32[]{:S(2)}, u32[]{:S(2)}) async-start(bf16[32,2,3584]{2,1,0:T(2,128)(2,1)} %reshape.152), calls=%async_computation | async-start | bytes 917504 | tf_op jit(solution)/shard_map/all_to_all | solution.py:50
  41.2 13.6 %all-to-all-done = bf16[32,2,3584]{2,1,0:T(2,128)(2,1)S(1)} async-done(((bf16[32,2,3584]{2,1,0:T(2,128)(2,1)}), bf16[32,2,3584]{2,1,0:T(2,128)(2,1)S(1)}, u32[]{:S(2)}, u32[]{:S(2)}) %all-to-all-start) | async-done | bytes 458784 | tf_op jit(solution)/shard_map/all_to_all | solution.py:50
  54.9 4.5 %all-to-all-start.4 = ((bf16[32,2,448]{2,1,0:T(2,128)(2,1)}), bf16[32,2,448]{2,1,0:T(2,128)(2,1)S(1)}, u32[]{:S(2)}, u32[]{:S(2)}) async-start(bf16[32,2,448]{2,1,0:T(2,128)(2,1)} %reshape.148), calls=%async_computation.4 | async-start | bytes 131072 | tf_op jit(solution)/shard_map/all_to_all | solution.py:77
  63.9 4.6 %all-to-all-done.4 = bf16[32,2,448]{2,1,0:T(2,128)(2,1)S(1)} async-done(((bf16[32,2,448]{2,1,0:T(2,128)(2,1)}), bf16[32,2,448]{2,1,0:T(2,128)(2,1)S(1)}, u32[]{:S(2)}, u32[]{:S(2)}) %all-to-all-start.4) | async-done | bytes 57376 | tf_op jit(solution)/shard_map/all_to_all | solution.py:77
  68.5 38.4 %all-to-all-start.5 = ((bf16[32,2,448]{2,1,0:T(2,128)(2,1)}), bf16[32,2,448]{2,1,0:T(2,128)(2,1)S(1)}, u32[]{:S(2)}, u32[]{:S(2)}) async-start(bf16[32,2,448]{2,1,0:T(2,128)(2,1)} %reshape.150), calls=%async_computation.5 | async-start | bytes 131072 | tf_op jit(solution)/shard_map/all_to_all | solution.py:80
  110.2 5.6 %all-to-all-done.5 = bf16[32,2,448]{2,1,0:T(2,128)(2,1)S(1)} async-done(((bf16[32,2,448]{2,1,0:T(2,128)(2,1)}), bf16[32,2,448]{2,1,0:T(2,128)(2,1)S(1)}, u32[]{:S(2)}, u32[]{:S(2)}) %all-to-all-start.5) | async-done | bytes 57376 | tf_op jit(solution)/shard_map/all_to_all | solution.py:80
  115.8 3.9 all-to-all-start.1
  122.1 19.1 %all-to-all-done.1 = bf16[64,7,1024]{2,1,0:T(8,128)(2,1)S(1)} async-done(((bf16[64,7,1024]{2,1,0:T(8,128)(2,1)}), bf16[64,7,1024]{2,1,0:T(8,128)(2,1)S(1)}, u32[]{:S(2)}, u32[]{:S(2)}) %all-to-all-start.1) | async-done | bytes 917536 | tf_op jit(solution)/shard_map/all_to_all | solution.py:71
  141.2 4.8 %all-to-all-start.2 = ((bf16[64,7,1024]{2,1,0:T(8,128)(2,1)}), bf16[64,7,1024]{2,1,0:T(8,128)(2,1)}, u32[]{:S(2)}, u32[]{:S(2)}) async-start(bf16[64,7,1024]{2,1,0:T(8,128)(2,1)} %copy.137), calls=%async_computation.2 | async-start | bytes 2097152 | tf_op jit(solution)/shard_map/all_to_all | solution.py:74
  156.1 22.4 %all-to-all-done.2 = bf16[64,7,1024]{2,1,0:T(8,128)(2,1)} async-done(((bf16[64,7,1024]{2,1,0:T(8,128)(2,1)}), bf16[64,7,1024]{2,1,0:T(8,128)(2,1)}, u32[]{:S(2)}, u32[]{:S(2)}) %all-to-all-start.2) | async-done | bytes 917536 | tf_op jit(solution)/shard_map/all_to_all | solution.py:74
  197.4 3.8 fusion.12
  203.1 9.0 %all-to-all-start.6 = ((bf16[2,224,1024]{2,0,1:T(2,128)(2,1)}), bf16[2,224,1024]{2,0,1:T(2,128)(2,1)S(1)}, u32[]{:S(2)}, u32[]{:S(2)}) async-start(bf16[2,224,1024]{2,0,1:T(2,128)(2,1)} %copy.157), calls=%async_computation.6 | async-start | bytes 1835008 | tf_op jit(solution)/shard_map/all_to_all | solution.py:108
  214.0 15.8 %all-to-all-done.6 = bf16[2,224,1024]{2,0,1:T(2,128)(2,1)S(1)} async-done(((bf16[2,224,1024]{2,0,1:T(2,128)(2,1)}), bf16[2,224,1024]{2,0,1:T(2,128)(2,1)S(1)}, u32[]{:S(2)}, u32[]{:S(2)}) %all-to-all-start.6) | async-done | bytes 917536 | tf_op jit(solution)/shard_map/all_to_all | solution.py:108
  229.8 13.1 %all-to-all-start.7 = ((bf16[2,224,1024]{2,0,1:T(2,128)(2,1)}), bf16[2,224,1024]{2,0,1:T(2,128)(2,1)S(1)}, u32[]{:S(2)}, u32[]{:S(2)}) async-start(bf16[2,224,1024]{2,0,1:T(2,128)(2,1)} %copy.159), calls=%async_computation.7 | async-start | bytes 1835008 | tf_op jit(solution)/shard_map/all_to_all | solution.py:111
  243.9 14.0 %all-to-all-done.7 = bf16[2,224,1024]{2,0,1:T(2,128)(2,1)S(1)} async-done(((bf16[2,224,1024]{2,0,1:T(2,128)(2,1)}), bf16[2,224,1024]{2,0,1:T(2,128)(2,1)S(1)}, u32[]{:S(2)}, u32[]{:S(2)}) %all-to-all-start.7) | async-done | bytes 917536 | tf_op jit(solution)/shard_map/all_to_all | solution.py:111
  264.3 5.7 %all-to-all-start.8 = ((bf16[32,7,1024]{2,1,0:T(8,128)(2,1)}), bf16[32,7,1024]{2,1,0:T(8,128)(2,1)S(1)}, u32[]{:S(2)}, u32[]{:S(2)}) async-start(bf16[32,7,1024]{2,1,0:T(8,128)(2,1)} %copy.161), calls=%async_computation.8 | async-start | bytes 1048576 | tf_op jit(solution)/shard_map/all_to_all | solution.py:118
  271.4 9.5 %all-to-all-done.8 = bf16[32,7,1024]{2,1,0:T(8,128)(2,1)S(1)} async-done(((bf16[32,7,1024]{2,1,0:T(8,128)(2,1)}), bf16[32,7,1024]{2,1,0:T(8,128)(2,1)S(1)}, u32[]{:S(2)}, u32[]{:S(2)}) %all-to-all-start.8) | async-done | bytes 458784 | tf_op jit(solution)/shard_map/all_to_all | solution.py:118
  281.0 7.3 %fusion.22 = f32[224,4096]{1,0:T(8,128)} fusion(bf16[1024,4096]{1,0:T(8,128)(2,1)} %param.16, f32[224,1024]{1,0:T(8,128)S(1)} %reshape.139, bf16[224,1024]{1,0:T(8,128)(2,1)S(1)} %copy-done.5), kind=kOutput, calls=%fused_computation.47 | convolution fusion | flops 1879736320 | bytes 13434880 | tf_op jit(solution)/shard_map/dot_general | solution.py:251
  290.7 23.2 %shard_map.92 = (f32[224,1024]{1,0:T(8,128)}, f32[8,224,1]{2,1,0:T(8,128)S(1)}, f32[8,224,1]{2,1,0:T(8,128)S(1)}) custom-call(s32[2]{0:T(128)S(1)} %copy-done.1, bf16[224,1024]{1,0:T(8,128)(2,1)S(1)} %collective-permute-done.q_ref, bf16[3584,1024]{1,0:T(8,128)(2,1)} %all-gather.3.cloned.1.call-done.k_ref, bf16[3584,1024]{1,0:T(8,128)(2,1)} %all-gather.5.cloned.1.call-done.v_ref), custom_call_target="tpu_custom_call" | custom-call | flops 3288334336 | bytes 16056320 | tf_op jit(solution)/shard_map/pallas_call | solution.py:182
  319.4 8.4 %shard_map.91 = (f32[224,1024]{1,0:T(8,128)S(1)}, f32[8,224,1]{2,1,0:T(8,128)S(1)}, f32[8,224,1]{2,1,0:T(8,128)S(1)}) custom-call(s32[2]{0:T(128)S(1)} %pad_add_fusion.info_ref, bf16[224,1024]{1,0:T(8,128)(2,1)S(1)} %copy-done, bf16[3584,1024]{1,0:T(8,128)(2,1)} %all-gather.3.cloned.1.call-done.k_ref, bf16[3584,1024]{1,0:T(8,128)(2,1)} %all-gather.5.cloned.1.call-done.v_ref), custom_call_target="tpu_custom_call" | custom-call | flops 3288334336 | bytes 16056320 | tf_op jit(solution)/shard_map/pallas_call | solution.py:182
  330.4 3.4 fusion.29
  341.3 8.4 %fusion = bf16[224,4096]{1,0:T(8,128)(2,1)} fusion(f32[224,4096]{1,0:T(8,128)} %fusion.22, bf16[1024,4096]{1,0:T(8,128)(2,1)} %param.17, f32[28,8,8,128]{3,2,1,0:T(8,128)S(1)} %bitcast.164, f32[224,1024]{1,0:T(8,128)} %collective-permute-done.2, f32[28,8,8,128]{3,2,1,0:T(8,128)S(1)} %bitcast.163, f32[224,1024]{1,0:T(8,128)S(1)} %get-tuple-element.11, ...), kind=kOutput, calls=%fused_computation.1 | convolution fusion | flops 1882030080 | bytes 18481152 | tf_op jit(solution)/shard_map/dot_general | solution.py:252
  349.7 38.3 %reduce-scatter.2.cloned.1.call-done = bf16[56,4096]{1,0:T(8,128)(2,1)} async-done(((bf16[224,4096]{1,0:T(8,128)(2,1)}), bf16[56,4096]{1,0:T(8,128)(2,1)}) %reduce-scatter.2.cloned.1.call-update) | async-done | bytes 458768 | tf_op jit(solution)/shard_map/reduce_scatter | solution.py:249
  (102 shorter events, 85.8 us)
Async XLA Ops:
  6.5 284.2 %all-gather.3.cloned.1.call-start = ((), (), s32[]{:S(2)}) async-start(), calls=%async_computation.10 | async-start | bytes 7798784 | tf_op jit(solution)/shard_map/all_gather | solution.py:215
  7.3 283.5 %all-gather.5.cloned.1.call-start = ((), (), s32[]{:S(2)}) async-start(), calls=%async_computation.11 | async-start | bytes 7798784 | tf_op jit(solution)/shard_map/all_gather | solution.py:216
  11.1 20.3 %all-to-all-start.3 = ((bf16[32,2,224]{2,1,0:T(2,128)(2,1)}), bf16[32,2,224]{2,1,0:T(2,128)(2,1)S(1)}, u32[]{:S(2)}, u32[]{:S(2)}) async-start(bf16[32,2,224]{2,1,0:T(2,128)(2,1)} %reshape.146), calls=%async_computation.3 | async-start | bytes 65536 | tf_op jit(solution)/shard_map/all_to_all | solution.py:53
  31.4 23.5 %all-to-all-start = ((bf16[32,2,3584]{2,1,0:T(2,128)(2,1)}), bf16[32,2,3584]{2,1,0:T(2,128)(2,1)S(1)}, u32[]{:S(2)}, u32[]{:S(2)}) async-start(bf16[32,2,3584]{2,1,0:T(2,128)(2,1)} %reshape.152), calls=%async_computation | async-start | bytes 917504 | tf_op jit(solution)/shard_map/all_to_all | solution.py:50
  54.9 13.7 %all-to-all-start.4 = ((bf16[32,2,448]{2,1,0:T(2,128)(2,1)}), bf16[32,2,448]{2,1,0:T(2,128)(2,1)S(1)}, u32[]{:S(2)}, u32[]{:S(2)}) async-start(bf16[32,2,448]{2,1,0:T(2,128)(2,1)} %reshape.148), calls=%async_computation.4 | async-start | bytes 131072 | tf_op jit(solution)/shard_map/all_to_all | solution.py:77
  68.5 47.3 %all-to-all-start.5 = ((bf16[32,2,448]{2,1,0:T(2,128)(2,1)}), bf16[32,2,448]{2,1,0:T(2,128)(2,1)S(1)}, u32[]{:S(2)}, u32[]{:S(2)}) async-start(bf16[32,2,448]{2,1,0:T(2,128)(2,1)} %reshape.150), calls=%async_computation.5 | async-start | bytes 131072 | tf_op jit(solution)/shard_map/all_to_all | solution.py:80
  115.8 25.4 %all-to-all-start.1 = ((bf16[64,7,1024]{2,1,0:T(8,128)(2,1)}), bf16[64,7,1024]{2,1,0:T(8,128)(2,1)S(1)}, u32[]{:S(2)}, u32[]{:S(2)}) async-start(bf16[64,7,1024]{2,1,0:T(8,128)(2,1)} %copy.134), calls=%async_computation.1 | async-start | bytes 2097152 | tf_op jit(solution)/shard_map/all_to_all | solution.py:71
  141.2 37.4 %all-to-all-start.2 = ((bf16[64,7,1024]{2,1,0:T(8,128)(2,1)}), bf16[64,7,1024]{2,1,0:T(8,128)(2,1)}, u32[]{:S(2)}, u32[]{:S(2)}) async-start(bf16[64,7,1024]{2,1,0:T(8,128)(2,1)} %copy.137), calls=%async_computation.2 | async-start | bytes 2097152 | tf_op jit(solution)/shard_map/all_to_all | solution.py:74
  184.5 2.0 copy-start.2
  184.6 2.1 copy-start.3
  203.1 26.7 %all-to-all-start.6 = ((bf16[2,224,1024]{2,0,1:T(2,128)(2,1)}), bf16[2,224,1024]{2,0,1:T(2,128)(2,1)S(1)}, u32[]{:S(2)}, u32[]{:S(2)}) async-start(bf16[2,224,1024]{2,0,1:T(2,128)(2,1)} %copy.157), calls=%async_computation.6 | async-start | bytes 1835008 | tf_op jit(solution)/shard_map/all_to_all | solution.py:108
  229.8 28.1 %all-to-all-start.7 = ((bf16[2,224,1024]{2,0,1:T(2,128)(2,1)}), bf16[2,224,1024]{2,0,1:T(2,128)(2,1)S(1)}, u32[]{:S(2)}, u32[]{:S(2)}) async-start(bf16[2,224,1024]{2,0,1:T(2,128)(2,1)} %copy.159), calls=%async_computation.7 | async-start | bytes 1835008 | tf_op jit(solution)/shard_map/all_to_all | solution.py:111
  262.6 7.4 %copy-start = (bf16[224,1024]{1,0:T(8,128)(2,1)S(1)}, bf16[224,1024]{1,0:T(8,128)(2,1)}, u32[]{:S(2)}) copy-start(bf16[224,1024]{1,0:T(8,128)(2,1)} %q_ref.1) | copy-start | bytes 1376260
  263.2 17.8 %copy-start.5 = (bf16[224,1024]{1,0:T(8,128)(2,1)S(1)}, bf16[224,1024]{1,0:T(8,128)(2,1)}, u32[]{:S(2)}) copy-start(bf16[224,1024]{1,0:T(8,128)(2,1)} %param.9) | copy-start | bytes 1376260
  264.3 16.6 %all-to-all-start.8 = ((bf16[32,7,1024]{2,1,0:T(8,128)(2,1)}), bf16[32,7,1024]{2,1,0:T(8,128)(2,1)S(1)}, u32[]{:S(2)}, u32[]{:S(2)}) async-start(bf16[32,7,1024]{2,1,0:T(8,128)(2,1)} %copy.161), calls=%async_computation.8 | async-start | bytes 1048576 | tf_op jit(solution)/shard_map/all_to_all | solution.py:118
  270.0 118.1 %reduce-scatter.2.cloned.1.call-start = ((), (), s32[]{:S(2)}) async-start(), calls=%async_computation.12 | async-start | bytes 2293760 | tf_op jit(solution)/shard_map/reduce_scatter | solution.py:249
  270.0 20.7 %collective-permute-start = (bf16[224,1024]{1,0:T(8,128)(2,1)S(1)}, bf16[224,1024]{1,0:T(8,128)(2,1)S(1)}, u32[]{:S(2)}, u32[]{:S(2)}) collective-permute-start(bf16[224,1024]{1,0:T(8,128)(2,1)S(1)} %copy-done), channel_id=1, source_target_pairs={{64,0},{65,1},{66,2},{67,3},{68,4},{69,5},{70,6},{71,7},{72,8},{73... | collective-permute-start | bytes 1376264 | tf_op jit(solution)/shard_map/ppermute | solution.py:219
  281.0 9.7 %copy-start.1 = (s32[2]{0:T(128)S(1)}, s32[2]{0:T(128)}, u32[]{:S(2)}) copy-start(s32[2]{0:T(128)} %constant.103.clone.1.info_ref) | copy-start | bytes 28
  314.3 13.5 %collective-permute-start.1 = (f32[8,224,1]{1,0,2:T(8,128)S(1)}, f32[8,224,1]{1,0,2:T(8,128)S(1)}, u32[]{:S(2)}, u32[]{:S(2)}) collective-permute-start(f32[8,224,1]{1,0,2:T(8,128)S(1)} %copy.162), channel_id=1, source_target_pairs={{0,64},{1,65},{2,66},{3,67},{4,68},{5,69},{6,70},{7,71},{8,72},{9,... | collective-permute-start | bytes 21512 | tf_op jit(solution)/shard_map/ppermute | solution.py:223
  315.9 13.2 %collective-permute-start.3 = (f32[8,224,1]{1,0,2:T(8,128)S(1)}, f32[8,224,1]{1,0,2:T(8,128)S(1)}, u32[]{:S(2)}, u32[]{:S(2)}) collective-permute-start(f32[8,224,1]{1,0,2:T(8,128)S(1)} %copy.167), channel_id=1, source_target_pairs={{0,64},{1,65},{2,66},{3,67},{4,68},{5,69},{6,70},{7,71},{8,72},{9,... | collective-permute-start | bytes 21512 | tf_op jit(solution)/shard_map/ppermute | solution.py:223
  317.2 23.2 %collective-permute-start.2 = (f32[224,1024]{1,0:T(8,128)}, f32[224,1024]{1,0:T(8,128)}, u32[]{:S(2)}, u32[]{:S(2)}) collective-permute-start(f32[224,1024]{1,0:T(8,128)} %get-tuple-element.14), channel_id=1, source_target_pairs={{0,64},{1,65},{2,66},{3,67},{4,68},{5,69},{6,70},{7,71},{8,72},{9,... | collective-permute-start | bytes 2752520 | tf_op jit(solution)/shard_map/ppermute | solution.py:223
  333.8 5.2 %copy-start.4 = (f32[224,8,1]{2,0,1:T(8,128)S(1)}, f32[224,8,1]{2,0,1:T(8,128)}, u32[]{:S(2)}) copy-start(f32[224,8,1]{2,0,1:T(8,128)} %get-tuple-element.24) | copy-start | bytes 21508
Sparse Core Ops, SparseCore 0:
  9.0 98.8 all-gather.2
  109.5 118.0 all-gather.4
  349.8 38.1 reduce-scatter.1

commit v5 on v4

--- a/solution.py
+++ b/solution.py
@@ -46,14 +46,12 @@
     share = chans // groups
     sub_rows = tok_rows // count_ctx
     period = 2 * count_ctx * tok_rows
-    got_source, got_filter = (
-        lax.all_to_all(
-            gated.reshape(1, tok_rows, chans), CTX, split_axis=1, concat_axis=0, tiled=True
-        ),
-        lax.all_to_all(
-            filters.reshape(1, tok_rows, groups), CTX, split_axis=1, concat_axis=0, tiled=True
-        ),
-    )
+    both = lax.all_to_all(
+        jnp.concatenate([gated, filters], axis=1).reshape(1, tok_rows, chans + groups),
+        CTX, split_axis=1, concat_axis=0, tiled=True,
+    )
+    got_source = both[:, :, :chans]
+    got_filter = both[:, :, chans:]
     coarse_idx = jnp.arange(count_ctx, dtype=jnp.int32)
     coarse_freq = jnp.arange(2 * count_ctx, dtype=jnp.int32)
     coarse_angle = angle_table(coarse_freq, coarse_idx, 2 * count_ctx)
@@ -67,20 +65,14 @@
     filter_re, filter_im = section_coarse(
         got_filter.astype(jnp.float32), cos_coarse, sin_coarse, twist_in
     )
-    source_re, source_im, filter_re, filter_im = (
-        lax.all_to_all(
-            source_re.astype(jnp.bfloat16), CTX, split_axis=0, concat_axis=1, tiled=True
-        ).astype(source_re.dtype),
-        lax.all_to_all(
-            source_im.astype(jnp.bfloat16), CTX, split_axis=0, concat_axis=1, tiled=True
-        ).astype(source_im.dtype),
-        lax.all_to_all(
-            filter_re.astype(jnp.bfloat16), CTX, split_axis=0, concat_axis=1, tiled=True
-        ).astype(filter_re.dtype),
-        lax.all_to_all(
-            filter_im.astype(jnp.bfloat16), CTX, split_axis=0, concat_axis=1, tiled=True
-        ).astype(filter_im.dtype),
-    )
+    packed = lax.all_to_all(
+        jnp.concatenate([source_re, source_im, filter_re, filter_im], axis=2).astype(jnp.bfloat16),
+        CTX, split_axis=0, concat_axis=1, tiled=True,
+    ).astype(jnp.float32)
+    source_re = packed[:, :, :chans]
+    source_im = packed[:, :, chans:2 * chans]
+    filter_re = packed[:, :, 2 * chans:2 * chans + groups]
+    filter_im = packed[:, :, 2 * chans + groups:]
     fine_idx = jnp.arange(tok_rows, dtype=jnp.int32)
     fine_angle = angle_table(fine_idx, fine_idx, tok_rows)
     cos_fine = jnp.cos(fine_angle)
@@ -104,14 +96,12 @@
     sin_out = jnp.sin(twist_out)[:, :, None]
     turned_re = back_re * cos_out - back_im * sin_out
     turned_im = back_re * sin_out + back_im * cos_out
-    turned_re, turned_im = (
-        lax.all_to_all(
-            turned_re.astype(jnp.bfloat16), CTX, split_axis=1, concat_axis=0, tiled=True
-        ).astype(turned_re.dtype),
-        lax.all_to_all(
-            turned_im.astype(jnp.bfloat16), CTX, split_axis=1, concat_axis=0, tiled=True
-        ).astype(turned_im.dtype),
-    )
+    turned = lax.all_to_all(
+        jnp.concatenate([turned_re, turned_im], axis=2).astype(jnp.bfloat16),
+        CTX, split_axis=1, concat_axis=0, tiled=True,
+    ).astype(jnp.float32)
+    turned_re = turned[:, :, :chans]
+    turned_im = turned[:, :, chans:]
     result = jnp.einsum("nk,ksc->nsc", cos_coarse.T, turned_re, precision=highest)
     result = result - jnp.einsum("nk,ksc->nsc", sin_coarse.T, turned_im, precision=highest)
     rounded = (result / period).astype(jnp.bfloat16)

time: 402 us -> 381 us (0.948); the launches traced: 395 us -> 379 us
  starting transfers between devices: 104 us -> 25.9 us
  blocking collectives: 0 us -> 61.3 us
    all_to_all x8 -> x2, starting transfers between devices: 92 us -> 15.8 us  [the longest x1 11.5 us: spectral_conv(): lax.all_to_all(jnp.concatenate([gated, filters], axis=1).reshape(1, tok_r...]
    all_to_all x0 -> x1, blocking collectives: none -> 61.3 us  [spectral_conv(): lax.all_to_all(jnp.concatenate([turned_re, turned_im], axis=2).astype(jnp...]
    all_to_all x8 -> x2, waiting for transfers between devices: 97.6 us -> 67.6 us  [the longest x1 49.5 us: spectral_conv(): lax.all_to_all(jnp.concatenate([source_re, source_im, filter_re, filter_i...]
    reduce_scatter x1, waiting for transfers between devices: 38.3 us -> 50 us  [local(): lax.psum_scatter((jnp.dot(mixed, w_conv_out, preferred_element_type=jnp.f...]
    ppermute x1, waiting for transfers between devices: 2.38 us -> 13.9 us  [attention(): visiting = lax.ppermute(q_attn, 'zh', [(1, 0)])]
    convert_element_type x6 -> x0, local copies, waits for them, and re-layouts: 6.97 us -> none  [the longest x1 1.9 us: spectral_conv(): turned_re.astype(jnp.bfloat16)]
    concatenate x0 -> x3, local copies, waits for them, and re-layouts: none -> 6.59 us  [the longest x2 4.7 us: spectral_conv(): jnp.concatenate([source_re, source_im, filter_re, filter_im], axis=2)]
    all_to_all x1, waiting for transfers between devices: 9.45 us -> 13.9 us  [spectral_conv(): lax.all_to_all(rounded, CTX, split_axis=0, concat_axis=1, tiled=True)]
  transfers between devices with their start and end apart: 16 -> 10, of which waited for: 11 -> 5; matrix products, arithmetic and copies ran while one was open for 21% -> 22% of each run, Pallas kernels for 2% -> 2%
where the time goes in v5:
time: 381 us; the launch traced here: 379 us
  waiting for transfers between devices  147 us (39%)
  blocking collectives  61.3 us (16%)
  matrix products  46.7 us (12%)
  local copies, waits for them, and re-layouts  43.4 us (11%)
  Pallas kernels  31.7 us (8%)
  starting transfers between devices  25.9 us (7%)
  between operations  13.8 us (4%)
  other arithmetic  9.12 us (2%)
    all_to_all x1, blocking collectives, spectral_conv(): lax.all_to_all(jnp.concatenate([turned_re, turned_im], axis=2).astype(jnp...  61.3 us
    reduce_scatter x1, waiting for transfers between devices, local(): lax.psum_scatter((jnp.dot(mixed, w_conv_out, preferred_element_type=jnp.f...  50 us
    all_to_all x1, waiting for transfers between devices, spectral_conv(): lax.all_to_all(jnp.concatenate([source_re, source_im, filter_re, filter_i...  49.5 us
    pallas_call x2, Pallas kernels, flash_partial(): pl.pallas_call(kernel, out_shape=(jax.ShapeDtypeStruct((tok_rows, width),...  31.7 us
    all_to_all x1, waiting for transfers between devices, spectral_conv(): lax.all_to_all(jnp.concatenate([gated, filters], axis=1).reshape(1, tok_r...  18.2 us
    all_to_all x1, waiting for transfers between devices, spectral_conv(): lax.all_to_all(rounded, CTX, split_axis=0, concat_axis=1, tiled=True)  13.9 us
    ppermute x1, waiting for transfers between devices, attention(): visiting = lax.ppermute(q_attn, 'zh', [(1, 0)])  13.9 us
    all_to_all x1, starting transfers between devices, spectral_conv(): lax.all_to_all(jnp.concatenate([gated, filters], axis=1).reshape(1, tok_r...  11.5 us
  transfers between devices with their start and end apart: 10, of which 5 were waited for; matrix products, arithmetic and copies ran while one was open for 22% of the time, Pallas kernels for 2%

profile of v5, /device:TPU:1, one launch (start us, length us, event | category | flops | bytes accessed | tf_op | source)
XLA Modules:
  0.0 378.6 jit_solution(3840902522210872350)
XLA Ops:
  11.6 3.9 %reduce.2 = bf16[224,1088]{1,0:T(8,128)(2,1)S(1)} reduce(bf16[224,1,1088]{2,1,0:T(2,128)(2,1)S(1)} %bitcast.135, bf16[]{:T(256)} %broadcast.195), dimensions={1}, to_apply=%bitcast.128.reduce_sub_computation | reduce | bytes 974850
  17.2 11.5 %all-to-all-start = ((bf16[32,2,3808]{2,1,0:T(2,128)(2,1)}), bf16[32,2,3808]{2,1,0:T(2,128)(2,1)S(1)}, u32[]{:S(2)}, u32[]{:S(2)}) async-start(bf16[32,2,3808]{2,1,0:T(2,128)(2,1)} %reshape.138), calls=%async_computation | async-start | bytes 983040 | tf_op jit(solution)/shard_map/all_to_all | solution.py:49
  28.8 18.2 %all-to-all-done = bf16[32,2,3808]{2,1,0:T(2,128)(2,1)S(1)} async-done(((bf16[32,2,3808]{2,1,0:T(2,128)(2,1)}), bf16[32,2,3808]{2,1,0:T(2,128)(2,1)S(1)}, u32[]{:S(2)}, u32[]{:S(2)}) %all-to-all-start) | async-done | bytes 487456 | tf_op jit(solution)/shard_map/all_to_all | solution.py:49
  48.0 2.9 bitcast_reduce_fusion
  53.3 2.7 subtract_convert_fusion.1
  60.8 4.3 %all-to-all-start.1 = ((bf16[64,7,2176]{2,1,0:T(8,128)(2,1)}), bf16[64,7,2176]{2,1,0:T(8,128)(2,1)S(1)}, u32[]{:S(2)}, u32[]{:S(2)}) async-start(bf16[64,7,2176]{2,1,0:T(8,128)(2,1)} %copy.97), calls=%async_computation.1 | async-start | bytes 4456448 | tf_op jit(solution)/shard_map/all_to_all | solution.py:68
  65.2 49.5 %all-to-all-done.1 = bf16[64,7,2176]{2,1,0:T(8,128)(2,1)S(1)} async-done(((bf16[64,7,2176]{2,1,0:T(8,128)(2,1)}), bf16[64,7,2176]{2,1,0:T(8,128)(2,1)S(1)}, u32[]{:S(2)}, u32[]{:S(2)}) %all-to-all-start.1) | async-done | bytes 1949728 | tf_op jit(solution)/shard_map/all_to_all | solution.py:68
  126.9 2.7 fusion.197
  137.9 2.7 fusion.40
  140.6 2.8 fusion.42
  143.4 2.7 convolution_add_fusion.1
  146.1 3.8 %fusion.11 = (bf16[2,224,1024]{2,1,0:T(8,128)(2,1)S(1)}, bf16[2,224,1024]{2,1,0:T(8,128)(2,1)S(1)}) fusion(f32[2,1024,224]{1,2,0:T(8,128)S(1)} %convolution_add_fusion.1, f32[2,224]{1,0:T(2,128)S(1)} %get-tuple-element.33, f32[2,224]{1,0:T(2,128)S(1)} %get-tuple-element.32, f32[2,1024,224]{1,2,0:T(8,128)S(1)} %fusion.42, ...), kind=kOutput, calls=%fused_computation.31 | convolution fusion | flops 1237705728 | bytes 7343616 | tf_op jit(solution)/shard_map/kn,anc->akc/dot_general | solution.py:39
  152.0 61.3 %all_to_all.57 = bf16[2,224,2048]{2,0,1:T(2,128)(2,1)S(1)} all-to-all(bf16[2,224,2048]{2,0,1:T(2,128)(2,1)S(1)} %copy.107), channel_id=1, replica_groups=mesh['zh'=2,'zl'=2,'yh'=2,'x'=4,'ch'=4] {'zh','zl','yh','x'}, dimensions={1} | all-to-all | bytes 3670016 | tf_op jit(solution)/shard_map/all_to_all | solution.py:99
  215.7 4.1 %all_to_all.51 = bf16[64,7,2048]{2,0,1:T(8,128)(2,1)S(1)} reshape(bf16[32,2,7,2048]{3,1,0,2:T(2,128)(2,1)} %copy.108) | data formatting | bytes 3670016 | tf_op jit(solution)/shard_map/all_to_all | solution.py:99
  222.2 3.9 %all-to-all-start.3 = ((bf16[32,7,1024]{2,1,0:T(8,128)(2,1)}), bf16[32,7,1024]{2,1,0:T(8,128)(2,1)S(1)}, u32[]{:S(2)}, u32[]{:S(2)}) async-start(bf16[32,7,1024]{2,1,0:T(8,128)(2,1)} %copy.109), calls=%async_computation.3 | async-start | bytes 1048576 | tf_op jit(solution)/shard_map/all_to_all | solution.py:108
  227.5 13.9 %all-to-all-done.3 = bf16[32,7,1024]{2,1,0:T(8,128)(2,1)S(1)} async-done(((bf16[32,7,1024]{2,1,0:T(8,128)(2,1)}), bf16[32,7,1024]{2,1,0:T(8,128)(2,1)S(1)}, u32[]{:S(2)}, u32[]{:S(2)}) %all-to-all-start.3) | async-done | bytes 458784 | tf_op jit(solution)/shard_map/all_to_all | solution.py:108
  241.6 7.4 %fusion.24 = f32[224,4096]{1,0:T(8,128)} fusion(bf16[1024,4096]{1,0:T(8,128)(2,1)} %param.16, f32[224,1024]{1,0:T(8,128)S(1)} %reshape.132, bf16[224,1024]{1,0:T(8,128)(2,1)S(1)} %copy-done.6), kind=kOutput, calls=%fused_computation.51 | convolution fusion | flops 1879736320 | bytes 13434880 | tf_op jit(solution)/shard_map/dot_general | solution.py:241
  248.9 13.9 %collective-permute-done.q_ref = bf16[224,1024]{1,0:T(8,128)(2,1)S(1)} collective-permute-done((bf16[224,1024]{1,0:T(8,128)(2,1)S(1)}, bf16[224,1024]{1,0:T(8,128)(2,1)S(1)}, u32[]{:S(2)}, u32[]{:S(2)}) %collective-permute-start) | collective-permute-done | bytes 458784 | tf_op jit(solution)/shard_map/ppermute | solution.py:209
  262.8 23.0 %shard_map.92 = (f32[224,1024]{1,0:T(8,128)}, f32[8,224,1]{2,1,0:T(8,128)S(1)}, f32[8,224,1]{2,1,0:T(8,128)S(1)}) custom-call(s32[2]{0:T(128)S(1)} %copy-done.1, bf16[224,1024]{1,0:T(8,128)(2,1)S(1)} %collective-permute-done.q_ref, bf16[3584,1024]{1,0:T(8,128)(2,1)} %all-gather.3.cloned.1.call-done.k_ref, bf16[3584,1024]{1,0:T(8,128)(2,1)} %all-gather.5.cloned.1.call-done.v_ref), custom_call_target="tpu_custom_call" | custom-call | flops 3288334336 | bytes 16056320 | tf_op jit(solution)/shard_map/pallas_call | solution.py:172
  291.4 8.6 %shard_map.91 = (f32[224,1024]{1,0:T(8,128)S(1)}, f32[8,224,1]{2,1,0:T(8,128)S(1)}, f32[8,224,1]{2,1,0:T(8,128)S(1)}) custom-call(s32[2]{0:T(128)S(1)} %pad_add_fusion.info_ref, bf16[224,1024]{1,0:T(8,128)(2,1)S(1)} %copy-done, bf16[3584,1024]{1,0:T(8,128)(2,1)} %all-gather.3.cloned.1.call-done.k_ref, bf16[3584,1024]{1,0:T(8,128)(2,1)} %all-gather.5.cloned.1.call-done.v_ref), custom_call_target="tpu_custom_call" | custom-call | flops 3288334336 | bytes 16056320 | tf_op jit(solution)/shard_map/pallas_call | solution.py:172
  302.6 3.4 fusion.31
  306.0 2.6 copy.118
  313.5 8.4 %fusion = bf16[224,4096]{1,0:T(8,128)(2,1)} fusion(f32[224,4096]{1,0:T(8,128)} %fusion.24, bf16[1024,4096]{1,0:T(8,128)(2,1)} %param.17, f32[28,8,8,128]{3,2,1,0:T(8,128)S(1)} %bitcast.138, f32[224,1024]{1,0:T(8,128)} %collective-permute-done.2, f32[28,8,8,128]{3,2,1,0:T(8,128)S(1)} %bitcast.137, f32[224,1024]{1,0:T(8,128)S(1)} %get-tuple-element.11, ...), kind=kOutput, calls=%fused_computation.1 | convolution fusion | flops 1882030080 | bytes 18481152 | tf_op jit(solution)/shard_map/dot_general | solution.py:242
  321.9 50.0 %reduce-scatter.2.cloned.1.call-done = bf16[56,4096]{1,0:T(8,128)(2,1)} async-done(((bf16[224,4096]{1,0:T(8,128)(2,1)}), bf16[56,4096]{1,0:T(8,128)(2,1)}) %reduce-scatter.2.cloned.1.call-update) | async-done | bytes 458768 | tf_op jit(solution)/shard_map/reduce_scatter | solution.py:239
  (82 shorter events, 56.7 us)
Async XLA Ops:
  6.5 256.3 %all-gather.3.cloned.1.call-start = ((), (), s32[]{:S(2)}) async-start(), calls=%async_computation.5 | async-start | bytes 7798784 | tf_op jit(solution)/shard_map/all_gather | solution.py:205
  7.3 255.6 %all-gather.5.cloned.1.call-start = ((), (), s32[]{:S(2)}) async-start(), calls=%async_computation.6 | async-start | bytes 7798784 | tf_op jit(solution)/shard_map/all_gather | solution.py:206
  17.2 29.9 %all-to-all-start = ((bf16[32,2,3808]{2,1,0:T(2,128)(2,1)}), bf16[32,2,3808]{2,1,0:T(2,128)(2,1)S(1)}, u32[]{:S(2)}, u32[]{:S(2)}) async-start(bf16[32,2,3808]{2,1,0:T(2,128)(2,1)} %reshape.138), calls=%async_computation | async-start | bytes 983040 | tf_op jit(solution)/shard_map/all_to_all | solution.py:49
  60.8 53.9 %all-to-all-start.1 = ((bf16[64,7,2176]{2,1,0:T(8,128)(2,1)}), bf16[64,7,2176]{2,1,0:T(8,128)(2,1)S(1)}, u32[]{:S(2)}, u32[]{:S(2)}) async-start(bf16[64,7,2176]{2,1,0:T(8,128)(2,1)} %copy.97), calls=%async_computation.1 | async-start | bytes 4456448 | tf_op jit(solution)/shard_map/all_to_all | solution.py:68
  116.2 1.3 copy-start.2
  133.3 2.0 copy-start.3
  133.4 2.0 copy-start.4
  220.4 5.7 %copy-start = (bf16[224,1024]{1,0:T(8,128)(2,1)S(1)}, bf16[224,1024]{1,0:T(8,128)(2,1)}, u32[]{:S(2)}) copy-start(bf16[224,1024]{1,0:T(8,128)(2,1)} %q_ref.1) | copy-start | bytes 1376260
  221.1 20.5 %copy-start.6 = (bf16[224,1024]{1,0:T(8,128)(2,1)S(1)}, bf16[224,1024]{1,0:T(8,128)(2,1)}, u32[]{:S(2)}) copy-start(bf16[224,1024]{1,0:T(8,128)(2,1)} %param.9) | copy-start | bytes 1376260
  222.2 19.3 %all-to-all-start.3 = ((bf16[32,7,1024]{2,1,0:T(8,128)(2,1)}), bf16[32,7,1024]{2,1,0:T(8,128)(2,1)S(1)}, u32[]{:S(2)}, u32[]{:S(2)}) async-start(bf16[32,7,1024]{2,1,0:T(8,128)(2,1)} %copy.109), calls=%async_computation.3 | async-start | bytes 1048576 | tf_op jit(solution)/shard_map/all_to_all | solution.py:108
  226.1 145.9 %reduce-scatter.2.cloned.1.call-start = ((), (), s32[]{:S(2)}) async-start(), calls=%async_computation.7 | async-start | bytes 2293760 | tf_op jit(solution)/shard_map/reduce_scatter | solution.py:239
  226.1 36.7 %collective-permute-start = (bf16[224,1024]{1,0:T(8,128)(2,1)S(1)}, bf16[224,1024]{1,0:T(8,128)(2,1)S(1)}, u32[]{:S(2)}, u32[]{:S(2)}) collective-permute-start(bf16[224,1024]{1,0:T(8,128)(2,1)S(1)} %copy-done), channel_id=1, source_target_pairs={{64,0},{65,1},{66,2},{67,3},{68,4},{69,5},{70,6},{71,7},{72,8},{73... | collective-permute-start | bytes 1376264 | tf_op jit(solution)/shard_map/ppermute | solution.py:209
  241.6 21.3 %copy-start.1 = (s32[2]{0:T(128)S(1)}, s32[2]{0:T(128)}, u32[]{:S(2)}) copy-start(s32[2]{0:T(128)} %constant.103.clone.1.info_ref) | copy-start | bytes 28
  286.2 13.8 %collective-permute-start.1 = (f32[8,224,1]{1,0,2:T(8,128)S(1)}, f32[8,224,1]{1,0,2:T(8,128)S(1)}, u32[]{:S(2)}, u32[]{:S(2)}) collective-permute-start(f32[8,224,1]{1,0,2:T(8,128)S(1)} %copy.110), channel_id=1, source_target_pairs={{0,64},{1,65},{2,66},{3,67},{4,68},{5,69},{6,70},{7,71},{8,72},{9,... | collective-permute-start | bytes 21512 | tf_op jit(solution)/shard_map/ppermute | solution.py:213
  287.8 13.5 %collective-permute-start.3 = (f32[8,224,1]{1,0,2:T(8,128)S(1)}, f32[8,224,1]{1,0,2:T(8,128)S(1)}, u32[]{:S(2)}, u32[]{:S(2)}) collective-permute-start(f32[8,224,1]{1,0,2:T(8,128)S(1)} %copy.115), channel_id=1, source_target_pairs={{0,64},{1,65},{2,66},{3,67},{4,68},{5,69},{6,70},{7,71},{8,72},{9,... | collective-permute-start | bytes 21512 | tf_op jit(solution)/shard_map/ppermute | solution.py:213
  289.1 23.5 %collective-permute-start.2 = (f32[224,1024]{1,0:T(8,128)}, f32[224,1024]{1,0:T(8,128)}, u32[]{:S(2)}, u32[]{:S(2)}) collective-permute-start(f32[224,1024]{1,0:T(8,128)} %get-tuple-element.14), channel_id=1, source_target_pairs={{0,64},{1,65},{2,66},{3,67},{4,68},{5,69},{6,70},{7,71},{8,72},{9,... | collective-permute-start | bytes 2752520 | tf_op jit(solution)/shard_map/ppermute | solution.py:213
  306.0 5.2 %copy-start.5 = (f32[224,8,1]{2,0,1:T(8,128)S(1)}, f32[224,8,1]{2,0,1:T(8,128)}, u32[]{:S(2)}) copy-start(f32[224,8,1]{2,0,1:T(8,128)} %get-tuple-element.28) | copy-start | bytes 21508
Sparse Core Ops, SparseCore 0:
  9.0 122.4 all-gather.2
  133.1 116.7 all-gather.4
  322.1 49.8 reduce-scatter.1

commit v6 on v5

--- a/solution.py
+++ b/solution.py
@@ -109,8 +109,8 @@
     return returned.reshape(tok_rows, chans)
 
 
-CTX = ("zh", "zl", "yh", "x")
-HALF = ("zl", "yh", "x")
+CTX = ("z", "yh", "x")
+HALF = ("yh", "x")
 
 
 def flash_kernel(info_ref, q_ref, k_ref, v_ref, acc_ref, m_ref, l_ref, *, heads, tok_rows, key_block, scale):
@@ -196,35 +196,45 @@
 def attention(q_attn, k_attn, v_attn, tok_rows):
     width = q_attn.shape[1]
     heads = width // HD
-    upper = lax.axis_index("zh")
+    quarters = lax.axis_size("z")
+    quarter = lax.axis_index("z")
     half_count = 1
     for name in HALF:
         half_count = half_count * lax.axis_size(name)
     my_index = lax.axis_index(CTX)
-    local_index = my_index - upper * half_count
-    key_half = lax.all_gather(k_attn, HALF, axis=0, tiled=True)
-    value_half = lax.all_gather(v_attn, HALF, axis=0, tiled=True)
-    half_rows = key_half.shape[0]
-    key_block = 896 if half_rows % 896 == 0 else tok_rows
-    visiting = lax.ppermute(q_attn, "zh", [(1, 0)])
-    cross = flash_partial(
-        visiting, key_half, value_half, jnp.int32(half_rows), jnp.int32(half_rows // key_block), key_block
-    )
-    cross_acc, cross_max, cross_total = lax.ppermute(cross, "zh", [(0, 1)])
+    local_index = my_index - quarter * half_count
+    key_part = lax.all_gather(k_attn, HALF, axis=0, tiled=True)
+    value_part = lax.all_gather(v_attn, HALF, axis=0, tiled=True)
+    part_rows = key_part.shape[0]
+    key_block = 896 if part_rows % 896 == 0 else tok_rows
+    states = []
+    for shift in range(1, quarters):
+        visiting = lax.ppermute(q_attn, "z", [(k, k - shift) for k in range(shift, quarters)])
+        cross = flash_partial(
+            visiting, key_part, value_part, jnp.int32(part_rows), jnp.int32(part_rows // key_block), key_block
+        )
+        stats = jnp.concatenate([cross[1].reshape(heads, tok_rows), cross[2].reshape(heads, tok_rows)])
+        back_acc, back_stats = lax.ppermute(
+            (cross[0], stats), "z", [(k - shift, k) for k in range(shift, quarters)]
+        )
+        back_max = jnp.where(quarter >= shift, back_stats[:heads], neg_large)
+        states.append((back_acc, back_max, back_stats[heads:]))
     needed = ((local_index + 1) * tok_rows + key_block - 1) // key_block
     own_acc, own_max, own_total = flash_partial(
-        q_attn, key_half, value_half, local_index * tok_rows, needed, key_block
-    )
-    cross_max = jnp.where(upper == 0, neg_large, cross_max)
-    top = jnp.maximum(own_max, cross_max)
-    own_scale = jnp.exp(own_max - top)
-    cross_scale = jnp.exp(cross_max - top)
-    totals = own_total * own_scale + cross_total * cross_scale
-    to_rows = lambda stat: stat.transpose(1, 0, 2)
-    merged = (
-        own_acc.reshape(tok_rows, heads, HD) * to_rows(own_scale)
-        + cross_acc.reshape(tok_rows, heads, HD) * to_rows(cross_scale)
-    ) / to_rows(totals)
+        q_attn, key_part, value_part, local_index * tok_rows, needed, key_block
+    )
+    states.append((own_acc, own_max.reshape(heads, tok_rows), own_total.reshape(heads, tok_rows)))
+    top = states[0][1]
+    for state in states[1:]:
+        top = jnp.maximum(top, state[1])
+    merged = None
+    totals = None
+    for acc, row_max, row_total in states:
+        scale = jnp.exp(row_max - top)
+        part = acc.reshape(tok_rows, heads, HD) * scale.T[:, :, None]
+        merged = part if merged is None else merged + part
+        totals = scale * row_total if totals is None else totals + scale * row_total
+    merged = merged / totals.T[:, :, None]
     return merged.reshape(tok_rows, width).astype(jnp.bfloat16)
 
 
@@ -250,7 +260,7 @@
 def solution(mesh):
     ctx_size, ch_size = mesh.devices.shape
     split_mesh = jax.sharding.Mesh(
-        mesh.devices.reshape(2, 2, 2, ctx_size // 8, ch_size), CTX + ("ch",)
+        mesh.devices.reshape(ctx_size // 8, 2, 4, ch_size), CTX + ("ch",)
     )
     tokens = P(CTX, "ch")
     return jax.shard_map(

time: 381 us -> 333 us (0.87)
  waiting for transfers between devices: 147 us -> 90.4 us
  blocking collectives: 61.3 us -> 38.7 us
  Pallas kernels: 31.7 us -> 47.2 us
  starting transfers between devices: 25.9 us -> 39.8 us
  local copies, waits for them, and re-layouts: 43.4 us -> 37.6 us
    all_to_all x1, blocking collectives: 61.3 us -> 38.7 us  [spectral_conv(): lax.all_to_all(jnp.concatenate([turned_re, turned_im], axis=2).astype(jnp...]
    reduce_scatter x1, waiting for transfers between devices: 50 us -> 27.8 us  [local(): lax.psum_scatter((jnp.dot(mixed, w_conv_out, preferred_element_type=jnp.f...]
    all_to_all x1, waiting for transfers between devices: 49.5 us -> 32.7 us  [spectral_conv(): lax.all_to_all(jnp.concatenate([source_re, source_im, filter_re, filter_i...]
    pallas_call x2 -> x4, Pallas kernels: 31.7 us -> 47.2 us  [flash_partial(): pl.pallas_call(kernel, out_shape=(jax.ShapeDtypeStruct((tok_rows, width),...]
    ppermute x4 -> x9, starting transfers between devices: 6.12 us -> 18.4 us  [the longest x6 14.1 us: attention(): lax.ppermute((cross[0], stats), 'z', [(k - shift, k) for k in range(shift...]
    ppermute x4 -> x9, waiting for transfers between devices: 13.9 us -> 4.95 us  [the longest x6 4.95 us: attention(): lax.ppermute((cross[0], stats), 'z', [(k - shift, k) for k in range(shift...]
    all_to_all x1, waiting for transfers between devices: 13.9 us -> 8.27 us  [spectral_conv(): lax.all_to_all(rounded, CTX, split_axis=0, concat_axis=1, tiled=True)]
    mul x4, local copies, waits for them, and re-layouts: 5.8 us -> 1.2 us  [attention(): part = acc.reshape(tok_rows, heads, HD) * scale.T[:, :, None]]
  transfers between devices with their start and end apart: 10 -> 15, of which waited for: 5 -> 5; matrix products, arithmetic and copies ran while one was open for 22% -> 24% of each run, Pallas kernels for 2% -> 14%
where the time goes in v6:
time: 333 us; the launch traced here: 327 us
  waiting for transfers between devices  90.4 us (27%)
  matrix products  49.6 us (15%)
  Pallas kernels  47.2 us (14%)
  starting transfers between devices  39.8 us (12%)
  blocking collectives  38.7 us (12%)
  local copies, waits for them, and re-layouts  37.6 us (11%)
  between operations  14.3 us (4%)
  other arithmetic  9.69 us (3%)
    pallas_call x4, Pallas kernels, flash_partial(): pl.pallas_call(kernel, out_shape=(jax.ShapeDtypeStruct((tok_rows, width),...  47.2 us
    all_to_all x1, blocking collectives, spectral_conv(): lax.all_to_all(jnp.concatenate([turned_re, turned_im], axis=2).astype(jnp...  38.7 us
    all_to_all x1, waiting for transfers between devices, spectral_conv(): lax.all_to_all(jnp.concatenate([source_re, source_im, filter_re, filter_i...  32.7 us
    reduce_scatter x1, waiting for transfers between devices, local(): lax.psum_scatter((jnp.dot(mixed, w_conv_out, preferred_element_type=jnp.f...  27.8 us
    all_to_all x1, waiting for transfers between devices, spectral_conv(): lax.all_to_all(jnp.concatenate([gated, filters], axis=1).reshape(1, tok_r...  15.6 us
    ppermute x6, starting transfers between devices, attention(): lax.ppermute((cross[0], stats), 'z', [(k - shift, k) for k in range(shift...  14.1 us
    all_to_all x1, starting transfers between devices, spectral_conv(): lax.all_to_all(jnp.concatenate([gated, filters], axis=1).reshape(1, tok_r...  11.5 us
    unnamed x30, local copies, waits for them, and re-layouts  8.92 us
  transfers between devices with their start and end apart: 15, of which 5 were waited for; matrix products, arithmetic and copies ran while one was open for 24% of the time, Pallas kernels for 14%

profile of v6, /device:TPU:1, one launch (start us, length us, event | category | flops | bytes accessed | tf_op | source)
XLA Modules:
  0.0 327.3 jit_solution(6533486322058129111)
XLA Ops:
  10.8 3.9 %reduce.10 = bf16[224,1088]{1,0:T(8,128)(2,1)S(1)} reduce(bf16[224,1,1088]{2,1,0:T(2,128)(2,1)S(1)} %bitcast.152, bf16[]{:T(256)} %broadcast.210), dimensions={1}, to_apply=%bitcast.145.reduce_sub_computation | reduce | bytes 974850
  16.4 11.5 %all-to-all-start = ((bf16[32,2,3808]{2,1,0:T(2,128)(2,1)}), bf16[32,2,3808]{2,1,0:T(2,128)(2,1)S(1)}, u32[]{:S(2)}, u32[]{:S(2)}) async-start(bf16[32,2,3808]{2,1,0:T(2,128)(2,1)} %reshape.187), calls=%async_computation | async-start | bytes 983040 | tf_op jit(solution)/shard_map/all_to_all | solution.py:49
  28.1 15.6 %all-to-all-done = bf16[32,2,3808]{2,1,0:T(2,128)(2,1)S(1)} async-done(((bf16[32,2,3808]{2,1,0:T(2,128)(2,1)}), bf16[32,2,3808]{2,1,0:T(2,128)(2,1)S(1)}, u32[]{:S(2)}, u32[]{:S(2)}) %all-to-all-start) | async-done | bytes 487456 | tf_op jit(solution)/shard_map/all_to_all | solution.py:49
  44.7 2.9 bitcast_reduce_fusion
  57.6 4.6 %all-to-all-start.1 = ((bf16[64,7,2176]{2,1,0:T(8,128)(2,1)}), bf16[64,7,2176]{2,1,0:T(8,128)(2,1)S(1)}, u32[]{:S(2)}, u32[]{:S(2)}) async-start(bf16[64,7,2176]{2,1,0:T(8,128)(2,1)} %copy.69), calls=%async_computation.1 | async-start | bytes 4456448 | tf_op jit(solution)/shard_map/all_to_all | solution.py:68
  63.1 32.7 %all-to-all-done.1 = bf16[64,7,2176]{2,1,0:T(8,128)(2,1)S(1)} async-done(((bf16[64,7,2176]{2,1,0:T(8,128)(2,1)}), bf16[64,7,2176]{2,1,0:T(8,128)(2,1)S(1)}, u32[]{:S(2)}, u32[]{:S(2)}) %all-to-all-start.1) | async-done | bytes 1949728 | tf_op jit(solution)/shard_map/all_to_all | solution.py:68
  99.9 3.1 fusion.22
  112.1 3.2 fusion.18
  125.4 2.9 convolution_add_fusion.1
  128.3 3.8 %fusion.9 = (bf16[2,224,1024]{2,1,0:T(8,128)(2,1)S(1)}, bf16[2,224,1024]{2,1,0:T(8,128)(2,1)S(1)}) fusion(f32[2,1024,224]{1,2,0:T(8,128)S(1)} %convolution_add_fusion.1, f32[2,224]{1,0:T(2,128)S(1)} %get-tuple-element.48, f32[2,224]{1,0:T(2,128)S(1)} %get-tuple-element.47, f32[2,1024,224]{1,2,0:T(8,128)S(1)} %fusion.40, ...), kind=kOutput, calls=%fused_computation.27 | convolution fusion | flops 1237705728 | bytes 7343616 | tf_op jit(solution)/shard_map/kn,anc->akc/dot_general | solution.py:39
  134.1 38.7 %all_to_all.57 = bf16[2,224,2048]{2,0,1:T(2,128)(2,1)S(1)} all-to-all(bf16[2,224,2048]{2,0,1:T(2,128)(2,1)S(1)} %copy.79), channel_id=1, replica_groups=mesh['z'=4,'yh'=2,'x'=4,'ch'=4] {'z','yh','x'}, dimensions={1} | all-to-all | bytes 3670016 | tf_op jit(solution)/shard_map/all_to_all | solution.py:99
  175.5 4.1 %all_to_all.51 = bf16[64,7,2048]{2,0,1:T(8,128)(2,1)S(1)} reshape(bf16[32,2,7,2048]{3,1,0,2:T(2,128)(2,1)} %copy.80) | data formatting | bytes 3670016 | tf_op jit(solution)/shard_map/all_to_all | solution.py:99
  181.9 4.7 %all-to-all-start.3 = ((bf16[32,7,1024]{2,1,0:T(8,128)(2,1)}), bf16[32,7,1024]{2,1,0:T(8,128)(2,1)S(1)}, u32[]{:S(2)}, u32[]{:S(2)}) async-start(bf16[32,7,1024]{2,1,0:T(8,128)(2,1)} %copy.81), calls=%async_computation.3 | async-start | bytes 1048576 | tf_op jit(solution)/shard_map/all_to_all | solution.py:108
  191.1 8.3 %all-to-all-done.3 = bf16[32,7,1024]{2,1,0:T(8,128)(2,1)S(1)} async-done(((bf16[32,7,1024]{2,1,0:T(8,128)(2,1)}), bf16[32,7,1024]{2,1,0:T(8,128)(2,1)S(1)}, u32[]{:S(2)}, u32[]{:S(2)}) %all-to-all-start.3) | async-done | bytes 458784 | tf_op jit(solution)/shard_map/all_to_all | solution.py:108
  199.5 7.4 %fusion.24 = f32[224,4096]{1,0:T(8,128)} fusion(bf16[1024,4096]{1,0:T(8,128)(2,1)} %param.16, f32[224,1024]{1,0:T(8,128)S(1)} %reshape.173, bf16[224,1024]{1,0:T(8,128)(2,1)S(1)} %copy-done.11), kind=kOutput, calls=%fused_computation.50 | convolution fusion | flops 1879736320 | bytes 13434880 | tf_op jit(solution)/shard_map/dot_general | solution.py:251
  206.9 12.3 %shard_map.91 = (f32[224,1024]{1,0:T(8,128)S(1)}, f32[8,224,1]{2,1,0:T(8,128)S(1)}, f32[8,224,1]{2,1,0:T(8,128)S(1)}) custom-call(s32[2]{0:T(128)S(1)} %copy-done.4, bf16[224,1024]{1,0:T(8,128)(2,1)S(1)} %collective-permute-done.q_ref, bf16[1792,1024]{1,0:T(8,128)(2,1)} %all-gather.3.cloned.1.call-done.k_ref, ...), custom_call_target="tpu_custom_call" | custom-call | flops 1644167168 | bytes 8716288 | tf_op jit(solution)/shard_map/pallas_call | solution.py:172
  220.8 3.3 %collective-permute-start.1 = (f32[224,1024]{1,0:T(8,128)}, f32[224,1024]{1,0:T(8,128)}, u32[]{:S(2)}, u32[]{:S(2)}) collective-permute-start(f32[224,1024]{1,0:T(8,128)} %copy-done.5), channel_id=1, source_target_pairs={{0,32},{32,64},{64,96},{1,33},{33,65},{65,97},{2,34},{34,66},{66,9... | collective-permute-start | bytes 2752520 | tf_op jit(solution)/shard_map/ppermute | solution.py:217
  226.0 13.3 %shard_map.92 = (f32[224,1024]{1,0:T(8,128)}, f32[8,224,1]{2,1,0:T(8,128)S(1)}, f32[8,224,1]{2,1,0:T(8,128)S(1)}) custom-call(s32[2]{0:T(128)S(1)} %copy-done.4, bf16[224,1024]{1,0:T(8,128)(2,1)S(1)} %copy-done.3, bf16[1792,1024]{1,0:T(8,128)(2,1)} %all-gather.3.cloned.1.call-done.k_ref, bf16[1792,1024]{1,0:T(8,128)(2,1)} %all-gather.5.cloned.1.call-done.v_ref), custom_call_target="tpu_custom_call" | custom-call | flops 1644167168 | bytes 8716288 | tf_op jit(solution)/shard_map/pallas_call | solution.py:172
  239.2 4.4 %collective-permute-start.7 = (f32[224,1024]{1,0:T(8,128)}, f32[224,1024]{1,0:T(8,128)}, u32[]{:S(2)}, u32[]{:S(2)}) collective-permute-start(f32[224,1024]{1,0:T(8,128)} %get-tuple-element.25), channel_id=1, source_target_pairs={{0,64},{32,96},{1,65},{33,97},{2,66},{34,98},{3,67},{35,99},{4,68}... | collective-permute-start | bytes 2752520 | tf_op jit(solution)/shard_map/ppermute | solution.py:217
  243.6 13.3 %shard_map.93 = (f32[224,1024]{1,0:T(8,128)}, f32[8,224,1]{2,1,0:T(8,128)S(1)}, f32[8,224,1]{2,1,0:T(8,128)S(1)}) custom-call(s32[2]{0:T(128)S(1)} %copy-done.4, bf16[224,1024]{1,0:T(8,128)(2,1)} %collective-permute-done.5.q_ref, bf16[1792,1024]{1,0:T(8,128)(2,1)} %all-gather.3.cloned.1.call-done.k_ref, bf16[1792,1024]{1,0:T(8,128)(2,1)} %all-gather.5.cloned.1.call-done.v_ref), custom_call_target="tpu_custom_call" | custom-call | flops 1644167168 | bytes 8716288 | tf_op jit(solution)/shard_map/pallas_call | solution.py:172
  266.9 8.3 %shard_map.94 = (f32[224,1024]{1,0:T(8,128)S(1)}, f32[8,224,1]{2,1,0:T(8,128)S(1)}, f32[8,224,1]{2,1,0:T(8,128)S(1)}) custom-call(s32[2]{0:T(128)S(1)} %pad_add_fusion.info_ref, bf16[224,1024]{1,0:T(8,128)(2,1)S(1)} %copy-done.1, bf16[1792,1024]{1,0:T(8,128)(2,1)} %all-gather.3.cloned.1.call-done.k_ref, bf16[1792,1024]{1,0:T(8,128)(2,1)} %all-gather.5.cloned.1.call-done.v_ref), custom_call_target="tpu_custom_call" | custom-call | flops 1644167168 | bytes 8716288 | tf_op jit(solution)/shard_map/pallas_call | solution.py:172
  275.9 4.9 %collective-permute-done.6 = f32[16,224]{1,0:T(8,128)S(1)} collective-permute-done((f32[16,224]{1,0:T(8,128)S(1)}, f32[16,224]{1,0:T(8,128)S(1)}, u32[]{:S(2)}, u32[]{:S(2)}) %collective-permute-start.6) | collective-permute-done | bytes 14368 | tf_op jit(solution)/shard_map/ppermute | solution.py:217
  283.8 8.6 %fusion = bf16[224,4096]{1,0:T(8,128)(2,1)} fusion(f32[224,4096]{1,0:T(8,128)S(1)} %copy-done.6, bf16[1024,4096]{1,0:T(8,128)(2,1)} %param.17, f32[28,8,8,128]{3,2,1,0:T(8,128)S(1)} %bitcast.156, f32[224,1024]{1,0:T(8,128)S(1)} %get-tuple-element.27, f32[28,8,8,128]{3,2,1,0:T(8,128)S(1)} %bitcast.155, f32[224,1024]{1,0:T(8,128)} %collective-permute-done.8, ...), kind=kOutput, calls=%fused_computation.1 | convolution fusion | flops 1882947584 | bytes 22151168 | tf_op jit(solution)/shard_map/dot_general | solution.py:252
  292.5 27.8 %reduce-scatter.2.cloned.1.call-done = bf16[56,4096]{1,0:T(8,128)(2,1)} async-done(((bf16[224,4096]{1,0:T(8,128)(2,1)}), bf16[56,4096]{1,0:T(8,128)(2,1)}) %reduce-scatter.2.cloned.1.call-update) | async-done | bytes 458768 | tf_op jit(solution)/shard_map/reduce_scatter | solution.py:249
  (115 shorter events, 69.2 us)
Async XLA Ops:
  6.5 200.4 %all-gather.3.cloned.1.call-start = ((), (), s32[]{:S(2)}) async-start(), calls=%async_computation.5 | async-start | bytes 4128768 | tf_op jit(solution)/shard_map/all_gather | solution.py:206
  16.4 27.3 %all-to-all-start = ((bf16[32,2,3808]{2,1,0:T(2,128)(2,1)}), bf16[32,2,3808]{2,1,0:T(2,128)(2,1)S(1)}, u32[]{:S(2)}, u32[]{:S(2)}) async-start(bf16[32,2,3808]{2,1,0:T(2,128)(2,1)} %reshape.187), calls=%async_computation | async-start | bytes 983040 | tf_op jit(solution)/shard_map/all_to_all | solution.py:49
  57.6 38.3 %all-to-all-start.1 = ((bf16[64,7,2176]{2,1,0:T(8,128)(2,1)}), bf16[64,7,2176]{2,1,0:T(8,128)(2,1)S(1)}, u32[]{:S(2)}, u32[]{:S(2)}) async-start(bf16[64,7,2176]{2,1,0:T(8,128)(2,1)} %copy.69), calls=%async_computation.1 | async-start | bytes 4456448 | tf_op jit(solution)/shard_map/all_to_all | solution.py:68
  62.2 144.7 %all-gather.5.cloned.1.call-start = ((), (), s32[]{:S(2)}) async-start(), calls=%async_computation.6 | async-start | bytes 4128768 | tf_op jit(solution)/shard_map/all_gather | solution.py:207
  112.1 3.2 copy-start.7
  112.1 3.2 copy-start.8
  115.3 2.0 copy-start.9
  115.3 2.2 copy-start.10
  180.2 6.5 %copy-start.1 = (bf16[224,1024]{1,0:T(8,128)(2,1)S(1)}, bf16[224,1024]{1,0:T(8,128)(2,1)}, u32[]{:S(2)}) copy-start(bf16[224,1024]{1,0:T(8,128)(2,1)} %q_ref.1) | copy-start | bytes 1376260
  180.8 18.7 %copy-start.11 = (bf16[224,1024]{1,0:T(8,128)(2,1)S(1)}, bf16[224,1024]{1,0:T(8,128)(2,1)}, u32[]{:S(2)}) copy-start(bf16[224,1024]{1,0:T(8,128)(2,1)} %param.9) | copy-start | bytes 1376260
  181.9 17.5 %all-to-all-start.3 = ((bf16[32,7,1024]{2,1,0:T(8,128)(2,1)}), bf16[32,7,1024]{2,1,0:T(8,128)(2,1)S(1)}, u32[]{:S(2)}, u32[]{:S(2)}) async-start(bf16[32,7,1024]{2,1,0:T(8,128)(2,1)} %copy.81), calls=%async_computation.3 | async-start | bytes 1048576 | tf_op jit(solution)/shard_map/all_to_all | solution.py:108
  186.6 133.7 %reduce-scatter.2.cloned.1.call-start = ((), (), s32[]{:S(2)}) async-start(), calls=%async_computation.7 | async-start | bytes 2293760 | tf_op jit(solution)/shard_map/reduce_scatter | solution.py:249
  186.7 20.2 %collective-permute-start = (bf16[224,1024]{1,0:T(8,128)(2,1)S(1)}, bf16[224,1024]{1,0:T(8,128)(2,1)S(1)}, u32[]{:S(2)}, u32[]{:S(2)}) collective-permute-start(bf16[224,1024]{1,0:T(8,128)(2,1)S(1)} %copy-done.1), channel_id=1, source_target_pairs={{32,0},{64,32},{96,64},{33,1},{65,33},{97,65},{34,2},{66,34},{98,6... | collective-permute-start | bytes 1376264 | tf_op jit(solution)/shard_map/ppermute | solution.py:212
  188.0 36.2 %collective-permute-start.3 = (bf16[224,1024]{1,0:T(8,128)(2,1)S(1)}, bf16[224,1024]{1,0:T(8,128)(2,1)S(1)}, u32[]{:S(2)}, u32[]{:S(2)}) collective-permute-start(bf16[224,1024]{1,0:T(8,128)(2,1)S(1)} %copy-done.1), channel_id=1, source_target_pairs={{64,0},{96,32},{65,1},{97,33},{66,2},{98,34},{67,3},{99,35},{68,4}... | collective-permute-start | bytes 1376264 | tf_op jit(solution)/shard_map/ppermute | solution.py:212
  189.3 54.4 %collective-permute-start.5 = (bf16[224,1024]{1,0:T(8,128)(2,1)S(1)}, bf16[224,1024]{1,0:T(8,128)(2,1)}, u32[]{:S(2)}, u32[]{:S(2)}) collective-permute-start(bf16[224,1024]{1,0:T(8,128)(2,1)S(1)} %copy-done.1), channel_id=1, source_target_pairs={{96,0},{97,1},{98,2},{99,3},{100,4},{101,5},{102,6},{103,7},{104,8... | collective-permute-start | bytes 1376264 | tf_op jit(solution)/shard_map/ppermute | solution.py:212
  199.5 7.4 %copy-start.4 = (s32[2]{0:T(128)S(1)}, s32[2]{0:T(128)}, u32[]{:S(2)}) copy-start(s32[2]{0:T(128)} %constant.92.clone.1.info_ref) | copy-start | bytes 28
  220.8 60.6 %collective-permute-start.1 = (f32[224,1024]{1,0:T(8,128)}, f32[224,1024]{1,0:T(8,128)}, u32[]{:S(2)}, u32[]{:S(2)}) collective-permute-start(f32[224,1024]{1,0:T(8,128)} %copy-done.5), channel_id=1, source_target_pairs={{0,32},{32,64},{64,96},{1,33},{33,65},{65,97},{2,34},{34,66},{66,9... | collective-permute-start | bytes 2752520 | tf_op jit(solution)/shard_map/ppermute | solution.py:217
  224.9 1.0 copy-start.3
  239.2 42.3 %collective-permute-start.7 = (f32[224,1024]{1,0:T(8,128)}, f32[224,1024]{1,0:T(8,128)}, u32[]{:S(2)}, u32[]{:S(2)}) collective-permute-start(f32[224,1024]{1,0:T(8,128)} %get-tuple-element.25), channel_id=1, source_target_pairs={{0,64},{32,96},{1,65},{33,97},{2,66},{34,98},{3,67},{35,99},{4,68}... | collective-permute-start | bytes 2752520 | tf_op jit(solution)/shard_map/ppermute | solution.py:217
  257.9 23.6 %collective-permute-start.8 = (f32[224,1024]{1,0:T(8,128)}, f32[224,1024]{1,0:T(8,128)}, u32[]{:S(2)}, u32[]{:S(2)}) collective-permute-start(f32[224,1024]{1,0:T(8,128)} %get-tuple-element.26), channel_id=1, source_target_pairs={{0,96},{1,97},{2,98},{3,99},{4,100},{5,101},{6,102},{7,103},{8,104... | collective-permute-start | bytes 2752520 | tf_op jit(solution)/shard_map/ppermute | solution.py:217
  260.2 5.2 %collective-permute-start.2 = (f32[16,224]{1,0:T(8,128)S(1)}, f32[16,224]{1,0:T(8,128)S(1)}, u32[]{:S(2)}, u32[]{:S(2)}) collective-permute-start(f32[16,224]{1,0:T(8,128)S(1)} %pad_maximum_fusion.1), channel_id=1, source_target_pairs={{0,32},{32,64},{64,96},{1,33},{33,65},{65,97},{2,34},{34,66},{66,9... | collective-permute-start | bytes 43016 | tf_op jit(solution)/shard_map/ppermute | solution.py:217
  262.2 13.7 %collective-permute-start.4 = (f32[16,224]{1,0:T(8,128)S(1)}, f32[16,224]{1,0:T(8,128)S(1)}, u32[]{:S(2)}, u32[]{:S(2)}) collective-permute-start(f32[16,224]{1,0:T(8,128)S(1)} %pad_maximum_fusion.2), channel_id=1, source_target_pairs={{0,64},{32,96},{1,65},{33,97},{2,66},{34,98},{3,67},{35,99},{4,68}... | collective-permute-start | bytes 43016 | tf_op jit(solution)/shard_map/ppermute | solution.py:217
  265.4 15.5 %collective-permute-start.6 = (f32[16,224]{1,0:T(8,128)S(1)}, f32[16,224]{1,0:T(8,128)S(1)}, u32[]{:S(2)}, u32[]{:S(2)}) collective-permute-start(f32[16,224]{1,0:T(8,128)S(1)} %pad_maximum_fusion.3), channel_id=1, source_target_pairs={{0,96},{1,97},{2,98},{3,99},{4,100},{5,101},{6,102},{7,103},{8,104... | collective-permute-start | bytes 43016 | tf_op jit(solution)/shard_map/ppermute | solution.py:217
  281.8 2.0 copy-start.6
  (3 other events, 2.6 us)
Sparse Core Ops, SparseCore 0:
  9.6 95.2 all-gather.2
  107.3 88.2 all-gather.4
  292.6 27.6 reduce-scatter.1

commit v7 on v6

--- a/solution.py
+++ b/solution.py
@@ -110,6 +110,7 @@
 
 
 CTX = ("z", "yh", "x")
+EXP2_SCALE = math.log2(math.e) * HD ** (-0.5)
 HALF = ("yh", "x")
 
 
@@ -135,15 +136,15 @@
             scores = lax.dot_general(
                 q_ref[:, cols], k_ref[:, cols], (((1,), (1,)), ((), ())),
                 preferred_element_type=jnp.float32,
-            ) * scale
+            )
             if masked:
                 scores = jnp.where(allowed, scores, neg_large)
             m_prev = m_ref[h]
             m_new = jnp.maximum(m_prev, jnp.max(scores, axis=1, keepdims=True))
-            weights = jnp.exp(scores - m_new)
+            weights = jnp.exp2((scores - m_new) * scale)
             if masked:
                 weights = jnp.where(allowed, weights, 0.0)
-            factor = jnp.exp(m_prev - m_new)
+            factor = jnp.exp2((m_prev - m_new) * scale)
             l_ref[h] = l_ref[h] * factor + jnp.sum(weights, axis=1, keepdims=True)
             acc_ref[:, cols] = acc_ref[:, cols] * factor + jnp.dot(
                 weights.astype(jnp.bfloat16), v_ref[:, cols], preferred_element_type=jnp.float32
@@ -166,7 +167,7 @@
     heads = width // HD
     total_rows = keys.shape[0]
     info = jnp.stack([q_first, needed]).astype(jnp.int32)
-    kernel = partial(flash_kernel, heads=heads, tok_rows=tok_rows, key_block=key_block, scale=HD ** (-0.5))
+    kernel = partial(flash_kernel, heads=heads, tok_rows=tok_rows, key_block=key_block, scale=EXP2_SCALE)
     kv_spec = pl.BlockSpec((key_block, width), lambda j, info: (jnp.minimum(j, info[1] - 1), 0))
     stat_spec = pl.BlockSpec((heads, tok_rows, 1), lambda j, info: (0, 0, 0))
     return pl.pallas_call(
@@ -230,7 +231,7 @@
     merged = None
     totals = None
     for acc, row_max, row_total in states:
-        scale = jnp.exp(row_max - top)
+        scale = jnp.exp2((row_max - top) * EXP2_SCALE)
         part = acc.reshape(tok_rows, heads, HD) * scale.T[:, :, None]
         merged = part if merged is None else merged + part
         totals = scale * row_total if totals is None else totals + scale * row_total
@@ -245,12 +246,10 @@
     gated = (k_conv.astype(jnp.float32) * v_conv.astype(jnp.float32)).astype(jnp.bfloat16)
     conv = spectral_conv(gated, conv_filter, my_index, tok_rows, count_ctx)
     mixed = (q_conv.astype(jnp.float32) * conv.astype(jnp.float32)).astype(jnp.bfloat16)
+    conv_part = jnp.dot(mixed, w_conv_out, preferred_element_type=jnp.float32)
     attended = attention(q_attn, k_attn, v_attn, tok_rows)
     return lax.psum_scatter(
-        (
-            jnp.dot(mixed, w_conv_out, preferred_element_type=jnp.float32)
-            + jnp.dot(attended, w_attn_out, preferred_element_type=jnp.float32)
-        ).astype(jnp.bfloat16),
+        (conv_part + jnp.dot(attended, w_attn_out, preferred_element_type=jnp.float32)).astype(jnp.bfloat16),
         "ch",
         scatter_dimension=0,
         tiled=True,

time: 333 us -> 333 us (level)
  no operation moved by 1% of the time
where the time goes in v7:
time: 333 us; the launch traced here: 327 us
  waiting for transfers between devices  90.6 us (27%)
  matrix products  49.6 us (15%)
  Pallas kernels  46.7 us (14%)
  starting transfers between devices  39.8 us (12%)
  blocking collectives  38.7 us (12%)
  local copies, waits for them, and re-layouts  37.6 us (11%)
  between operations  14.3 us (4%)
  other arithmetic  9.69 us (3%)
    pallas_call x4, Pallas kernels, flash_partial(): pl.pallas_call(kernel, out_shape=(jax.ShapeDtypeStruct((tok_rows, width),...  46.7 us
    all_to_all x1, blocking collectives, spectral_conv(): lax.all_to_all(jnp.concatenate([turned_re, turned_im], axis=2).astype(jnp...  38.7 us
    all_to_all x1, waiting for transfers between devices, spectral_conv(): lax.all_to_all(jnp.concatenate([source_re, source_im, filter_re, filter_i...  32.7 us
    reduce_scatter x1, waiting for transfers between devices, local(): lax.psum_scatter((conv_part + jnp.dot(attended, w_attn_out, preferred_ele...  27.7 us
    all_to_all x1, waiting for transfers between devices, spectral_conv(): lax.all_to_all(jnp.concatenate([gated, filters], axis=1).reshape(1, tok_r...  15.6 us
    ppermute x6, starting transfers between devices, attention(): lax.ppermute((cross[0], stats), 'z', [(k - shift, k) for k in range(shift...  14.1 us
    all_to_all x1, starting transfers between devices, spectral_conv(): lax.all_to_all(jnp.concatenate([gated, filters], axis=1).reshape(1, tok_r...  11.5 us
    unnamed x30, local copies, waits for them, and re-layouts  8.92 us
  transfers between devices with their start and end apart: 15, of which 5 were waited for; matrix products, arithmetic and copies ran while one was open for 24% of the time, Pallas kernels for 14%

profile of v7, /device:TPU:1, one launch (start us, length us, event | category | flops | bytes accessed | tf_op | source)
XLA Modules:
  0.0 327.1 jit_solution(6118917674054887275)
XLA Ops:
  10.8 3.9 %reduce.10 = bf16[224,1088]{1,0:T(8,128)(2,1)S(1)} reduce(bf16[224,1,1088]{2,1,0:T(2,128)(2,1)S(1)} %bitcast.152, bf16[]{:T(256)} %broadcast.216), dimensions={1}, to_apply=%bitcast.145.reduce_sub_computation | reduce | bytes 974850
  16.4 11.5 %all-to-all-start = ((bf16[32,2,3808]{2,1,0:T(2,128)(2,1)}), bf16[32,2,3808]{2,1,0:T(2,128)(2,1)S(1)}, u32[]{:S(2)}, u32[]{:S(2)}) async-start(bf16[32,2,3808]{2,1,0:T(2,128)(2,1)} %reshape.187), calls=%async_computation | async-start | bytes 983040 | tf_op jit(solution)/shard_map/all_to_all | solution.py:49
  28.1 15.6 %all-to-all-done = bf16[32,2,3808]{2,1,0:T(2,128)(2,1)S(1)} async-done(((bf16[32,2,3808]{2,1,0:T(2,128)(2,1)}), bf16[32,2,3808]{2,1,0:T(2,128)(2,1)S(1)}, u32[]{:S(2)}, u32[]{:S(2)}) %all-to-all-start) | async-done | bytes 487456 | tf_op jit(solution)/shard_map/all_to_all | solution.py:49
  44.7 2.9 bitcast_reduce_fusion
  57.6 4.6 %all-to-all-start.1 = ((bf16[64,7,2176]{2,1,0:T(8,128)(2,1)}), bf16[64,7,2176]{2,1,0:T(8,128)(2,1)S(1)}, u32[]{:S(2)}, u32[]{:S(2)}) async-start(bf16[64,7,2176]{2,1,0:T(8,128)(2,1)} %copy.69), calls=%async_computation.1 | async-start | bytes 4456448 | tf_op jit(solution)/shard_map/all_to_all | solution.py:68
  63.1 32.7 %all-to-all-done.1 = bf16[64,7,2176]{2,1,0:T(8,128)(2,1)S(1)} async-done(((bf16[64,7,2176]{2,1,0:T(8,128)(2,1)}), bf16[64,7,2176]{2,1,0:T(8,128)(2,1)S(1)}, u32[]{:S(2)}, u32[]{:S(2)}) %all-to-all-start.1) | async-done | bytes 1949728 | tf_op jit(solution)/shard_map/all_to_all | solution.py:68
  99.9 3.1 fusion.22
  112.1 3.2 fusion.18
  125.4 2.9 convolution_add_fusion.1
  128.3 3.8 %fusion.9 = (bf16[2,224,1024]{2,1,0:T(8,128)(2,1)S(1)}, bf16[2,224,1024]{2,1,0:T(8,128)(2,1)S(1)}) fusion(f32[2,1024,224]{1,2,0:T(8,128)S(1)} %convolution_add_fusion.1, f32[2,224]{1,0:T(2,128)S(1)} %get-tuple-element.48, f32[2,224]{1,0:T(2,128)S(1)} %get-tuple-element.47, f32[2,1024,224]{1,2,0:T(8,128)S(1)} %fusion.40, ...), kind=kOutput, calls=%fused_computation.27 | convolution fusion | flops 1237705728 | bytes 7343616 | tf_op jit(solution)/shard_map/kn,anc->akc/dot_general | solution.py:39
  134.1 38.7 %all_to_all.57 = bf16[2,224,2048]{2,0,1:T(2,128)(2,1)S(1)} all-to-all(bf16[2,224,2048]{2,0,1:T(2,128)(2,1)S(1)} %copy.79), channel_id=1, replica_groups=mesh['z'=4,'yh'=2,'x'=4,'ch'=4] {'z','yh','x'}, dimensions={1} | all-to-all | bytes 3670016 | tf_op jit(solution)/shard_map/all_to_all | solution.py:99
  175.5 4.1 %all_to_all.51 = bf16[64,7,2048]{2,0,1:T(8,128)(2,1)S(1)} reshape(bf16[32,2,7,2048]{3,1,0,2:T(2,128)(2,1)} %copy.80) | data formatting | bytes 3670016 | tf_op jit(solution)/shard_map/all_to_all | solution.py:99
  181.9 4.7 %all-to-all-start.3 = ((bf16[32,7,1024]{2,1,0:T(8,128)(2,1)}), bf16[32,7,1024]{2,1,0:T(8,128)(2,1)S(1)}, u32[]{:S(2)}, u32[]{:S(2)}) async-start(bf16[32,7,1024]{2,1,0:T(8,128)(2,1)} %copy.81), calls=%async_computation.3 | async-start | bytes 1048576 | tf_op jit(solution)/shard_map/all_to_all | solution.py:108
  191.1 8.3 %all-to-all-done.3 = bf16[32,7,1024]{2,1,0:T(8,128)(2,1)S(1)} async-done(((bf16[32,7,1024]{2,1,0:T(8,128)(2,1)}), bf16[32,7,1024]{2,1,0:T(8,128)(2,1)S(1)}, u32[]{:S(2)}, u32[]{:S(2)}) %all-to-all-start.3) | async-done | bytes 458784 | tf_op jit(solution)/shard_map/all_to_all | solution.py:108
  199.5 7.4 %fusion.24 = f32[224,4096]{1,0:T(8,128)} fusion(bf16[1024,4096]{1,0:T(8,128)(2,1)} %param.16, f32[224,1024]{1,0:T(8,128)S(1)} %reshape.173, bf16[224,1024]{1,0:T(8,128)(2,1)S(1)} %copy-done.11), kind=kOutput, calls=%fused_computation.50 | convolution fusion | flops 1879736320 | bytes 13434880 | tf_op jit(solution)/shard_map/dot_general | solution.py:249
  206.9 12.2 %shard_map.91 = (f32[224,1024]{1,0:T(8,128)S(1)}, f32[8,224,1]{2,1,0:T(8,128)S(1)}, f32[8,224,1]{2,1,0:T(8,128)S(1)}) custom-call(s32[2]{0:T(128)S(1)} %copy-done.4, bf16[224,1024]{1,0:T(8,128)(2,1)S(1)} %collective-permute-done.q_ref, bf16[1792,1024]{1,0:T(8,128)(2,1)} %all-gather.3.cloned.1.call-done.k_ref, ...), custom_call_target="tpu_custom_call" | custom-call | flops 1644167168 | bytes 8716288 | tf_op jit(solution)/shard_map/pallas_call | solution.py:173
  220.7 3.3 %collective-permute-start.1 = (f32[224,1024]{1,0:T(8,128)}, f32[224,1024]{1,0:T(8,128)}, u32[]{:S(2)}, u32[]{:S(2)}) collective-permute-start(f32[224,1024]{1,0:T(8,128)} %copy-done.5), channel_id=1, source_target_pairs={{0,32},{32,64},{64,96},{1,33},{33,65},{65,97},{2,34},{34,66},{66,9... | collective-permute-start | bytes 2752520 | tf_op jit(solution)/shard_map/ppermute | solution.py:218
  225.8 13.1 %shard_map.92 = (f32[224,1024]{1,0:T(8,128)}, f32[8,224,1]{2,1,0:T(8,128)S(1)}, f32[8,224,1]{2,1,0:T(8,128)S(1)}) custom-call(s32[2]{0:T(128)S(1)} %copy-done.4, bf16[224,1024]{1,0:T(8,128)(2,1)S(1)} %copy-done.3, bf16[1792,1024]{1,0:T(8,128)(2,1)} %all-gather.3.cloned.1.call-done.k_ref, bf16[1792,1024]{1,0:T(8,128)(2,1)} %all-gather.5.cloned.1.call-done.v_ref), custom_call_target="tpu_custom_call" | custom-call | flops 1644167168 | bytes 8716288 | tf_op jit(solution)/shard_map/pallas_call | solution.py:173
  238.9 4.4 %collective-permute-start.7 = (f32[224,1024]{1,0:T(8,128)}, f32[224,1024]{1,0:T(8,128)}, u32[]{:S(2)}, u32[]{:S(2)}) collective-permute-start(f32[224,1024]{1,0:T(8,128)} %get-tuple-element.25), channel_id=1, source_target_pairs={{0,64},{32,96},{1,65},{33,97},{2,66},{34,98},{3,67},{35,99},{4,68}... | collective-permute-start | bytes 2752520 | tf_op jit(solution)/shard_map/ppermute | solution.py:218
  243.3 13.2 %shard_map.93 = (f32[224,1024]{1,0:T(8,128)}, f32[8,224,1]{2,1,0:T(8,128)S(1)}, f32[8,224,1]{2,1,0:T(8,128)S(1)}) custom-call(s32[2]{0:T(128)S(1)} %copy-done.4, bf16[224,1024]{1,0:T(8,128)(2,1)} %collective-permute-done.5.q_ref, bf16[1792,1024]{1,0:T(8,128)(2,1)} %all-gather.3.cloned.1.call-done.k_ref, bf16[1792,1024]{1,0:T(8,128)(2,1)} %all-gather.5.cloned.1.call-done.v_ref), custom_call_target="tpu_custom_call" | custom-call | flops 1644167168 | bytes 8716288 | tf_op jit(solution)/shard_map/pallas_call | solution.py:173
  266.5 8.2 %shard_map.94 = (f32[224,1024]{1,0:T(8,128)S(1)}, f32[8,224,1]{2,1,0:T(8,128)S(1)}, f32[8,224,1]{2,1,0:T(8,128)S(1)}) custom-call(s32[2]{0:T(128)S(1)} %pad_add_fusion.info_ref, bf16[224,1024]{1,0:T(8,128)(2,1)S(1)} %copy-done.1, bf16[1792,1024]{1,0:T(8,128)(2,1)} %all-gather.3.cloned.1.call-done.k_ref, bf16[1792,1024]{1,0:T(8,128)(2,1)} %all-gather.5.cloned.1.call-done.v_ref), custom_call_target="tpu_custom_call" | custom-call | flops 1644167168 | bytes 8716288 | tf_op jit(solution)/shard_map/pallas_call | solution.py:173
  275.4 5.3 %collective-permute-done.6 = f32[16,224]{1,0:T(8,128)S(1)} collective-permute-done((f32[16,224]{1,0:T(8,128)S(1)}, f32[16,224]{1,0:T(8,128)S(1)}, u32[]{:S(2)}, u32[]{:S(2)}) %collective-permute-start.6) | collective-permute-done | bytes 14368 | tf_op jit(solution)/shard_map/ppermute | solution.py:218
  283.7 8.6 %fusion = bf16[224,4096]{1,0:T(8,128)(2,1)} fusion(f32[224,4096]{1,0:T(8,128)S(1)} %copy-done.6, bf16[1024,4096]{1,0:T(8,128)(2,1)} %param.17, f32[28,8,8,128]{3,2,1,0:T(8,128)S(1)} %bitcast.156, f32[224,1024]{1,0:T(8,128)S(1)} %get-tuple-element.27, f32[28,8,8,128]{3,2,1,0:T(8,128)S(1)} %bitcast.155, f32[224,1024]{1,0:T(8,128)} %collective-permute-done.8, ...), kind=kOutput, calls=%fused_computation.1 | convolution fusion | flops 1882947584 | bytes 22151168 | tf_op jit(solution)/shard_map/dot_general | solution.py:252
  292.4 27.7 %reduce-scatter.2.cloned.1.call-done = bf16[56,4096]{1,0:T(8,128)(2,1)} async-done(((bf16[224,4096]{1,0:T(8,128)(2,1)}), bf16[56,4096]{1,0:T(8,128)(2,1)}) %reduce-scatter.2.cloned.1.call-update) | async-done | bytes 458768 | tf_op jit(solution)/shard_map/reduce_scatter | solution.py:251
  (115 shorter events, 69.2 us)
Async XLA Ops:
  6.5 200.4 %all-gather.3.cloned.1.call-start = ((), (), s32[]{:S(2)}) async-start(), calls=%async_computation.5 | async-start | bytes 4128768 | tf_op jit(solution)/shard_map/all_gather | solution.py:207
  16.4 27.3 %all-to-all-start = ((bf16[32,2,3808]{2,1,0:T(2,128)(2,1)}), bf16[32,2,3808]{2,1,0:T(2,128)(2,1)S(1)}, u32[]{:S(2)}, u32[]{:S(2)}) async-start(bf16[32,2,3808]{2,1,0:T(2,128)(2,1)} %reshape.187), calls=%async_computation | async-start | bytes 983040 | tf_op jit(solution)/shard_map/all_to_all | solution.py:49
  57.6 38.3 %all-to-all-start.1 = ((bf16[64,7,2176]{2,1,0:T(8,128)(2,1)}), bf16[64,7,2176]{2,1,0:T(8,128)(2,1)S(1)}, u32[]{:S(2)}, u32[]{:S(2)}) async-start(bf16[64,7,2176]{2,1,0:T(8,128)(2,1)} %copy.69), calls=%async_computation.1 | async-start | bytes 4456448 | tf_op jit(solution)/shard_map/all_to_all | solution.py:68
  62.2 144.7 %all-gather.5.cloned.1.call-start = ((), (), s32[]{:S(2)}) async-start(), calls=%async_computation.6 | async-start | bytes 4128768 | tf_op jit(solution)/shard_map/all_gather | solution.py:208
  112.1 3.2 copy-start.7
  112.1 3.2 copy-start.8
  115.3 2.0 copy-start.9
  115.3 2.2 copy-start.10
  180.2 6.5 %copy-start.1 = (bf16[224,1024]{1,0:T(8,128)(2,1)S(1)}, bf16[224,1024]{1,0:T(8,128)(2,1)}, u32[]{:S(2)}) copy-start(bf16[224,1024]{1,0:T(8,128)(2,1)} %q_ref.1) | copy-start | bytes 1376260
  180.8 18.7 %copy-start.11 = (bf16[224,1024]{1,0:T(8,128)(2,1)S(1)}, bf16[224,1024]{1,0:T(8,128)(2,1)}, u32[]{:S(2)}) copy-start(bf16[224,1024]{1,0:T(8,128)(2,1)} %param.9) | copy-start | bytes 1376260
  181.9 17.5 %all-to-all-start.3 = ((bf16[32,7,1024]{2,1,0:T(8,128)(2,1)}), bf16[32,7,1024]{2,1,0:T(8,128)(2,1)S(1)}, u32[]{:S(2)}, u32[]{:S(2)}) async-start(bf16[32,7,1024]{2,1,0:T(8,128)(2,1)} %copy.81), calls=%async_computation.3 | async-start | bytes 1048576 | tf_op jit(solution)/shard_map/all_to_all | solution.py:108
  186.6 133.4 %reduce-scatter.2.cloned.1.call-start = ((), (), s32[]{:S(2)}) async-start(), calls=%async_computation.7 | async-start | bytes 2293760 | tf_op jit(solution)/shard_map/reduce_scatter | solution.py:251
  186.7 20.2 %collective-permute-start = (bf16[224,1024]{1,0:T(8,128)(2,1)S(1)}, bf16[224,1024]{1,0:T(8,128)(2,1)S(1)}, u32[]{:S(2)}, u32[]{:S(2)}) collective-permute-start(bf16[224,1024]{1,0:T(8,128)(2,1)S(1)} %copy-done.1), channel_id=1, source_target_pairs={{32,0},{64,32},{96,64},{33,1},{65,33},{97,65},{34,2},{66,34},{98,6... | collective-permute-start | bytes 1376264 | tf_op jit(solution)/shard_map/ppermute | solution.py:213
  188.0 36.1 %collective-permute-start.3 = (bf16[224,1024]{1,0:T(8,128)(2,1)S(1)}, bf16[224,1024]{1,0:T(8,128)(2,1)S(1)}, u32[]{:S(2)}, u32[]{:S(2)}) collective-permute-start(bf16[224,1024]{1,0:T(8,128)(2,1)S(1)} %copy-done.1), channel_id=1, source_target_pairs={{64,0},{96,32},{65,1},{97,33},{66,2},{98,34},{67,3},{99,35},{68,4}... | collective-permute-start | bytes 1376264 | tf_op jit(solution)/shard_map/ppermute | solution.py:213
  189.3 54.1 %collective-permute-start.5 = (bf16[224,1024]{1,0:T(8,128)(2,1)S(1)}, bf16[224,1024]{1,0:T(8,128)(2,1)}, u32[]{:S(2)}, u32[]{:S(2)}) collective-permute-start(bf16[224,1024]{1,0:T(8,128)(2,1)S(1)} %copy-done.1), channel_id=1, source_target_pairs={{96,0},{97,1},{98,2},{99,3},{100,4},{101,5},{102,6},{103,7},{104,8... | collective-permute-start | bytes 1376264 | tf_op jit(solution)/shard_map/ppermute | solution.py:213
  199.5 7.4 %copy-start.4 = (s32[2]{0:T(128)S(1)}, s32[2]{0:T(128)}, u32[]{:S(2)}) copy-start(s32[2]{0:T(128)} %constant.98.clone.1.info_ref) | copy-start | bytes 28
  220.7 60.6 %collective-permute-start.1 = (f32[224,1024]{1,0:T(8,128)}, f32[224,1024]{1,0:T(8,128)}, u32[]{:S(2)}, u32[]{:S(2)}) collective-permute-start(f32[224,1024]{1,0:T(8,128)} %copy-done.5), channel_id=1, source_target_pairs={{0,32},{32,64},{64,96},{1,33},{33,65},{65,97},{2,34},{34,66},{66,9... | collective-permute-start | bytes 2752520 | tf_op jit(solution)/shard_map/ppermute | solution.py:218
  224.8 1.0 copy-start.3
  238.9 42.4 %collective-permute-start.7 = (f32[224,1024]{1,0:T(8,128)}, f32[224,1024]{1,0:T(8,128)}, u32[]{:S(2)}, u32[]{:S(2)}) collective-permute-start(f32[224,1024]{1,0:T(8,128)} %get-tuple-element.25), channel_id=1, source_target_pairs={{0,64},{32,96},{1,65},{33,97},{2,66},{34,98},{3,67},{35,99},{4,68}... | collective-permute-start | bytes 2752520 | tf_op jit(solution)/shard_map/ppermute | solution.py:218
  257.5 23.9 %collective-permute-start.8 = (f32[224,1024]{1,0:T(8,128)}, f32[224,1024]{1,0:T(8,128)}, u32[]{:S(2)}, u32[]{:S(2)}) collective-permute-start(f32[224,1024]{1,0:T(8,128)} %get-tuple-element.26), channel_id=1, source_target_pairs={{0,96},{1,97},{2,98},{3,99},{4,100},{5,101},{6,102},{7,103},{8,104... | collective-permute-start | bytes 2752520 | tf_op jit(solution)/shard_map/ppermute | solution.py:218
  259.7 5.2 %collective-permute-start.2 = (f32[16,224]{1,0:T(8,128)S(1)}, f32[16,224]{1,0:T(8,128)S(1)}, u32[]{:S(2)}, u32[]{:S(2)}) collective-permute-start(f32[16,224]{1,0:T(8,128)S(1)} %pad_maximum_fusion.1), channel_id=1, source_target_pairs={{0,32},{32,64},{64,96},{1,33},{33,65},{65,97},{2,34},{34,66},{66,9... | collective-permute-start | bytes 43016 | tf_op jit(solution)/shard_map/ppermute | solution.py:218
  261.7 13.6 %collective-permute-start.4 = (f32[16,224]{1,0:T(8,128)S(1)}, f32[16,224]{1,0:T(8,128)S(1)}, u32[]{:S(2)}, u32[]{:S(2)}) collective-permute-start(f32[16,224]{1,0:T(8,128)S(1)} %pad_maximum_fusion.2), channel_id=1, source_target_pairs={{0,64},{32,96},{1,65},{33,97},{2,66},{34,98},{3,67},{35,99},{4,68}... | collective-permute-start | bytes 43016 | tf_op jit(solution)/shard_map/ppermute | solution.py:218
  264.9 15.8 %collective-permute-start.6 = (f32[16,224]{1,0:T(8,128)S(1)}, f32[16,224]{1,0:T(8,128)S(1)}, u32[]{:S(2)}, u32[]{:S(2)}) collective-permute-start(f32[16,224]{1,0:T(8,128)S(1)} %pad_maximum_fusion.3), channel_id=1, source_target_pairs={{0,96},{1,97},{2,98},{3,99},{4,100},{5,101},{6,102},{7,103},{8,104... | collective-permute-start | bytes 43016 | tf_op jit(solution)/shard_map/ppermute | solution.py:218
  281.7 2.0 copy-start.6
  (3 other events, 2.6 us)
Sparse Core Ops, SparseCore 0:
  9.6 95.2 all-gather.2
  107.3 88.2 all-gather.4
  292.5 27.5 reduce-scatter.1

commit v8 on v7

--- a/solution.py
+++ b/solution.py
@@ -215,11 +215,12 @@
             visiting, key_part, value_part, jnp.int32(part_rows), jnp.int32(part_rows // key_block), key_block
         )
         stats = jnp.concatenate([cross[1].reshape(heads, tok_rows), cross[2].reshape(heads, tok_rows)])
-        back_acc, back_stats = lax.ppermute(
-            (cross[0], stats), "z", [(k - shift, k) for k in range(shift, quarters)]
+        back = lax.ppermute(
+            jnp.concatenate([cross[0], stats.T], axis=1), "z", [(k - shift, k) for k in range(shift, quarters)]
         )
+        back_stats = back[:, width:].T
         back_max = jnp.where(quarter >= shift, back_stats[:heads], neg_large)
-        states.append((back_acc, back_max, back_stats[heads:]))
+        states.append((back[:, :width], back_max, back_stats[heads:]))
     needed = ((local_index + 1) * tok_rows + key_block - 1) // key_block
     own_acc, own_max, own_total = flash_partial(
         q_attn, key_part, value_part, local_index * tok_rows, needed, key_block

time: 333 us -> 333 us (level)
  blocking collectives: 38.7 us -> 0 us
  waiting for transfers between devices: 90.6 us -> 122 us
  local copies, waits for them, and re-layouts: 37.6 us -> 45.6 us
    all_to_all x1 -> x0, blocking collectives: 38.7 us -> none  [spectral_conv(): lax.all_to_all(jnp.concatenate([turned_re, turned_im], axis=2).astype(jnp...]
    all_to_all x0 -> x1, waiting for transfers between devices: none -> 29.3 us  [spectral_conv(): lax.all_to_all(jnp.concatenate([turned_re, turned_im], axis=2).astype(jnp...]
    all_to_all x0 -> x1, starting transfers between devices: none -> 7.89 us  [spectral_conv(): lax.all_to_all(jnp.concatenate([turned_re, turned_im], axis=2).astype(jnp...]
    ppermute x6 -> x3, starting transfers between devices: 14.1 us -> 8.58 us  [attention(): lax.ppermute(jnp.concatenate([cross[0], stats.T], axis=1), 'z', [(k - shi...]
    unnamed x30 -> x26, local copies, waits for them, and re-layouts: 8.92 us -> 8.3 us
  transfers between devices with their start and end apart: 15 -> 13, of which waited for: 5 -> 6; matrix products, arithmetic and copies ran while one was open for 24% -> 26% of each run, Pallas kernels for 14% -> 14%
where the time goes in v8:
time: 333 us; the launch traced here: 327 us
  waiting for transfers between devices  122 us (37%)
  matrix products  46.9 us (14%)
  Pallas kernels  45.9 us (14%)
  local copies, waits for them, and re-layouts  45.6 us (14%)
  starting transfers between devices  42.3 us (13%)
  between operations  14 us (4%)
  other arithmetic  11.2 us (3%)
    pallas_call x4, Pallas kernels, flash_partial(): pl.pallas_call(kernel, out_shape=(jax.ShapeDtypeStruct((tok_rows, width),...  45.9 us
    all_to_all x1, waiting for transfers between devices, spectral_conv(): lax.all_to_all(jnp.concatenate([source_re, source_im, filter_re, filter_i...  32.7 us
    reduce_scatter x1, waiting for transfers between devices, local(): lax.psum_scatter((conv_part + jnp.dot(attended, w_attn_out, preferred_ele...  30.1 us
    all_to_all x1, waiting for transfers between devices, spectral_conv(): lax.all_to_all(jnp.concatenate([turned_re, turned_im], axis=2).astype(jnp...  29.3 us
    all_to_all x1, waiting for transfers between devices, spectral_conv(): lax.all_to_all(jnp.concatenate([gated, filters], axis=1).reshape(1, tok_r...  15.7 us
    all_to_all x1, starting transfers between devices, spectral_conv(): lax.all_to_all(jnp.concatenate([gated, filters], axis=1).reshape(1, tok_r...  11.5 us
    dot_general x1, matrix products, local(): jnp.dot(attended, w_attn_out, preferred_element_type=jnp.float32)  8.58 us
    ppermute x3, starting transfers between devices, attention(): lax.ppermute(jnp.concatenate([cross[0], stats.T], axis=1), 'z', [(k - shi...  8.58 us
  transfers between devices with their start and end apart: 13, of which 6 were waited for; matrix products, arithmetic and copies ran while one was open for 26% of the time, Pallas kernels for 14%

profile of v8, /device:TPU:1, one launch (start us, length us, event | category | flops | bytes accessed | tf_op | source)
XLA Modules:
  0.0 327.4 jit_solution(9924777338328125389)
XLA Ops:
  10.8 3.9 %reduce.8 = bf16[224,1088]{1,0:T(8,128)(2,1)S(1)} reduce(bf16[224,1,1088]{2,1,0:T(2,128)(2,1)S(1)} %bitcast.177, bf16[]{:T(256)} %broadcast.214), dimensions={1}, to_apply=%bitcast.170.reduce_sub_computation | reduce | bytes 974850
  16.4 11.5 %all-to-all-start = ((bf16[32,2,3808]{2,1,0:T(2,128)(2,1)}), bf16[32,2,3808]{2,1,0:T(2,128)(2,1)S(1)}, u32[]{:S(2)}, u32[]{:S(2)}) async-start(bf16[32,2,3808]{2,1,0:T(2,128)(2,1)} %reshape.185), calls=%async_computation | async-start | bytes 983040 | tf_op jit(solution)/shard_map/all_to_all | solution.py:49
  28.1 15.7 %all-to-all-done = bf16[32,2,3808]{2,1,0:T(2,128)(2,1)S(1)} async-done(((bf16[32,2,3808]{2,1,0:T(2,128)(2,1)}), bf16[32,2,3808]{2,1,0:T(2,128)(2,1)S(1)}, u32[]{:S(2)}, u32[]{:S(2)}) %all-to-all-start) | async-done | bytes 487456 | tf_op jit(solution)/shard_map/all_to_all | solution.py:49
  44.7 2.9 bitcast_reduce_fusion
  57.6 4.6 %all-to-all-start.1 = ((bf16[64,7,2176]{2,1,0:T(8,128)(2,1)}), bf16[64,7,2176]{2,1,0:T(8,128)(2,1)S(1)}, u32[]{:S(2)}, u32[]{:S(2)}) async-start(bf16[64,7,2176]{2,1,0:T(8,128)(2,1)} %copy.96), calls=%async_computation.1 | async-start | bytes 4456448 | tf_op jit(solution)/shard_map/all_to_all | solution.py:68
  63.1 32.7 %all-to-all-done.1 = bf16[64,7,2176]{2,1,0:T(8,128)(2,1)S(1)} async-done(((bf16[64,7,2176]{2,1,0:T(8,128)(2,1)}), bf16[64,7,2176]{2,1,0:T(8,128)(2,1)S(1)}, u32[]{:S(2)}, u32[]{:S(2)}) %all-to-all-start.1) | async-done | bytes 1949728 | tf_op jit(solution)/shard_map/all_to_all | solution.py:68
  122.0 2.8 fusion.40
  127.5 3.8 %fusion.9 = (bf16[2,224,1024]{2,1,0:T(8,128)(2,1)S(1)}, bf16[2,224,1024]{2,1,0:T(8,128)(2,1)S(1)}) fusion(f32[2,1024,224]{1,2,0:T(8,128)S(1)} %convolution_add_fusion.1, f32[2,224]{1,0:T(2,128)S(1)} %get-tuple-element.48, f32[2,224]{1,0:T(2,128)S(1)} %get-tuple-element.47, f32[2,1024,224]{1,2,0:T(8,128)S(1)} %fusion.40, ...), kind=kOutput, calls=%fused_computation.30 | convolution fusion | flops 1237705728 | bytes 7343616 | tf_op jit(solution)/shard_map/kn,anc->akc/dot_general | solution.py:39
  131.5 3.2 copy.106
  134.7 7.9 %all-to-all-start.2 = ((bf16[2,224,2048]{2,0,1:T(2,128)(2,1)}), bf16[2,224,2048]{2,0,1:T(2,128)(2,1)S(1)}, u32[]{:S(2)}, u32[]{:S(2)}) async-start(bf16[2,224,2048]{2,0,1:T(2,128)(2,1)} %copy.106), calls=%async_computation.2 | async-start | bytes 3670016 | tf_op jit(solution)/shard_map/all_to_all | solution.py:99
  143.9 29.3 %all-to-all-done.2 = bf16[2,224,2048]{2,0,1:T(2,128)(2,1)S(1)} async-done(((bf16[2,224,2048]{2,0,1:T(2,128)(2,1)}), bf16[2,224,2048]{2,0,1:T(2,128)(2,1)S(1)}, u32[]{:S(2)}, u32[]{:S(2)}) %all-to-all-start.2) | async-done | bytes 1835040 | tf_op jit(solution)/shard_map/all_to_all | solution.py:99
  173.2 2.8 copy.107
  175.9 4.3 %all_to_all.51 = bf16[64,7,2048]{2,0,1:T(8,128)(2,1)S(1)} reshape(bf16[32,2,7,2048]{3,1,0,2:T(2,128)(2,1)} %copy.107) | data formatting | bytes 3670016 | tf_op jit(solution)/shard_map/all_to_all | solution.py:99
  182.5 5.6 %all-to-all-start.3 = ((bf16[32,7,1024]{2,1,0:T(8,128)(2,1)}), bf16[32,7,1024]{2,1,0:T(8,128)(2,1)S(1)}, u32[]{:S(2)}, u32[]{:S(2)}) async-start(bf16[32,7,1024]{2,1,0:T(8,128)(2,1)} %copy.108), calls=%async_computation.3 | async-start | bytes 1048576 | tf_op jit(solution)/shard_map/all_to_all | solution.py:108
  190.9 8.5 %all-to-all-done.3 = bf16[32,7,1024]{2,1,0:T(8,128)(2,1)S(1)} async-done(((bf16[32,7,1024]{2,1,0:T(8,128)(2,1)}), bf16[32,7,1024]{2,1,0:T(8,128)(2,1)S(1)}, u32[]{:S(2)}, u32[]{:S(2)}) %all-to-all-start.3) | async-done | bytes 458784 | tf_op jit(solution)/shard_map/all_to_all | solution.py:108
  202.3 12.2 %shard_map.93 = (f32[224,1024]{1,0:T(8,128)S(1)}, f32[8,224,1]{2,1,0:T(8,128)S(1)}, f32[8,224,1]{2,1,0:T(8,128)S(1)}) custom-call(s32[2]{0:T(128)S(1)} %copy-done.3, bf16[224,1024]{1,0:T(8,128)(2,1)S(1)} %copy-done.2, bf16[1792,1024]{1,0:T(8,128)(2,1)} %all-gather.3.cloned.1.call-done.k_ref, bf16[1792,1024]{1,0:T(8,128)(2,1)} %all-gather.5.cloned.1.call-done.v_ref), custom_call_target="tpu_custom_call" | custom-call | flops 1644167168 | bytes 8716288 | tf_op jit(solution)/shard_map/pallas_call | solution.py:173
  216.4 3.7 %collective-permute-start.5 = (f32[224,1040]{1,0:T(8,128)}, f32[224,1040]{1,0:T(8,128)}, u32[]{:S(2)}, u32[]{:S(2)}) collective-permute-start(f32[224,1040]{1,0:T(8,128)} %pad_maximum_fusion.3), channel_id=1, source_target_pairs={{0,96},{1,97},{2,98},{3,99},{4,100},{5,101},{6,102},{7,103},{8,104... | collective-permute-start | bytes 2795528 | tf_op jit(solution)/shard_map/ppermute | solution.py:218
  220.1 12.7 %shard_map.92 = (f32[224,1024]{1,0:T(8,128)S(1)}, f32[8,224,1]{2,1,0:T(8,128)S(1)}, f32[8,224,1]{2,1,0:T(8,128)S(1)}) custom-call(s32[2]{0:T(128)S(1)} %copy-done.3, bf16[224,1024]{1,0:T(8,128)(2,1)} %collective-permute-done.2.q_ref, bf16[1792,1024]{1,0:T(8,128)(2,1)} %all-gather.3.cloned.1.call-done.k_ref, bf16[1792,1024]{1,0:T(8,128)(2,1)} %all-gather.5.cloned.1.call-done.v_ref), custom_call_target="tpu_custom_call" | custom-call | flops 1644167168 | bytes 8716288 | tf_op jit(solution)/shard_map/pallas_call | solution.py:173
  237.3 12.5 %shard_map.91 = (f32[224,1024]{1,0:T(8,128)S(1)}, f32[8,224,1]{2,1,0:T(8,128)S(1)}, f32[8,224,1]{2,1,0:T(8,128)S(1)}) custom-call(s32[2]{0:T(128)S(1)} %copy-done.3, bf16[224,1024]{1,0:T(8,128)(2,1)} %collective-permute-done.q_ref, bf16[1792,1024]{1,0:T(8,128)(2,1)} %all-gather.3.cloned.1.call-done.k_ref, bf16[1792,1024]{1,0:T(8,128)(2,1)} %all-gather.5.cloned.1.call-done.v_ref), custom_call_target="tpu_custom_call" | custom-call | flops 1644167168 | bytes 8716288 | tf_op jit(solution)/shard_map/pallas_call | solution.py:173
  254.0 7.4 %fusion.24 = f32[224,4096]{1,0:T(8,128)} fusion(bf16[1024,4096]{1,0:T(8,128)(2,1)} %param.16, f32[224,1024]{1,0:T(8,128)S(1)} %copy-done.8, bf16[224,1024]{1,0:T(8,128)(2,1)S(1)} %copy-done.9), kind=kOutput, calls=%fused_computation.53 | convolution fusion | flops 1879736320 | bytes 13434880 | tf_op jit(solution)/shard_map/dot_general | solution.py:250
  261.4 8.4 %shard_map.94 = (f32[224,1024]{1,0:T(8,128)S(1)}, f32[8,224,1]{2,1,0:T(8,128)S(1)}, f32[8,224,1]{2,1,0:T(8,128)S(1)}) custom-call(s32[2]{0:T(128)S(1)} %pad_add_fusion.info_ref, bf16[224,1024]{1,0:T(8,128)(2,1)S(1)} %copy-done, bf16[1792,1024]{1,0:T(8,128)(2,1)} %all-gather.3.cloned.1.call-done.k_ref, bf16[1792,1024]{1,0:T(8,128)(2,1)} %all-gather.5.cloned.1.call-done.v_ref), custom_call_target="tpu_custom_call" | custom-call | flops 1644167168 | bytes 8716288 | tf_op jit(solution)/shard_map/pallas_call | solution.py:173
  274.4 4.0 %collective-permute-done.1 = f32[224,1040]{1,0:T(8,128)} collective-permute-done((f32[224,1040]{1,0:T(8,128)}, f32[224,1040]{1,0:T(8,128)}, u32[]{:S(2)}, u32[]{:S(2)}) %collective-permute-start.1) | collective-permute-done | bytes 931872 | tf_op jit(solution)/shard_map/ppermute | solution.py:218
  281.9 8.6 %fusion = bf16[224,4096]{1,0:T(8,128)(2,1)} fusion(f32[224,4096]{1,0:T(8,128)S(1)} %copy-done.4, bf16[1024,4096]{1,0:T(8,128)(2,1)} %param.17, f32[28,8,8,128]{3,2,1,0:T(8,128)S(1)} %bitcast.181, f32[224,1024]{1,0:T(8,128)S(1)} %get-tuple-element.27, f32[28,8,8,128]{3,2,1,0:T(8,128)S(1)} %bitcast.180, f32[28,8,8,128]{3,2,1,0:T(8,128)S(1)} %bitcast.179, ...), kind=kOutput, calls=%fused_computation.1 | convolution fusion | flops 1882947584 | bytes 22151168 | tf_op jit(solution)/shard_map/dot_general | solution.py:253
  290.5 30.1 %reduce-scatter.2.cloned.1.call-done = bf16[56,4096]{1,0:T(8,128)(2,1)} async-done(((bf16[224,4096]{1,0:T(8,128)(2,1)}), bf16[56,4096]{1,0:T(8,128)(2,1)}) %reduce-scatter.2.cloned.1.call-update) | async-done | bytes 458768 | tf_op jit(solution)/shard_map/reduce_scatter | solution.py:252
  (110 shorter events, 74.3 us)
Async XLA Ops:
  6.5 194.7 %all-gather.3.cloned.1.call-start = ((), (), s32[]{:S(2)}) async-start(), calls=%async_computation.5 | async-start | bytes 4128768 | tf_op jit(solution)/shard_map/all_gather | solution.py:207
  16.4 27.4 %all-to-all-start = ((bf16[32,2,3808]{2,1,0:T(2,128)(2,1)}), bf16[32,2,3808]{2,1,0:T(2,128)(2,1)S(1)}, u32[]{:S(2)}, u32[]{:S(2)}) async-start(bf16[32,2,3808]{2,1,0:T(2,128)(2,1)} %reshape.185), calls=%async_computation | async-start | bytes 983040 | tf_op jit(solution)/shard_map/all_to_all | solution.py:49
  57.6 38.3 %all-to-all-start.1 = ((bf16[64,7,2176]{2,1,0:T(8,128)(2,1)}), bf16[64,7,2176]{2,1,0:T(8,128)(2,1)S(1)}, u32[]{:S(2)}, u32[]{:S(2)}) async-start(bf16[64,7,2176]{2,1,0:T(8,128)(2,1)} %copy.96), calls=%async_computation.1 | async-start | bytes 4456448 | tf_op jit(solution)/shard_map/all_to_all | solution.py:68
  62.2 139.0 %all-gather.5.cloned.1.call-start = ((), (), s32[]{:S(2)}) async-start(), calls=%async_computation.6 | async-start | bytes 4128768 | tf_op jit(solution)/shard_map/all_gather | solution.py:208
  97.4 1.4 copy-start.5
  114.7 2.0 copy-start.6
  114.7 2.1 copy-start.7
  134.7 7.9 %copy-start = (bf16[224,1024]{1,0:T(8,128)(2,1)S(1)}, bf16[224,1024]{1,0:T(8,128)(2,1)}, u32[]{:S(2)}) copy-start(bf16[224,1024]{1,0:T(8,128)(2,1)} %q_ref.1) | copy-start | bytes 1376260
  134.7 38.5 %all-to-all-start.2 = ((bf16[2,224,2048]{2,0,1:T(2,128)(2,1)}), bf16[2,224,2048]{2,0,1:T(2,128)(2,1)S(1)}, u32[]{:S(2)}, u32[]{:S(2)}) async-start(bf16[2,224,2048]{2,0,1:T(2,128)(2,1)} %copy.106), calls=%async_computation.2 | async-start | bytes 3670016 | tf_op jit(solution)/shard_map/all_to_all | solution.py:99
  142.6 57.9 %collective-permute-start.4 = (bf16[224,1024]{1,0:T(8,128)(2,1)S(1)}, bf16[224,1024]{1,0:T(8,128)(2,1)S(1)}, u32[]{:S(2)}, u32[]{:S(2)}) collective-permute-start(bf16[224,1024]{1,0:T(8,128)(2,1)S(1)} %copy-done), channel_id=1, source_target_pairs={{96,0},{97,1},{98,2},{99,3},{100,4},{101,5},{102,6},{103,7},{104,8... | collective-permute-start | bytes 1376264 | tf_op jit(solution)/shard_map/ppermute | solution.py:213
  181.5 19.8 %copy-start.3 = (s32[2]{0:T(128)S(1)}, s32[2]{0:T(128)}, u32[]{:S(2)}) copy-start(s32[2]{0:T(128)} %constant.98.clone.1.info_ref) | copy-start | bytes 28
  182.5 16.8 %all-to-all-start.3 = ((bf16[32,7,1024]{2,1,0:T(8,128)(2,1)}), bf16[32,7,1024]{2,1,0:T(8,128)(2,1)S(1)}, u32[]{:S(2)}, u32[]{:S(2)}) async-start(bf16[32,7,1024]{2,1,0:T(8,128)(2,1)} %copy.108), calls=%async_computation.3 | async-start | bytes 1048576 | tf_op jit(solution)/shard_map/all_to_all | solution.py:108
  188.1 132.5 %reduce-scatter.2.cloned.1.call-start = ((), (), s32[]{:S(2)}) async-start(), calls=%async_computation.7 | async-start | bytes 2293760 | tf_op jit(solution)/shard_map/reduce_scatter | solution.py:252
  188.2 31.9 %collective-permute-start.2 = (bf16[224,1024]{1,0:T(8,128)(2,1)S(1)}, bf16[224,1024]{1,0:T(8,128)(2,1)}, u32[]{:S(2)}, u32[]{:S(2)}) collective-permute-start(bf16[224,1024]{1,0:T(8,128)(2,1)S(1)} %copy-done), channel_id=1, source_target_pairs={{64,0},{96,32},{65,1},{97,33},{66,2},{98,34},{67,3},{99,35},{68,4}... | collective-permute-start | bytes 1376264 | tf_op jit(solution)/shard_map/ppermute | solution.py:213
  189.4 47.9 %collective-permute-start = (bf16[224,1024]{1,0:T(8,128)(2,1)S(1)}, bf16[224,1024]{1,0:T(8,128)(2,1)}, u32[]{:S(2)}, u32[]{:S(2)}) collective-permute-start(bf16[224,1024]{1,0:T(8,128)(2,1)S(1)} %copy-done), channel_id=1, source_target_pairs={{32,0},{64,32},{96,64},{33,1},{65,33},{97,65},{34,2},{66,34},{98,6... | collective-permute-start | bytes 1376264 | tf_op jit(solution)/shard_map/ppermute | solution.py:213
  200.5 0.8 copy-start.1
  201.3 1.0 copy-start.2
  216.4 56.2 %collective-permute-start.5 = (f32[224,1040]{1,0:T(8,128)}, f32[224,1040]{1,0:T(8,128)}, u32[]{:S(2)}, u32[]{:S(2)}) collective-permute-start(f32[224,1040]{1,0:T(8,128)} %pad_maximum_fusion.3), channel_id=1, source_target_pairs={{0,96},{1,97},{2,98},{3,99},{4,100},{5,101},{6,102},{7,103},{8,104... | collective-permute-start | bytes 2795528 | tf_op jit(solution)/shard_map/ppermute | solution.py:218
  234.7 38.8 %collective-permute-start.3 = (f32[224,1040]{1,0:T(8,128)}, f32[224,1040]{1,0:T(8,128)}, u32[]{:S(2)}, u32[]{:S(2)}) collective-permute-start(f32[224,1040]{1,0:T(8,128)} %pad_maximum_fusion.2), channel_id=1, source_target_pairs={{0,64},{32,96},{1,65},{33,97},{2,66},{34,98},{3,67},{35,99},{4,68}... | collective-permute-start | bytes 2795528 | tf_op jit(solution)/shard_map/ppermute | solution.py:218
  250.2 3.8 %copy-start.8 = (f32[224,1024]{1,0:T(8,128)S(1)}, f32[224,1024]{1,0:T(8,128)}, u32[]{:S(2)}) copy-start(f32[224,1024]{1,0:T(8,128)} %reshape.173) | copy-start | bytes 2752516
  250.5 3.4 %copy-start.9 = (bf16[224,1024]{1,0:T(8,128)(2,1)S(1)}, bf16[224,1024]{1,0:T(8,128)(2,1)}, u32[]{:S(2)}) copy-start(bf16[224,1024]{1,0:T(8,128)(2,1)} %param.9) | copy-start | bytes 1376260
  251.7 26.7 %collective-permute-start.1 = (f32[224,1040]{1,0:T(8,128)}, f32[224,1040]{1,0:T(8,128)}, u32[]{:S(2)}, u32[]{:S(2)}) collective-permute-start(f32[224,1040]{1,0:T(8,128)} %pad_maximum_fusion.1), channel_id=1, source_target_pairs={{0,32},{32,64},{64,96},{1,33},{33,65},{65,97},{2,34},{34,66},{66,9... | collective-permute-start | bytes 2795528 | tf_op jit(solution)/shard_map/ppermute | solution.py:218
  279.9 2.0 copy-start.4
Sparse Core Ops, SparseCore 0:
  9.6 95.1 all-gather.2
  107.2 86.1 all-gather.4
  290.6 29.9 reduce-scatter.1

commit v9 on v8

--- a/solution.py
+++ b/solution.py
@@ -131,8 +131,8 @@
             query_pos = q_first + lax.broadcasted_iota(jnp.int32, (tok_rows, key_block), 0)
             key_pos = key_first + lax.broadcasted_iota(jnp.int32, (tok_rows, key_block), 1)
             allowed = key_pos <= query_pos
-        for h in range(heads):
-            cols = slice(h * HD, (h + 1) * HD)
+        def one_head(h, carry):
+            cols = pl.ds(pl.multiple_of(h * HD, HD), HD)
             scores = lax.dot_general(
                 q_ref[:, cols], k_ref[:, cols], (((1,), (1,)), ((), ())),
                 preferred_element_type=jnp.float32,
@@ -150,6 +150,9 @@
                 weights.astype(jnp.bfloat16), v_ref[:, cols], preferred_element_type=jnp.float32
             )
             m_ref[h] = m_new
+            return carry
+
+        lax.fori_loop(0, heads, one_head, 0)
 
     full = key_first + key_block <= q_first
 

time: 333 us -> 341 us (1.024)
  Pallas kernels: 45.9 us -> 55.5 us
    pallas_call x4, Pallas kernels: 45.9 us -> 55.5 us  [flash_partial(): pl.pallas_call(kernel, out_shape=(jax.ShapeDtypeStruct((tok_rows, width),...]
    ppermute x3, waiting for transfers between devices: 4.01 us -> 0.26 us  [attention(): lax.ppermute(jnp.concatenate([cross[0], stats.T], axis=1), 'z', [(k - shi...]
  transfers between devices with their start and end apart: 13 -> 13, of which waited for: 6 -> 6; matrix products, arithmetic and copies ran while one was open for 26% -> 25% of each run, Pallas kernels for 14% -> 17%
where the time goes in v9:
time: 341 us; the launch traced here: 335 us
  waiting for transfers between devices  119 us (35%)
  Pallas kernels  55.5 us (16%)
  matrix products  46.9 us (14%)
  local copies, waits for them, and re-layouts  45.7 us (13%)
  starting transfers between devices  42.4 us (12%)
  between operations  14.1 us (4%)
  other arithmetic  11.2 us (3%)
    pallas_call x4, Pallas kernels, flash_partial(): pl.pallas_call(kernel, out_shape=(jax.ShapeDtypeStruct((tok_rows, width),...  55.5 us
    all_to_all x1, waiting for transfers between devices, spectral_conv(): lax.all_to_all(jnp.concatenate([source_re, source_im, filter_re, filter_i...  32.7 us
    reduce_scatter x1, waiting for transfers between devices, local(): lax.psum_scatter((conv_part + jnp.dot(attended, w_attn_out, preferred_ele...  31.5 us
    all_to_all x1, waiting for transfers between devices, spectral_conv(): lax.all_to_all(jnp.concatenate([turned_re, turned_im], axis=2).astype(jnp...  29.2 us
    all_to_all x1, waiting for transfers between devices, spectral_conv(): lax.all_to_all(jnp.concatenate([gated, filters], axis=1).reshape(1, tok_r...  15.6 us
    all_to_all x1, starting transfers between devices, spectral_conv(): lax.all_to_all(jnp.concatenate([gated, filters], axis=1).reshape(1, tok_r...  11.5 us
    dot_general x1, matrix products, local(): jnp.dot(attended, w_attn_out, preferred_element_type=jnp.float32)  8.58 us
    ppermute x3, starting transfers between devices, attention(): lax.ppermute(jnp.concatenate([cross[0], stats.T], axis=1), 'z', [(k - shi...  8.56 us
  transfers between devices with their start and end apart: 13, of which 6 were waited for; matrix products, arithmetic and copies ran while one was open for 25% of the time, Pallas kernels for 17%

profile of v9, /device:TPU:1, one launch (start us, length us, event | category | flops | bytes accessed | tf_op | source)
XLA Modules:
  0.0 334.9 jit_solution(18010930844273926378)
XLA Ops:
  10.8 3.9 %reduce.8 = bf16[224,1088]{1,0:T(8,128)(2,1)S(1)} reduce(bf16[224,1,1088]{2,1,0:T(2,128)(2,1)S(1)} %bitcast.177, bf16[]{:T(256)} %broadcast.214), dimensions={1}, to_apply=%bitcast.170.reduce_sub_computation | reduce | bytes 974850
  16.4 11.5 %all-to-all-start = ((bf16[32,2,3808]{2,1,0:T(2,128)(2,1)}), bf16[32,2,3808]{2,1,0:T(2,128)(2,1)S(1)}, u32[]{:S(2)}, u32[]{:S(2)}) async-start(bf16[32,2,3808]{2,1,0:T(2,128)(2,1)} %reshape.185), calls=%async_computation | async-start | bytes 983040 | tf_op jit(solution)/shard_map/all_to_all | solution.py:49
  28.1 15.6 %all-to-all-done = bf16[32,2,3808]{2,1,0:T(2,128)(2,1)S(1)} async-done(((bf16[32,2,3808]{2,1,0:T(2,128)(2,1)}), bf16[32,2,3808]{2,1,0:T(2,128)(2,1)S(1)}, u32[]{:S(2)}, u32[]{:S(2)}) %all-to-all-start) | async-done | bytes 487456 | tf_op jit(solution)/shard_map/all_to_all | solution.py:49
  44.7 2.9 bitcast_reduce_fusion
  57.6 4.6 %all-to-all-start.1 = ((bf16[64,7,2176]{2,1,0:T(8,128)(2,1)}), bf16[64,7,2176]{2,1,0:T(8,128)(2,1)S(1)}, u32[]{:S(2)}, u32[]{:S(2)}) async-start(bf16[64,7,2176]{2,1,0:T(8,128)(2,1)} %copy.96), calls=%async_computation.1 | async-start | bytes 4456448 | tf_op jit(solution)/shard_map/all_to_all | solution.py:68
  63.1 32.7 %all-to-all-done.1 = bf16[64,7,2176]{2,1,0:T(8,128)(2,1)S(1)} async-done(((bf16[64,7,2176]{2,1,0:T(8,128)(2,1)}), bf16[64,7,2176]{2,1,0:T(8,128)(2,1)S(1)}, u32[]{:S(2)}, u32[]{:S(2)}) %all-to-all-start.1) | async-done | bytes 1949728 | tf_op jit(solution)/shard_map/all_to_all | solution.py:68
  108.3 2.7 fusion.205
  122.1 2.8 fusion.40
  127.6 3.8 %fusion.9 = (bf16[2,224,1024]{2,1,0:T(8,128)(2,1)S(1)}, bf16[2,224,1024]{2,1,0:T(8,128)(2,1)S(1)}) fusion(f32[2,1024,224]{1,2,0:T(8,128)S(1)} %convolution_add_fusion.1, f32[2,224]{1,0:T(2,128)S(1)} %get-tuple-element.48, f32[2,224]{1,0:T(2,128)S(1)} %get-tuple-element.47, f32[2,1024,224]{1,2,0:T(8,128)S(1)} %fusion.40, ...), kind=kOutput, calls=%fused_computation.30 | convolution fusion | flops 1237705728 | bytes 7343616 | tf_op jit(solution)/shard_map/kn,anc->akc/dot_general | solution.py:39
  131.6 3.2 copy.106
  134.8 7.8 %all-to-all-start.2 = ((bf16[2,224,2048]{2,0,1:T(2,128)(2,1)}), bf16[2,224,2048]{2,0,1:T(2,128)(2,1)S(1)}, u32[]{:S(2)}, u32[]{:S(2)}) async-start(bf16[2,224,2048]{2,0,1:T(2,128)(2,1)} %copy.106), calls=%async_computation.2 | async-start | bytes 3670016 | tf_op jit(solution)/shard_map/all_to_all | solution.py:99
  143.9 29.2 %all-to-all-done.2 = bf16[2,224,2048]{2,0,1:T(2,128)(2,1)S(1)} async-done(((bf16[2,224,2048]{2,0,1:T(2,128)(2,1)}), bf16[2,224,2048]{2,0,1:T(2,128)(2,1)S(1)}, u32[]{:S(2)}, u32[]{:S(2)}) %all-to-all-start.2) | async-done | bytes 1835040 | tf_op jit(solution)/shard_map/all_to_all | solution.py:99
  173.2 2.8 copy.107
  175.9 4.3 %all_to_all.51 = bf16[64,7,2048]{2,0,1:T(8,128)(2,1)S(1)} reshape(bf16[32,2,7,2048]{3,1,0,2:T(2,128)(2,1)} %copy.107) | data formatting | bytes 3670016 | tf_op jit(solution)/shard_map/all_to_all | solution.py:99
  182.5 5.6 %all-to-all-start.3 = ((bf16[32,7,1024]{2,1,0:T(8,128)(2,1)}), bf16[32,7,1024]{2,1,0:T(8,128)(2,1)S(1)}, u32[]{:S(2)}, u32[]{:S(2)}) async-start(bf16[32,7,1024]{2,1,0:T(8,128)(2,1)} %copy.108), calls=%async_computation.3 | async-start | bytes 1048576 | tf_op jit(solution)/shard_map/all_to_all | solution.py:108
  190.9 8.5 %all-to-all-done.3 = bf16[32,7,1024]{2,1,0:T(8,128)(2,1)S(1)} async-done(((bf16[32,7,1024]{2,1,0:T(8,128)(2,1)}), bf16[32,7,1024]{2,1,0:T(8,128)(2,1)S(1)}, u32[]{:S(2)}, u32[]{:S(2)}) %all-to-all-start.3) | async-done | bytes 458784 | tf_op jit(solution)/shard_map/all_to_all | solution.py:108
  202.3 15.2 %shard_map.93 = (f32[224,1024]{1,0:T(8,128)S(1)}, f32[8,224,1]{2,1,0:T(8,128)S(1)}, f32[8,224,1]{2,1,0:T(8,128)S(1)}) custom-call(s32[2]{0:T(128)S(1)} %copy-done.3, bf16[224,1024]{1,0:T(8,128)(2,1)S(1)} %copy-done.2, bf16[1792,1024]{1,0:T(8,128)(2,1)} %all-gather.3.cloned.1.call-done.k_ref, bf16[1792,1024]{1,0:T(8,128)(2,1)} %all-gather.5.cloned.1.call-done.v_ref), custom_call_target="tpu_custom_call" | custom-call | flops 1644167168 | bytes 8716288 | tf_op jit(solution)/shard_map/pallas_call | solution.py:176
  219.4 3.7 %collective-permute-start.5 = (f32[224,1040]{1,0:T(8,128)}, f32[224,1040]{1,0:T(8,128)}, u32[]{:S(2)}, u32[]{:S(2)}) collective-permute-start(f32[224,1040]{1,0:T(8,128)} %pad_maximum_fusion.3), channel_id=1, source_target_pairs={{0,96},{1,97},{2,98},{3,99},{4,100},{5,101},{6,102},{7,103},{8,104... | collective-permute-start | bytes 2795528 | tf_op jit(solution)/shard_map/ppermute | solution.py:221
  223.1 15.3 %shard_map.92 = (f32[224,1024]{1,0:T(8,128)S(1)}, f32[8,224,1]{2,1,0:T(8,128)S(1)}, f32[8,224,1]{2,1,0:T(8,128)S(1)}) custom-call(s32[2]{0:T(128)S(1)} %copy-done.3, bf16[224,1024]{1,0:T(8,128)(2,1)} %collective-permute-done.2.q_ref, bf16[1792,1024]{1,0:T(8,128)(2,1)} %all-gather.3.cloned.1.call-done.k_ref, bf16[1792,1024]{1,0:T(8,128)(2,1)} %all-gather.5.cloned.1.call-done.v_ref), custom_call_target="tpu_custom_call" | custom-call | flops 1644167168 | bytes 8716288 | tf_op jit(solution)/shard_map/pallas_call | solution.py:176
  242.9 15.3 %shard_map.91 = (f32[224,1024]{1,0:T(8,128)S(1)}, f32[8,224,1]{2,1,0:T(8,128)S(1)}, f32[8,224,1]{2,1,0:T(8,128)S(1)}) custom-call(s32[2]{0:T(128)S(1)} %copy-done.3, bf16[224,1024]{1,0:T(8,128)(2,1)} %collective-permute-done.q_ref, bf16[1792,1024]{1,0:T(8,128)(2,1)} %all-gather.3.cloned.1.call-done.k_ref, bf16[1792,1024]{1,0:T(8,128)(2,1)} %all-gather.5.cloned.1.call-done.v_ref), custom_call_target="tpu_custom_call" | custom-call | flops 1644167168 | bytes 8716288 | tf_op jit(solution)/shard_map/pallas_call | solution.py:176
  262.4 7.4 %fusion.24 = f32[224,4096]{1,0:T(8,128)} fusion(bf16[1024,4096]{1,0:T(8,128)(2,1)} %param.16, f32[224,1024]{1,0:T(8,128)S(1)} %copy-done.8, bf16[224,1024]{1,0:T(8,128)(2,1)S(1)} %copy-done.9), kind=kOutput, calls=%fused_computation.53 | convolution fusion | flops 1879736320 | bytes 13434880 | tf_op jit(solution)/shard_map/dot_general | solution.py:253
  269.8 9.7 %shard_map.94 = (f32[224,1024]{1,0:T(8,128)S(1)}, f32[8,224,1]{2,1,0:T(8,128)S(1)}, f32[8,224,1]{2,1,0:T(8,128)S(1)}) custom-call(s32[2]{0:T(128)S(1)} %pad_add_fusion.info_ref, bf16[224,1024]{1,0:T(8,128)(2,1)S(1)} %copy-done, bf16[1792,1024]{1,0:T(8,128)(2,1)} %all-gather.3.cloned.1.call-done.k_ref, bf16[1792,1024]{1,0:T(8,128)(2,1)} %all-gather.5.cloned.1.call-done.v_ref), custom_call_target="tpu_custom_call" | custom-call | flops 1644167168 | bytes 8716288 | tf_op jit(solution)/shard_map/pallas_call | solution.py:176
  287.8 8.6 %fusion = bf16[224,4096]{1,0:T(8,128)(2,1)} fusion(f32[224,4096]{1,0:T(8,128)S(1)} %copy-done.4, bf16[1024,4096]{1,0:T(8,128)(2,1)} %param.17, f32[28,8,8,128]{3,2,1,0:T(8,128)S(1)} %bitcast.181, f32[224,1024]{1,0:T(8,128)S(1)} %get-tuple-element.27, f32[28,8,8,128]{3,2,1,0:T(8,128)S(1)} %bitcast.180, f32[28,8,8,128]{3,2,1,0:T(8,128)S(1)} %bitcast.179, ...), kind=kOutput, calls=%fused_computation.1 | convolution fusion | flops 1882947584 | bytes 22151168 | tf_op jit(solution)/shard_map/dot_general | solution.py:256
  296.4 31.5 %reduce-scatter.2.cloned.1.call-done = bf16[56,4096]{1,0:T(8,128)(2,1)} async-done(((bf16[224,4096]{1,0:T(8,128)(2,1)}), bf16[56,4096]{1,0:T(8,128)(2,1)}) %reduce-scatter.2.cloned.1.call-update) | async-done | bytes 458768 | tf_op jit(solution)/shard_map/reduce_scatter | solution.py:255
  (110 shorter events, 71.9 us)
Async XLA Ops:
  6.5 194.7 %all-gather.3.cloned.1.call-start = ((), (), s32[]{:S(2)}) async-start(), calls=%async_computation.5 | async-start | bytes 4128768 | tf_op jit(solution)/shard_map/all_gather | solution.py:210
  16.4 27.3 %all-to-all-start = ((bf16[32,2,3808]{2,1,0:T(2,128)(2,1)}), bf16[32,2,3808]{2,1,0:T(2,128)(2,1)S(1)}, u32[]{:S(2)}, u32[]{:S(2)}) async-start(bf16[32,2,3808]{2,1,0:T(2,128)(2,1)} %reshape.185), calls=%async_computation | async-start | bytes 983040 | tf_op jit(solution)/shard_map/all_to_all | solution.py:49
  57.6 38.3 %all-to-all-start.1 = ((bf16[64,7,2176]{2,1,0:T(8,128)(2,1)}), bf16[64,7,2176]{2,1,0:T(8,128)(2,1)S(1)}, u32[]{:S(2)}, u32[]{:S(2)}) async-start(bf16[64,7,2176]{2,1,0:T(8,128)(2,1)} %copy.96), calls=%async_computation.1 | async-start | bytes 4456448 | tf_op jit(solution)/shard_map/all_to_all | solution.py:68
  62.2 139.1 %all-gather.5.cloned.1.call-start = ((), (), s32[]{:S(2)}) async-start(), calls=%async_computation.6 | async-start | bytes 4128768 | tf_op jit(solution)/shard_map/all_gather | solution.py:211
  97.4 1.4 copy-start.5
  114.7 2.0 copy-start.6
  114.8 2.1 copy-start.7
  134.8 7.9 %copy-start = (bf16[224,1024]{1,0:T(8,128)(2,1)S(1)}, bf16[224,1024]{1,0:T(8,128)(2,1)}, u32[]{:S(2)}) copy-start(bf16[224,1024]{1,0:T(8,128)(2,1)} %q_ref.1) | copy-start | bytes 1376260
  134.8 38.4 %all-to-all-start.2 = ((bf16[2,224,2048]{2,0,1:T(2,128)(2,1)}), bf16[2,224,2048]{2,0,1:T(2,128)(2,1)S(1)}, u32[]{:S(2)}, u32[]{:S(2)}) async-start(bf16[2,224,2048]{2,0,1:T(2,128)(2,1)} %copy.106), calls=%async_computation.2 | async-start | bytes 3670016 | tf_op jit(solution)/shard_map/all_to_all | solution.py:99
  142.6 57.9 %collective-permute-start.4 = (bf16[224,1024]{1,0:T(8,128)(2,1)S(1)}, bf16[224,1024]{1,0:T(8,128)(2,1)S(1)}, u32[]{:S(2)}, u32[]{:S(2)}) collective-permute-start(bf16[224,1024]{1,0:T(8,128)(2,1)S(1)} %copy-done), channel_id=1, source_target_pairs={{96,0},{97,1},{98,2},{99,3},{100,4},{101,5},{102,6},{103,7},{104,8... | collective-permute-start | bytes 1376264 | tf_op jit(solution)/shard_map/ppermute | solution.py:216
  181.5 19.8 %copy-start.3 = (s32[2]{0:T(128)S(1)}, s32[2]{0:T(128)}, u32[]{:S(2)}) copy-start(s32[2]{0:T(128)} %constant.98.clone.1.info_ref) | copy-start | bytes 28
  182.5 16.9 %all-to-all-start.3 = ((bf16[32,7,1024]{2,1,0:T(8,128)(2,1)}), bf16[32,7,1024]{2,1,0:T(8,128)(2,1)S(1)}, u32[]{:S(2)}, u32[]{:S(2)}) async-start(bf16[32,7,1024]{2,1,0:T(8,128)(2,1)} %copy.108), calls=%async_computation.3 | async-start | bytes 1048576 | tf_op jit(solution)/shard_map/all_to_all | solution.py:108
  188.1 139.8 %reduce-scatter.2.cloned.1.call-start = ((), (), s32[]{:S(2)}) async-start(), calls=%async_computation.7 | async-start | bytes 2293760 | tf_op jit(solution)/shard_map/reduce_scatter | solution.py:255
  188.2 34.9 %collective-permute-start.2 = (bf16[224,1024]{1,0:T(8,128)(2,1)S(1)}, bf16[224,1024]{1,0:T(8,128)(2,1)}, u32[]{:S(2)}, u32[]{:S(2)}) collective-permute-start(bf16[224,1024]{1,0:T(8,128)(2,1)S(1)} %copy-done), channel_id=1, source_target_pairs={{64,0},{96,32},{65,1},{97,33},{66,2},{98,34},{67,3},{99,35},{68,4}... | collective-permute-start | bytes 1376264 | tf_op jit(solution)/shard_map/ppermute | solution.py:216
  189.5 53.5 %collective-permute-start = (bf16[224,1024]{1,0:T(8,128)(2,1)S(1)}, bf16[224,1024]{1,0:T(8,128)(2,1)}, u32[]{:S(2)}, u32[]{:S(2)}) collective-permute-start(bf16[224,1024]{1,0:T(8,128)(2,1)S(1)} %copy-done), channel_id=1, source_target_pairs={{32,0},{64,32},{96,64},{33,1},{65,33},{97,65},{34,2},{66,34},{98,6... | collective-permute-start | bytes 1376264 | tf_op jit(solution)/shard_map/ppermute | solution.py:216
  200.5 0.8 copy-start.1
  201.3 1.0 copy-start.2
  219.4 62.8 %collective-permute-start.5 = (f32[224,1040]{1,0:T(8,128)}, f32[224,1040]{1,0:T(8,128)}, u32[]{:S(2)}, u32[]{:S(2)}) collective-permute-start(f32[224,1040]{1,0:T(8,128)} %pad_maximum_fusion.3), channel_id=1, source_target_pairs={{0,96},{1,97},{2,98},{3,99},{4,100},{5,101},{6,102},{7,103},{8,104... | collective-permute-start | bytes 2795528 | tf_op jit(solution)/shard_map/ppermute | solution.py:221
  240.3 42.8 %collective-permute-start.3 = (f32[224,1040]{1,0:T(8,128)}, f32[224,1040]{1,0:T(8,128)}, u32[]{:S(2)}, u32[]{:S(2)}) collective-permute-start(f32[224,1040]{1,0:T(8,128)} %pad_maximum_fusion.2), channel_id=1, source_target_pairs={{0,64},{32,96},{1,65},{33,97},{2,66},{34,98},{3,67},{35,99},{4,68}... | collective-permute-start | bytes 2795528 | tf_op jit(solution)/shard_map/ppermute | solution.py:221
  258.6 3.8 %copy-start.8 = (f32[224,1024]{1,0:T(8,128)S(1)}, f32[224,1024]{1,0:T(8,128)}, u32[]{:S(2)}) copy-start(f32[224,1024]{1,0:T(8,128)} %reshape.173) | copy-start | bytes 2752516
  258.9 3.4 %copy-start.9 = (bf16[224,1024]{1,0:T(8,128)(2,1)S(1)}, bf16[224,1024]{1,0:T(8,128)(2,1)}, u32[]{:S(2)}) copy-start(bf16[224,1024]{1,0:T(8,128)(2,1)} %param.9) | copy-start | bytes 1376260
  260.1 24.2 %collective-permute-start.1 = (f32[224,1040]{1,0:T(8,128)}, f32[224,1040]{1,0:T(8,128)}, u32[]{:S(2)}, u32[]{:S(2)}) collective-permute-start(f32[224,1040]{1,0:T(8,128)} %pad_maximum_fusion.1), channel_id=1, source_target_pairs={{0,32},{32,64},{64,96},{1,33},{33,65},{65,97},{2,34},{34,66},{66,9... | collective-permute-start | bytes 2795528 | tf_op jit(solution)/shard_map/ppermute | solution.py:221
  285.8 2.0 copy-start.4
Sparse Core Ops, SparseCore 0:
  9.6 95.2 all-gather.2
  107.3 86.0 all-gather.4
  296.5 31.3 reduce-scatter.1

commit v10 on v8

--- a/solution.py
+++ b/solution.py
@@ -110,8 +110,9 @@
 
 
 CTX = ("z", "yh", "x")
+GROUP = ("z", "yh")
 EXP2_SCALE = math.log2(math.e) * HD ** (-0.5)
-HALF = ("yh", "x")
+HALF = ("x",)
 
 
 def flash_kernel(info_ref, q_ref, k_ref, v_ref, acc_ref, m_ref, l_ref, *, heads, tok_rows, key_block, scale):
@@ -197,8 +198,10 @@
 def attention(q_attn, k_attn, v_attn, tok_rows):
     width = q_attn.shape[1]
     heads = width // HD
-    quarters = lax.axis_size("z")
-    quarter = lax.axis_index("z")
+    quarters = 1
+    for name in GROUP:
+        quarters = quarters * lax.axis_size(name)
+    quarter = lax.axis_index(GROUP)
     half_count = 1
     for name in HALF:
         half_count = half_count * lax.axis_size(name)
@@ -210,13 +213,13 @@
     key_block = 896 if part_rows % 896 == 0 else tok_rows
     states = []
     for shift in range(1, quarters):
-        visiting = lax.ppermute(q_attn, "z", [(k, k - shift) for k in range(shift, quarters)])
+        visiting = lax.ppermute(q_attn, GROUP, [(k, k - shift) for k in range(shift, quarters)])
         cross = flash_partial(
             visiting, key_part, value_part, jnp.int32(part_rows), jnp.int32(part_rows // key_block), key_block
         )
         stats = jnp.concatenate([cross[1].reshape(heads, tok_rows), cross[2].reshape(heads, tok_rows)])
         back = lax.ppermute(
-            jnp.concatenate([cross[0], stats.T], axis=1), "z", [(k - shift, k) for k in range(shift, quarters)]
+            jnp.concatenate([cross[0], stats.T], axis=1), GROUP, [(k - shift, k) for k in range(shift, quarters)]
         )
         back_stats = back[:, width:].T
         back_max = jnp.where(quarter >= shift, back_stats[:heads], neg_large)

time: 333 us -> 410 us (1.23)
  other arithmetic: 11.2 us -> 36.2 us
  starting transfers between devices: 42.3 us -> 65 us
  local copies, waits for them, and re-layouts: 45.6 us -> 65.8 us
  Pallas kernels: 45.9 us -> 58.1 us
  waiting for transfers between devices: 122 us -> 114 us
    ppermute x6 -> x14, waiting for transfers between devices: 4.02 us -> 45.5 us  [the longest x7 37.8 us: attention(): lax.ppermute(jnp.concatenate([cross[0], stats.T], axis=1), GROUP, [(k - s...]
    all_to_all x1, waiting for transfers between devices: 29.3 us -> 0.01 us  [spectral_conv(): lax.all_to_all(jnp.concatenate([turned_re, turned_im], axis=2).astype(jnp...]
    ppermute x6 -> x14, starting transfers between devices: 12.5 us -> 32.3 us  [the longest x7 23.1 us: attention(): lax.ppermute(jnp.concatenate([cross[0], stats.T], axis=1), GROUP, [(k - s...]
    unnamed x26 -> x92, local copies, waits for them, and re-layouts: 8.3 us -> 22.6 us
    pallas_call x4 -> x8, Pallas kernels: 45.9 us -> 58.1 us  [flash_partial(): pl.pallas_call(kernel, out_shape=(jax.ShapeDtypeStruct((tok_rows, width),...]
    concatenate x3 -> x7, other arithmetic: 3.18 us -> 14.6 us  [attention(): jnp.concatenate([cross[0], stats.T], axis=1)]
    pallas_call x6 -> x14, other arithmetic: 2.04 us -> 13.1 us  [flash_partial(): pl.pallas_call(kernel, out_shape=(jax.ShapeDtypeStruct((tok_rows, width),...]
    all_to_all x1, waiting for transfers between devices: 32.7 us -> 21.8 us  [spectral_conv(): lax.all_to_all(jnp.concatenate([source_re, source_im, filter_re, filter_i...]
  transfers between devices with their start and end apart: 13 -> 21, of which waited for: 6 -> 7; matrix products, arithmetic and copies ran while one was open for 26% -> 23% of each run, Pallas kernels for 14% -> 14%
where the time goes in v10:
time: 410 us; the launch traced here: 403 us
  waiting for transfers between devices  114 us (28%)
  local copies, waits for them, and re-layouts  65.8 us (16%)
  starting transfers between devices  65 us (16%)
  Pallas kernels  58.1 us (14%)
  matrix products  49.4 us (12%)
  other arithmetic  36.2 us (9%)
  between operations  14.4 us (4%)
    pallas_call x8, Pallas kernels, flash_partial(): pl.pallas_call(kernel, out_shape=(jax.ShapeDtypeStruct((tok_rows, width),...  58.1 us
    ppermute x7, waiting for transfers between devices, attention(): lax.ppermute(jnp.concatenate([cross[0], stats.T], axis=1), GROUP, [(k - s...  37.8 us
    reduce_scatter x1, waiting for transfers between devices, local(): lax.psum_scatter((conv_part + jnp.dot(attended, w_attn_out, preferred_ele...  27.1 us
    ppermute x7, starting transfers between devices, attention(): lax.ppermute(jnp.concatenate([cross[0], stats.T], axis=1), GROUP, [(k - s...  23.1 us
    unnamed x92, local copies, waits for them, and re-layouts  22.6 us
    all_to_all x1, waiting for transfers between devices, spectral_conv(): lax.all_to_all(jnp.concatenate([source_re, source_im, filter_re, filter_i...  21.8 us
    concatenate x7, other arithmetic, attention(): jnp.concatenate([cross[0], stats.T], axis=1)  14.6 us
    pallas_call x14, other arithmetic, flash_partial(): pl.pallas_call(kernel, out_shape=(jax.ShapeDtypeStruct((tok_rows, width),...  13.1 us
  transfers between devices with their start and end apart: 21, of which 7 were waited for; matrix products, arithmetic and copies ran while one was open for 23% of the time, Pallas kernels for 14%

profile of v10, /device:TPU:1, one launch (start us, length us, event | category | flops | bytes accessed | tf_op | source)
XLA Modules:
  0.0 403.0 jit_solution(9491792833179329265)
XLA Ops:
  15.7 11.3 %all-to-all-start = ((bf16[32,2,3808]{2,1,0:T(2,128)(2,1)}), bf16[32,2,3808]{2,1,0:T(2,128)(2,1)S(1)}, u32[]{:S(2)}, u32[]{:S(2)}) async-start(bf16[32,2,3808]{2,1,0:T(2,128)(2,1)} %reshape.237), calls=%async_computation | async-start | bytes 983040 | tf_op jit(solution)/shard_map/all_to_all | solution.py:49
  27.9 10.1 %all-to-all-done = bf16[32,2,3808]{2,1,0:T(2,128)(2,1)S(1)} async-done(((bf16[32,2,3808]{2,1,0:T(2,128)(2,1)}), bf16[32,2,3808]{2,1,0:T(2,128)(2,1)S(1)}, u32[]{:S(2)}, u32[]{:S(2)}) %all-to-all-start) | async-done | bytes 487456 | tf_op jit(solution)/shard_map/all_to_all | solution.py:49
  51.8 5.1 %all-to-all-start.1 = ((bf16[64,7,2176]{2,1,0:T(8,128)(2,1)}), bf16[64,7,2176]{2,1,0:T(8,128)(2,1)S(1)}, u32[]{:S(2)}, u32[]{:S(2)}) async-start(bf16[64,7,2176]{2,1,0:T(8,128)(2,1)} %copy.116), calls=%async_computation.1 | async-start | bytes 4456448 | tf_op jit(solution)/shard_map/all_to_all | solution.py:68
  63.9 21.8 %all-to-all-done.1 = bf16[64,7,2176]{2,1,0:T(8,128)(2,1)S(1)} async-done(((bf16[64,7,2176]{2,1,0:T(8,128)(2,1)}), bf16[64,7,2176]{2,1,0:T(8,128)(2,1)S(1)}, u32[]{:S(2)}, u32[]{:S(2)}) %all-to-all-start.1) | async-done | bytes 1949728 | tf_op jit(solution)/shard_map/all_to_all | solution.py:68
  125.5 8.2 %all-to-all-start.2 = ((bf16[2,224,2048]{2,0,1:T(2,128)(2,1)}), bf16[2,224,2048]{2,0,1:T(2,128)(2,1)}, u32[]{:S(2)}, u32[]{:S(2)}) async-start(bf16[2,224,2048]{2,0,1:T(2,128)(2,1)} %copy.126), calls=%async_computation.2 | async-start | bytes 3670016 | tf_op jit(solution)/shard_map/all_to_all | solution.py:99
  136.5 7.3 %shard_map.97 = (f32[224,1024]{1,0:T(8,128)S(1)}, f32[8,224,1]{2,1,0:T(8,128)S(1)}, f32[8,224,1]{2,1,0:T(8,128)S(1)}) custom-call(s32[2]{0:T(128)S(1)} %copy-done.20, bf16[224,1024]{1,0:T(8,128)(2,1)S(1)} %collective-permute-done.12.q_ref, bf16[896,1024]{1,0:T(8,128)(2,1)S(1)} %copy-done, bf16[896,1024]{1,0:T(8,128)(2,1)} %all-gather.5.cloned.1.call-done.v_ref), custom_call_target="tpu_custom_call" | custom-call | flops 822083584 | bytes 5046272 | tf_op jit(solution)/shard_map/pallas_call | solution.py:174
  149.2 7.0 %shard_map.91 = (f32[224,1024]{1,0:T(8,128)S(1)}, f32[8,224,1]{2,1,0:T(8,128)S(1)}, f32[8,224,1]{2,1,0:T(8,128)S(1)}) custom-call(s32[2]{0:T(128)S(1)} %copy-done.20, bf16[224,1024]{1,0:T(8,128)(2,1)} %collective-permute-done.q_ref, bf16[896,1024]{1,0:T(8,128)(2,1)S(1)} %copy-done.1, bf16[896,1024]{1,0:T(8,128)(2,1)} %all-gather.5.cloned.1.call-done.v_ref), custom_call_target="tpu_custom_call" | custom-call | flops 822083584 | bytes 5046272 | tf_op jit(solution)/shard_map/pallas_call | solution.py:174
  162.3 7.7 %collective-permute-done.2.q_ref = bf16[224,1024]{1,0:T(8,128)(2,1)} collective-permute-done((bf16[224,1024]{1,0:T(8,128)(2,1)S(1)}, bf16[224,1024]{1,0:T(8,128)(2,1)}, u32[]{:S(2)}, u32[]{:S(2)}) %collective-permute-start.2) | collective-permute-done | bytes 458784 | tf_op jit(solution)/shard_map/ppermute | solution.py:216
  170.0 9.8 %collective-permute-start.13 = (f32[224,1040]{1,0:T(8,128)}, f32[224,1040]{1,0:T(8,128)}, u32[]{:S(2)}, u32[]{:S(2)}) collective-permute-start(f32[224,1040]{1,0:T(8,128)} %pad_maximum_fusion.7), channel_id=1, source_target_pairs={{0,112},{1,113},{2,114},{3,115},{4,116},{5,117},{6,118},{7,119},{8... | collective-permute-start | bytes 2795528 | tf_op jit(solution)/shard_map/ppermute | solution.py:221
  179.8 7.2 %shard_map.92 = (f32[224,1024]{1,0:T(8,128)S(1)}, f32[8,224,1]{2,1,0:T(8,128)S(1)}, f32[8,224,1]{2,1,0:T(8,128)S(1)}) custom-call(s32[2]{0:T(128)S(1)} %copy-done.20, bf16[224,1024]{1,0:T(8,128)(2,1)} %collective-permute-done.2.q_ref, bf16[896,1024]{1,0:T(8,128)(2,1)S(1)} %copy-done.1, bf16[896,1024]{1,0:T(8,128)(2,1)} %all-gather.5.cloned.1.call-done.v_ref), custom_call_target="tpu_custom_call" | custom-call | flops 822083584 | bytes 5046272 | tf_op jit(solution)/shard_map/pallas_call | solution.py:174
  195.5 7.2 %shard_map.93 = (f32[224,1024]{1,0:T(8,128)S(1)}, f32[8,224,1]{2,1,0:T(8,128)S(1)}, f32[8,224,1]{2,1,0:T(8,128)S(1)}) custom-call(s32[2]{0:T(128)S(1)} %copy-done.20, bf16[224,1024]{1,0:T(8,128)(2,1)} %collective-permute-done.4.q_ref, bf16[896,1024]{1,0:T(8,128)(2,1)S(1)} %copy-done.1, bf16[896,1024]{1,0:T(8,128)(2,1)} %all-gather.5.cloned.1.call-done.v_ref), custom_call_target="tpu_custom_call" | custom-call | flops 822083584 | bytes 5046272 | tf_op jit(solution)/shard_map/pallas_call | solution.py:174
  211.1 7.4 %shard_map.94 = (f32[224,1024]{1,0:T(8,128)S(1)}, f32[8,224,1]{2,1,0:T(8,128)S(1)}, f32[8,224,1]{2,1,0:T(8,128)S(1)}) custom-call(s32[2]{0:T(128)S(1)} %copy-done.20, bf16[224,1024]{1,0:T(8,128)(2,1)} %collective-permute-done.6.q_ref, bf16[896,1024]{1,0:T(8,128)(2,1)S(1)} %copy-done.1, bf16[896,1024]{1,0:T(8,128)(2,1)} %all-gather.5.cloned.1.call-done.v_ref), custom_call_target="tpu_custom_call" | custom-call | flops 822083584 | bytes 5046272 | tf_op jit(solution)/shard_map/pallas_call | solution.py:174
  229.4 7.2 %shard_map.95 = (f32[224,1024]{1,0:T(8,128)S(1)}, f32[8,224,1]{2,1,0:T(8,128)S(1)}, f32[8,224,1]{2,1,0:T(8,128)S(1)}) custom-call(s32[2]{0:T(128)S(1)} %copy-done.20, bf16[224,1024]{1,0:T(8,128)(2,1)} %collective-permute-done.8.q_ref, bf16[896,1024]{1,0:T(8,128)(2,1)S(1)} %copy-done.1, bf16[896,1024]{1,0:T(8,128)(2,1)} %all-gather.5.cloned.1.call-done.v_ref), custom_call_target="tpu_custom_call" | custom-call | flops 822083584 | bytes 5046272 | tf_op jit(solution)/shard_map/pallas_call | solution.py:174
  244.9 7.2 %shard_map.96 = (f32[224,1024]{1,0:T(8,128)S(1)}, f32[8,224,1]{2,1,0:T(8,128)S(1)}, f32[8,224,1]{2,1,0:T(8,128)S(1)}) custom-call(s32[2]{0:T(128)S(1)} %copy-done.20, bf16[224,1024]{1,0:T(8,128)(2,1)} %collective-permute-done.10.q_ref, bf16[896,1024]{1,0:T(8,128)(2,1)S(1)} %copy-done.1, bf16[896,1024]{1,0:T(8,128)(2,1)} %all-gather.5.cloned.1.call-done.v_ref), custom_call_target="tpu_custom_call" | custom-call | flops 822083584 | bytes 5046272 | tf_op jit(solution)/shard_map/pallas_call | solution.py:174
  258.2 7.6 %shard_map.98 = (f32[224,1024]{1,0:T(8,128)S(1)}, f32[8,224,1]{2,1,0:T(8,128)S(1)}, f32[8,224,1]{2,1,0:T(8,128)S(1)}) custom-call(s32[2]{0:T(128)S(1)} %pad_add_fusion.info_ref, bf16[224,1024]{1,0:T(8,128)(2,1)S(1)} %copy-done.19, bf16[896,1024]{1,0:T(8,128)(2,1)S(1)} %copy-done.1, bf16[896,1024]{1,0:T(8,128)(2,1)} %all-gather.5.cloned.1.call-done.v_ref), custom_call_target="tpu_custom_call" | custom-call | flops 822083584 | bytes 5046272 | tf_op jit(solution)/shard_map/pallas_call | solution.py:174
  280.9 5.7 %collective-permute-done.9 = f32[224,1040]{1,0:T(8,128)S(1)} collective-permute-done((f32[224,1040]{1,0:T(8,128)}, f32[224,1040]{1,0:T(8,128)S(1)}, u32[]{:S(2)}, u32[]{:S(2)}) %collective-permute-start.9) | collective-permute-done | bytes 931872 | tf_op jit(solution)/shard_map/ppermute | solution.py:221
  286.6 32.1 %collective-permute-done.11 = f32[224,1040]{1,0:T(8,128)S(1)} collective-permute-done((f32[224,1040]{1,0:T(8,128)}, f32[224,1040]{1,0:T(8,128)S(1)}, u32[]{:S(2)}, u32[]{:S(2)}) %collective-permute-start.11) | collective-permute-done | bytes 931872 | tf_op jit(solution)/shard_map/ppermute | solution.py:221
  320.5 4.2 %copy.127 = bf16[32,2,7,2048]{3,1,0,2:T(2,128)(2,1)} copy(bf16[32,2,7,2048]{3,1,2,0:T(2,128)(2,1)} %bitcast.18) | data formatting | bytes 3670016 | tf_op jit(solution)/shard_map/all_to_all | solution.py:99
  324.7 4.1 %all_to_all.51 = bf16[64,7,2048]{2,0,1:T(8,128)(2,1)S(1)} reshape(bf16[32,2,7,2048]{3,1,0,2:T(2,128)(2,1)} %copy.127) | data formatting | bytes 3670016 | tf_op jit(solution)/shard_map/all_to_all | solution.py:99
  331.1 7.6 %all-to-all-start.3 = ((bf16[32,7,1024]{2,1,0:T(8,128)(2,1)}), bf16[32,7,1024]{2,1,0:T(8,128)(2,1)S(1)}, u32[]{:S(2)}, u32[]{:S(2)}) async-start(bf16[32,7,1024]{2,1,0:T(8,128)(2,1)} %copy.128), calls=%async_computation.3 | async-start | bytes 1048576 | tf_op jit(solution)/shard_map/all_to_all | solution.py:108
  340.6 9.2 %all-to-all-done.3 = bf16[32,7,1024]{2,1,0:T(8,128)(2,1)S(1)} async-done(((bf16[32,7,1024]{2,1,0:T(8,128)(2,1)}), bf16[32,7,1024]{2,1,0:T(8,128)(2,1)S(1)}, u32[]{:S(2)}, u32[]{:S(2)}) %all-to-all-start.3) | async-done | bytes 458784 | tf_op jit(solution)/shard_map/all_to_all | solution.py:108
  350.0 5.5 %fusion.28 = f32[224,4096]{1,0:T(8,128)S(1)} fusion(bf16[1024,4096]{1,0:T(8,128)(2,1)} %param.16, f32[224,1024]{1,0:T(8,128)S(1)} %reshape.217, bf16[224,1024]{1,0:T(8,128)(2,1)S(1)} %copy-done.33), kind=kOutput, calls=%fused_computation.65 | convolution fusion | flops 1879736320 | bytes 13434880 | tf_op jit(solution)/shard_map/dot_general | solution.py:253
  358.8 10.3 %fusion = bf16[224,4096]{1,0:T(8,128)(2,1)} fusion(f32[224,4096]{1,0:T(8,128)S(1)} %fusion.28, bf16[1024,4096]{1,0:T(8,128)(2,1)} %param.17, f32[28,8,8,128]{3,2,1,0:T(8,128)S(1)} %bitcast.230, f32[224,1024]{1,0:T(8,128)S(1)} %get-tuple-element.51, f32[28,8,8,128]{3,2,1,0:T(8,128)S(1)} %bitcast.231, f32[28,8,8,128]{3,2,1,0:T(8,128)S(1)} %bitcast.232, ...), kind=kOutput, calls=%fused_computation.1 | convolution fusion | flops 1884782592 | bytes 29491200 | tf_op jit(solution)/shard_map/dot_general | solution.py:256
  369.2 27.1 %reduce-scatter.2.cloned.1.call-done = bf16[56,4096]{1,0:T(8,128)(2,1)} async-done(((bf16[224,4096]{1,0:T(8,128)(2,1)}), bf16[56,4096]{1,0:T(8,128)(2,1)}) %reduce-scatter.2.cloned.1.call-update) | async-done | bytes 458768 | tf_op jit(solution)/shard_map/reduce_scatter | solution.py:255
  (225 shorter events, 150.7 us)
Async XLA Ops:
  15.7 22.4 %all-to-all-start = ((bf16[32,2,3808]{2,1,0:T(2,128)(2,1)}), bf16[32,2,3808]{2,1,0:T(2,128)(2,1)S(1)}, u32[]{:S(2)}, u32[]{:S(2)}) async-start(bf16[32,2,3808]{2,1,0:T(2,128)(2,1)} %reshape.237), calls=%async_computation | async-start | bytes 983040 | tf_op jit(solution)/shard_map/all_to_all | solution.py:49
  27.0 108.0 %all-gather.3.cloned.1.call-start = ((), (), s32[]{:S(2)}) async-start(), calls=%async_computation.5 | async-start | bytes 2293760 | tf_op jit(solution)/shard_map/all_gather | solution.py:210
  51.8 33.9 %all-to-all-start.1 = ((bf16[64,7,2176]{2,1,0:T(8,128)(2,1)}), bf16[64,7,2176]{2,1,0:T(8,128)(2,1)S(1)}, u32[]{:S(2)}, u32[]{:S(2)}) async-start(bf16[64,7,2176]{2,1,0:T(8,128)(2,1)} %copy.116), calls=%async_computation.1 | async-start | bytes 4456448 | tf_op jit(solution)/shard_map/all_to_all | solution.py:68
  56.8 78.2 %all-gather.5.cloned.1.call-start = ((), (), s32[]{:S(2)}) async-start(), calls=%async_computation.6 | async-start | bytes 2293760 | tf_op jit(solution)/shard_map/all_gather | solution.py:211
  56.9 185.7 %collective-permute-start.10 = (bf16[224,1024]{1,0:T(8,128)(2,1)S(1)}, bf16[224,1024]{1,0:T(8,128)(2,1)}, u32[]{:S(2)}, u32[]{:S(2)}) collective-permute-start(bf16[224,1024]{1,0:T(8,128)(2,1)S(1)} %copy-done.19), channel_id=1, source_target_pairs={{96,0},{112,16},{97,1},{113,17},{98,2},{114,18},{99,3},{115,19},{1... | collective-permute-start | bytes 1376264 | tf_op jit(solution)/shard_map/ppermute | solution.py:216
  58.2 167.6 %collective-permute-start.8 = (bf16[224,1024]{1,0:T(8,128)(2,1)S(1)}, bf16[224,1024]{1,0:T(8,128)(2,1)}, u32[]{:S(2)}, u32[]{:S(2)}) collective-permute-start(bf16[224,1024]{1,0:T(8,128)(2,1)S(1)} %copy-done.19), channel_id=1, source_target_pairs={{80,0},{96,16},{112,32},{81,1},{97,17},{113,33},{82,2},{98,18},{11... | collective-permute-start | bytes 1376264 | tf_op jit(solution)/shard_map/ppermute | solution.py:216
  59.5 149.3 %collective-permute-start.6 = (bf16[224,1024]{1,0:T(8,128)(2,1)S(1)}, bf16[224,1024]{1,0:T(8,128)(2,1)}, u32[]{:S(2)}, u32[]{:S(2)}) collective-permute-start(bf16[224,1024]{1,0:T(8,128)(2,1)S(1)} %copy-done.19), channel_id=1, source_target_pairs={{64,0},{80,16},{96,32},{112,48},{65,1},{81,17},{97,33},{113,49},{6... | collective-permute-start | bytes 1376264 | tf_op jit(solution)/shard_map/ppermute | solution.py:216
  60.8 87.1 %collective-permute-start = (bf16[224,1024]{1,0:T(8,128)(2,1)S(1)}, bf16[224,1024]{1,0:T(8,128)(2,1)}, u32[]{:S(2)}, u32[]{:S(2)}) collective-permute-start(bf16[224,1024]{1,0:T(8,128)(2,1)S(1)} %copy-done.19), channel_id=1, source_target_pairs={{16,0},{32,16},{48,32},{64,48},{80,64},{96,80},{112,96},{17,1},{33... | collective-permute-start | bytes 1376264 | tf_op jit(solution)/shard_map/ppermute | solution.py:216
  62.1 71.6 %collective-permute-start.12 = (bf16[224,1024]{1,0:T(8,128)(2,1)S(1)}, bf16[224,1024]{1,0:T(8,128)(2,1)S(1)}, u32[]{:S(2)}, u32[]{:S(2)}) collective-permute-start(bf16[224,1024]{1,0:T(8,128)(2,1)S(1)} %copy-done.19), channel_id=1, source_target_pairs={{112,0},{113,1},{114,2},{115,3},{116,4},{117,5},{118,6},{119,7},{1... | collective-permute-start | bytes 1376264 | tf_op jit(solution)/shard_map/ppermute | solution.py:216
  125.5 9.6 %copy-start.20 = (s32[2]{0:T(128)S(1)}, s32[2]{0:T(128)}, u32[]{:S(2)}) copy-start(s32[2]{0:T(128)} %constant.104.clone.1.info_ref) | copy-start | bytes 28
  125.5 195.0 %all-to-all-start.2 = ((bf16[2,224,2048]{2,0,1:T(2,128)(2,1)}), bf16[2,224,2048]{2,0,1:T(2,128)(2,1)}, u32[]{:S(2)}, u32[]{:S(2)}) async-start(bf16[2,224,2048]{2,0,1:T(2,128)(2,1)} %copy.126), calls=%async_computation.2 | async-start | bytes 3670016 | tf_op jit(solution)/shard_map/all_to_all | solution.py:99
  133.7 59.5 %collective-permute-start.4 = (bf16[224,1024]{1,0:T(8,128)(2,1)S(1)}, bf16[224,1024]{1,0:T(8,128)(2,1)}, u32[]{:S(2)}, u32[]{:S(2)}) collective-permute-start(bf16[224,1024]{1,0:T(8,128)(2,1)S(1)} %copy-done.19), channel_id=1, source_target_pairs={{48,0},{64,16},{80,32},{96,48},{112,64},{49,1},{65,17},{81,33},{97... | collective-permute-start | bytes 1376264 | tf_op jit(solution)/shard_map/ppermute | solution.py:216
  147.9 22.1 %collective-permute-start.2 = (bf16[224,1024]{1,0:T(8,128)(2,1)S(1)}, bf16[224,1024]{1,0:T(8,128)(2,1)}, u32[]{:S(2)}, u32[]{:S(2)}) collective-permute-start(bf16[224,1024]{1,0:T(8,128)(2,1)S(1)} %copy-done.19), channel_id=1, source_target_pairs={{32,0},{48,16},{64,32},{80,48},{96,64},{112,80},{33,1},{49,17},{65... | collective-permute-start | bytes 1376264 | tf_op jit(solution)/shard_map/ppermute | solution.py:216
  170.0 103.4 %collective-permute-start.13 = (f32[224,1040]{1,0:T(8,128)}, f32[224,1040]{1,0:T(8,128)}, u32[]{:S(2)}, u32[]{:S(2)}) collective-permute-start(f32[224,1040]{1,0:T(8,128)} %pad_maximum_fusion.7), channel_id=1, source_target_pairs={{0,112},{1,113},{2,114},{3,115},{4,116},{5,117},{6,118},{7,119},{8... | collective-permute-start | bytes 2795528 | tf_op jit(solution)/shard_map/ppermute | solution.py:221
  193.2 82.5 %collective-permute-start.1 = (f32[224,1040]{1,0:T(8,128)}, f32[224,1040]{1,0:T(8,128)}, u32[]{:S(2)}, u32[]{:S(2)}) collective-permute-start(f32[224,1040]{1,0:T(8,128)} %pad_maximum_fusion.1), channel_id=1, source_target_pairs={{0,16},{16,32},{32,48},{48,64},{64,80},{80,96},{96,112},{1,17},{17... | collective-permute-start | bytes 2795528 | tf_op jit(solution)/shard_map/ppermute | solution.py:221
  208.8 69.4 %collective-permute-start.3 = (f32[224,1040]{1,0:T(8,128)}, f32[224,1040]{1,0:T(8,128)}, u32[]{:S(2)}, u32[]{:S(2)}) collective-permute-start(f32[224,1040]{1,0:T(8,128)} %pad_maximum_fusion.2), channel_id=1, source_target_pairs={{0,32},{16,48},{32,64},{48,80},{64,96},{80,112},{1,33},{17,49},{33... | collective-permute-start | bytes 2795528 | tf_op jit(solution)/shard_map/ppermute | solution.py:221
  225.8 53.3 %collective-permute-start.5 = (f32[224,1040]{1,0:T(8,128)}, f32[224,1040]{1,0:T(8,128)}, u32[]{:S(2)}, u32[]{:S(2)}) collective-permute-start(f32[224,1040]{1,0:T(8,128)} %pad_maximum_fusion.3), channel_id=1, source_target_pairs={{0,48},{16,64},{32,80},{48,96},{64,112},{1,49},{17,65},{33,81},{49... | collective-permute-start | bytes 2795528 | tf_op jit(solution)/shard_map/ppermute | solution.py:221
  242.6 37.4 %collective-permute-start.7 = (f32[224,1040]{1,0:T(8,128)}, f32[224,1040]{1,0:T(8,128)}, u32[]{:S(2)}, u32[]{:S(2)}) collective-permute-start(f32[224,1040]{1,0:T(8,128)} %pad_maximum_fusion.4), channel_id=1, source_target_pairs={{0,64},{16,80},{32,96},{48,112},{1,65},{17,81},{33,97},{49,113},{2... | collective-permute-start | bytes 2795528 | tf_op jit(solution)/shard_map/ppermute | solution.py:221
  270.2 50.2 %copy-start.27 = (f32[8,224,1]{0,1,2:T(8,128)}, f32[8,224,1]{0,1,2:T(8,128)S(1)}, u32[]{:S(2)}) copy-start(f32[8,224,1]{0,1,2:T(8,128)S(1)} %copy.140) | copy-start | bytes 21508
  273.5 13.2 %collective-permute-start.9 = (f32[224,1040]{1,0:T(8,128)}, f32[224,1040]{1,0:T(8,128)S(1)}, u32[]{:S(2)}, u32[]{:S(2)}) collective-permute-start(f32[224,1040]{1,0:T(8,128)} %pad_maximum_fusion.5), channel_id=1, source_target_pairs={{0,80},{16,96},{32,112},{1,81},{17,97},{33,113},{2,82},{18,98},{34... | collective-permute-start | bytes 2795528 | tf_op jit(solution)/shard_map/ppermute | solution.py:221
  275.7 43.0 %collective-permute-start.11 = (f32[224,1040]{1,0:T(8,128)}, f32[224,1040]{1,0:T(8,128)S(1)}, u32[]{:S(2)}, u32[]{:S(2)}) collective-permute-start(f32[224,1040]{1,0:T(8,128)} %pad_maximum_fusion.6), channel_id=1, source_target_pairs={{0,96},{16,112},{1,97},{17,113},{2,98},{18,114},{3,99},{19,115},{4... | collective-permute-start | bytes 2795528 | tf_op jit(solution)/shard_map/ppermute | solution.py:221
  286.6 33.8 %copy-start.29 = (f32[224,1040]{1,0:T(8,128)}, f32[224,1040]{1,0:T(8,128)S(1)}, u32[]{:S(2)}) copy-start(f32[224,1040]{1,0:T(8,128)S(1)} %collective-permute-done.9) | copy-start | bytes 2795524
  331.1 18.7 %all-to-all-start.3 = ((bf16[32,7,1024]{2,1,0:T(8,128)(2,1)}), bf16[32,7,1024]{2,1,0:T(8,128)(2,1)S(1)}, u32[]{:S(2)}, u32[]{:S(2)}) async-start(bf16[32,7,1024]{2,1,0:T(8,128)(2,1)} %copy.128), calls=%async_computation.3 | async-start | bytes 1048576 | tf_op jit(solution)/shard_map/all_to_all | solution.py:108
  338.7 57.6 %reduce-scatter.2.cloned.1.call-start = ((), (), s32[]{:S(2)}) async-start(), calls=%async_computation.7 | async-start | bytes 2293760 | tf_op jit(solution)/shard_map/reduce_scatter | solution.py:255
  (40 other events, 102.3 us)
Sparse Core Ops, SparseCore 0:
  29.5 30.0 all-gather.2
  63.7 37.8 all-gather.4
  369.3 26.9 reduce-scatter.1

commit v11 on v8

--- a/solution.py
+++ b/solution.py
@@ -209,14 +209,20 @@
     part_rows = key_part.shape[0]
     key_block = 896 if part_rows % 896 == 0 else tok_rows
     states = []
-    for shift in range(1, quarters):
-        visiting = lax.ppermute(q_attn, "z", [(k, k - shift) for k in range(shift, quarters)])
-        cross = flash_partial(
-            visiting, key_part, value_part, jnp.int32(part_rows), jnp.int32(part_rows // key_block), key_block
+    shifts = list(range(1, quarters))
+    visiting = jnp.concatenate(
+        [lax.ppermute(q_attn, "z", [(k, k - shift) for k in range(shift, quarters)]) for shift in shifts]
+    )
+    cross = flash_partial(
+        visiting, key_part, value_part, jnp.int32(part_rows), jnp.int32(part_rows // key_block), key_block
+    )
+    for slot, shift in enumerate(shifts):
+        rows = slice(slot * tok_rows, (slot + 1) * tok_rows)
+        stats = jnp.concatenate(
+            [cross[1][:, rows].reshape(heads, tok_rows), cross[2][:, rows].reshape(heads, tok_rows)]
         )
-        stats = jnp.concatenate([cross[1].reshape(heads, tok_rows), cross[2].reshape(heads, tok_rows)])
         back = lax.ppermute(
-            jnp.concatenate([cross[0], stats.T], axis=1), "z", [(k - shift, k) for k in range(shift, quarters)]
+            jnp.concatenate([cross[0][rows], stats.T], axis=1), "z", [(k - shift, k) for k in range(shift, quarters)]
         )
         back_stats = back[:, width:].T
         back_max = jnp.where(quarter >= shift, back_stats[:heads], neg_large)

time: 333 us -> 342 us (1.027)
  waiting for transfers between devices: 122 us -> 134 us
  Pallas kernels: 45.9 us -> 37.1 us
  local copies, waits for them, and re-layouts: 45.6 us -> 50.9 us
    ppermute x3, waiting for transfers between devices: 4.01 us -> 17.1 us  [attention(): lax.ppermute(jnp.concatenate([cross[0][rows], stats.T], axis=1), 'z', [(k...]
    pallas_call x4 -> x2, Pallas kernels: 45.9 us -> 37.1 us  [flash_partial(): pl.pallas_call(kernel, out_shape=(jax.ShapeDtypeStruct((tok_rows, width),...]
    slice x0 -> x2, local copies, waits for them, and re-layouts: none -> 5.74 us  [the longest x1 4.27 us: attention(): cross[2][:, rows].reshape(heads, tok_rows)]
    unnamed x26 -> x28, local copies, waits for them, and re-layouts: 8.3 us -> 7.76 us
  transfers between devices with their start and end apart: 13 -> 13, of which waited for: 6 -> 7; matrix products, arithmetic and copies ran while one was open for 26% -> 25% of each run, Pallas kernels for 14% -> 2%
where the time goes in v11:
time: 342 us; the launch traced here: 336 us
  waiting for transfers between devices  134 us (39%)
  local copies, waits for them, and re-layouts  50.9 us (15%)
  matrix products  47 us (14%)
  starting transfers between devices  41.6 us (12%)
  Pallas kernels  37.1 us (11%)
  between operations  13.9 us (4%)
  other arithmetic  11.5 us (3%)
    pallas_call x2, Pallas kernels, flash_partial(): pl.pallas_call(kernel, out_shape=(jax.ShapeDtypeStruct((tok_rows, width),...  37.1 us
    all_to_all x1, waiting for transfers between devices, spectral_conv(): lax.all_to_all(jnp.concatenate([source_re, source_im, filter_re, filter_i...  32.6 us
    reduce_scatter x1, waiting for transfers between devices, local(): lax.psum_scatter((conv_part + jnp.dot(attended, w_attn_out, preferred_ele...  30.9 us
    all_to_all x1, waiting for transfers between devices, spectral_conv(): lax.all_to_all(jnp.concatenate([turned_re, turned_im], axis=2).astype(jnp...  27.3 us
    ppermute x3, waiting for transfers between devices, attention(): lax.ppermute(jnp.concatenate([cross[0][rows], stats.T], axis=1), 'z', [(k...  17.1 us
    all_to_all x1, waiting for transfers between devices, spectral_conv(): lax.all_to_all(jnp.concatenate([gated, filters], axis=1).reshape(1, tok_r...  15.6 us
    all_to_all x1, starting transfers between devices, spectral_conv(): lax.all_to_all(jnp.concatenate([gated, filters], axis=1).reshape(1, tok_r...  11.9 us
    all_to_all x1, waiting for transfers between devices, spectral_conv(): lax.all_to_all(rounded, CTX, split_axis=0, concat_axis=1, tiled=True)  9.1 us
  transfers between devices with their start and end apart: 13, of which 7 were waited for; matrix products, arithmetic and copies ran while one was open for 25% of the time, Pallas kernels for 2%

profile of v11, /device:TPU:1, one launch (start us, length us, event | category | flops | bytes accessed | tf_op | source)
XLA Modules:
  0.0 335.9 jit_solution(8153340241702149934)
XLA Ops:
  10.8 3.9 %reduce.14 = bf16[224,1088]{1,0:T(8,128)(2,1)S(1)} reduce(bf16[224,1,1088]{2,1,0:T(2,128)(2,1)S(1)} %bitcast.177, bf16[]{:T(256)} %broadcast.214), dimensions={1}, to_apply=%bitcast.170.reduce_sub_computation | reduce | bytes 974850
  16.4 11.9 %all-to-all-start = ((bf16[32,2,3808]{2,1,0:T(2,128)(2,1)}), bf16[32,2,3808]{2,1,0:T(2,128)(2,1)S(1)}, u32[]{:S(2)}, u32[]{:S(2)}) async-start(bf16[32,2,3808]{2,1,0:T(2,128)(2,1)} %reshape.185), calls=%async_computation | async-start | bytes 983040 | tf_op jit(solution)/shard_map/all_to_all | solution.py:49
  28.4 15.6 %all-to-all-done = bf16[32,2,3808]{2,1,0:T(2,128)(2,1)S(1)} async-done(((bf16[32,2,3808]{2,1,0:T(2,128)(2,1)}), bf16[32,2,3808]{2,1,0:T(2,128)(2,1)S(1)}, u32[]{:S(2)}, u32[]{:S(2)}) %all-to-all-start) | async-done | bytes 487456 | tf_op jit(solution)/shard_map/all_to_all | solution.py:49
  45.0 2.9 bitcast_reduce_fusion
  57.8 4.5 %all-to-all-start.1 = ((bf16[64,7,2176]{2,1,0:T(8,128)(2,1)}), bf16[64,7,2176]{2,1,0:T(8,128)(2,1)S(1)}, u32[]{:S(2)}, u32[]{:S(2)}) async-start(bf16[64,7,2176]{2,1,0:T(8,128)(2,1)} %copy.102), calls=%async_computation.1 | async-start | bytes 4456448 | tf_op jit(solution)/shard_map/all_to_all | solution.py:68
  63.2 32.6 %all-to-all-done.1 = bf16[64,7,2176]{2,1,0:T(8,128)(2,1)S(1)} async-done(((bf16[64,7,2176]{2,1,0:T(8,128)(2,1)}), bf16[64,7,2176]{2,1,0:T(8,128)(2,1)S(1)}, u32[]{:S(2)}, u32[]{:S(2)}) %all-to-all-start.1) | async-done | bytes 1949728 | tf_op jit(solution)/shard_map/all_to_all | solution.py:68
  108.0 2.7 fusion.206
  121.7 2.9 fusion.40
  127.3 3.8 %fusion.9 = (bf16[2,224,1024]{2,1,0:T(8,128)(2,1)S(1)}, bf16[2,224,1024]{2,1,0:T(8,128)(2,1)S(1)}) fusion(f32[2,1024,224]{1,2,0:T(8,128)S(1)} %convolution_add_fusion.1, f32[2,224]{1,0:T(2,128)S(1)} %get-tuple-element.45, f32[2,224]{1,0:T(2,128)S(1)} %get-tuple-element.44, f32[2,1024,224]{1,2,0:T(8,128)S(1)} %fusion.40, ...), kind=kOutput, calls=%fused_computation.31 | convolution fusion | flops 1237705728 | bytes 7343616 | tf_op jit(solution)/shard_map/kn,anc->akc/dot_general | solution.py:39
  131.2 3.2 copy.112
  134.4 8.0 %all-to-all-start.2 = ((bf16[2,224,2048]{2,0,1:T(2,128)(2,1)}), bf16[2,224,2048]{2,0,1:T(2,128)(2,1)S(1)}, u32[]{:S(2)}, u32[]{:S(2)}) async-start(bf16[2,224,2048]{2,0,1:T(2,128)(2,1)} %copy.112), calls=%async_computation.2 | async-start | bytes 3670016 | tf_op jit(solution)/shard_map/all_to_all | solution.py:99
  146.3 27.3 %all-to-all-done.2 = bf16[2,224,2048]{2,0,1:T(2,128)(2,1)S(1)} async-done(((bf16[2,224,2048]{2,0,1:T(2,128)(2,1)}), bf16[2,224,2048]{2,0,1:T(2,128)(2,1)S(1)}, u32[]{:S(2)}, u32[]{:S(2)}) %all-to-all-start.2) | async-done | bytes 1835040 | tf_op jit(solution)/shard_map/all_to_all | solution.py:99
  173.7 2.8 copy.113
  176.4 4.6 %all_to_all.51 = bf16[64,7,2048]{2,0,1:T(8,128)(2,1)S(1)} reshape(bf16[32,2,7,2048]{3,1,0,2:T(2,128)(2,1)} %copy.113) | data formatting | bytes 3670016 | tf_op jit(solution)/shard_map/all_to_all | solution.py:99
  183.4 4.5 %all-to-all-start.3 = ((bf16[32,7,1024]{2,1,0:T(8,128)(2,1)}), bf16[32,7,1024]{2,1,0:T(8,128)(2,1)S(1)}, u32[]{:S(2)}, u32[]{:S(2)}) async-start(bf16[32,7,1024]{2,1,0:T(8,128)(2,1)} %copy.114), calls=%async_computation.3 | async-start | bytes 1048576 | tf_op jit(solution)/shard_map/all_to_all | solution.py:108
  190.4 9.1 %all-to-all-done.3 = bf16[32,7,1024]{2,1,0:T(8,128)(2,1)S(1)} async-done(((bf16[32,7,1024]{2,1,0:T(8,128)(2,1)}), bf16[32,7,1024]{2,1,0:T(8,128)(2,1)S(1)}, u32[]{:S(2)}, u32[]{:S(2)}) %all-to-all-start.3) | async-done | bytes 458784 | tf_op jit(solution)/shard_map/all_to_all | solution.py:108
  201.9 28.8 %shard_map.91 = (f32[672,1024]{1,0:T(8,128)S(1)}, f32[8,672,1]{2,1,0:T(8,128)}, f32[8,672,1]{2,1,0:T(8,128)}) custom-call(s32[2]{0:T(128)S(1)} %copy-done.2, bf16[672,1024]{1,0:T(8,128)(2,1)S(1)} %copy-done, bf16[1792,1024]{1,0:T(8,128)(2,1)} %all-gather.3.cloned.1.call-done.k_ref, bf16[1792,1024]{1,0:T(8,128)(2,1)} %all-gather.5.cloned.1.call-done.v_ref), custom_call_target="tpu_custom_call" | custom-call | flops 4932501504 | bytes 11468800 | tf_op jit(solution)/shard_map/pallas_call | solution.py:173
  230.7 4.3 %slice_reduce_fusion.4 = (f32[8,224]{1,0:T(8,128)S(1)}, f32[8,224]{1,0:T(8,128)S(1)}, f32[8,224]{1,0:T(8,128)S(1)}, f32[8,224]{1,0:T(8,128)S(1)}, f32[8,224]{1,0:T(8,128)S(1)}, /*index=5*/f32[8,224]{1,0:T(8,128)S(1)}) fusion(f32[8,672,1]{2,1,0:T(8,128)} %get-tuple-element.13, f32[8,672,1]{2,1,0:T(8,128)} %get-tuple-element.12), kind=kLoop, calls=%fused_computation.49 | loop fusion | bytes 86016 | tf_op jit(solution)/shard_map/slice | solution.py:222
  237.6 3.6 %collective-permute-start.5 = (f32[224,1040]{1,0:T(8,128)}, f32[224,1040]{1,0:T(8,128)}, u32[]{:S(2)}, u32[]{:S(2)}) collective-permute-start(f32[224,1040]{1,0:T(8,128)} %pad_maximum_fusion.4), channel_id=1, source_target_pairs={{0,96},{1,97},{2,98},{3,99},{4,100},{5,101},{6,102},{7,103},{8,104... | collective-permute-start | bytes 2795528 | tf_op jit(solution)/shard_map/ppermute | solution.py:224
  248.6 7.4 %fusion.24 = f32[224,4096]{1,0:T(8,128)} fusion(bf16[1024,4096]{1,0:T(8,128)(2,1)} %param.16, f32[224,1024]{1,0:T(8,128)S(1)} %copy-done.7, bf16[224,1024]{1,0:T(8,128)(2,1)S(1)} %copy-done.10), kind=kOutput, calls=%fused_computation.60 | convolution fusion | flops 1879736320 | bytes 13434880 | tf_op jit(solution)/shard_map/dot_general | solution.py:256
  256.0 8.3 %shard_map.92 = (f32[224,1024]{1,0:T(8,128)S(1)}, f32[8,224,1]{2,1,0:T(8,128)S(1)}, f32[8,224,1]{2,1,0:T(8,128)S(1)}) custom-call(s32[2]{0:T(128)S(1)} %pad_add_fusion.info_ref, bf16[224,1024]{1,0:T(8,128)(2,1)S(1)} %copy-done.1, bf16[1792,1024]{1,0:T(8,128)(2,1)} %all-gather.3.cloned.1.call-done.k_ref, bf16[1792,1024]{1,0:T(8,128)(2,1)} %all-gather.5.cloned.1.call-done.v_ref), custom_call_target="tpu_custom_call" | custom-call | flops 1644167168 | bytes 8716288 | tf_op jit(solution)/shard_map/pallas_call | solution.py:173
  267.1 15.2 %collective-permute-done.5 = f32[224,1040]{1,0:T(8,128)} collective-permute-done((f32[224,1040]{1,0:T(8,128)}, f32[224,1040]{1,0:T(8,128)}, u32[]{:S(2)}, u32[]{:S(2)}) %collective-permute-start.5) | collective-permute-done | bytes 931872 | tf_op jit(solution)/shard_map/ppermute | solution.py:224
  289.5 8.6 %fusion = bf16[224,4096]{1,0:T(8,128)(2,1)} fusion(f32[224,4096]{1,0:T(8,128)S(1)} %copy-done.3, bf16[1024,4096]{1,0:T(8,128)(2,1)} %param.17, f32[28,8,8,128]{3,2,1,0:T(8,128)S(1)} %bitcast.181, f32[224,1024]{1,0:T(8,128)S(1)} %get-tuple-element.15, f32[28,8,8,128]{3,2,1,0:T(8,128)S(1)} %bitcast.180, f32[28,8,8,128]{3,2,1,0:T(8,128)S(1)} %bitcast.179, ...), kind=kOutput, calls=%fused_computation.1 | convolution fusion | flops 1882947584 | bytes 22151168 | tf_op jit(solution)/shard_map/dot_general | solution.py:259
  298.2 30.9 %reduce-scatter.2.cloned.1.call-done = bf16[56,4096]{1,0:T(8,128)(2,1)} async-done(((bf16[224,4096]{1,0:T(8,128)(2,1)}), bf16[56,4096]{1,0:T(8,128)(2,1)}) %reduce-scatter.2.cloned.1.call-update) | async-done | bytes 458768 | tf_op jit(solution)/shard_map/reduce_scatter | solution.py:258
  (107 shorter events, 74.5 us)
Async XLA Ops:
  6.5 194.0 %all-gather.3.cloned.1.call-start = ((), (), s32[]{:S(2)}) async-start(), calls=%async_computation.5 | async-start | bytes 4128768 | tf_op jit(solution)/shard_map/all_gather | solution.py:207
  16.4 27.6 %all-to-all-start = ((bf16[32,2,3808]{2,1,0:T(2,128)(2,1)}), bf16[32,2,3808]{2,1,0:T(2,128)(2,1)S(1)}, u32[]{:S(2)}, u32[]{:S(2)}) async-start(bf16[32,2,3808]{2,1,0:T(2,128)(2,1)} %reshape.185), calls=%async_computation | async-start | bytes 983040 | tf_op jit(solution)/shard_map/all_to_all | solution.py:49
  57.8 38.0 %all-to-all-start.1 = ((bf16[64,7,2176]{2,1,0:T(8,128)(2,1)}), bf16[64,7,2176]{2,1,0:T(8,128)(2,1)S(1)}, u32[]{:S(2)}, u32[]{:S(2)}) async-start(bf16[64,7,2176]{2,1,0:T(8,128)(2,1)} %copy.102), calls=%async_computation.1 | async-start | bytes 4456448 | tf_op jit(solution)/shard_map/all_to_all | solution.py:68
  62.3 138.2 %all-gather.5.cloned.1.call-start = ((), (), s32[]{:S(2)}) async-start(), calls=%async_computation.6 | async-start | bytes 4128768 | tf_op jit(solution)/shard_map/all_gather | solution.py:208
  97.4 1.4 copy-start.4
  114.5 2.0 copy-start.5
  114.5 2.0 copy-start.6
  134.4 8.0 %copy-start.1 = (bf16[224,1024]{1,0:T(8,128)(2,1)S(1)}, bf16[224,1024]{1,0:T(8,128)(2,1)}, u32[]{:S(2)}) copy-start(bf16[224,1024]{1,0:T(8,128)(2,1)} %q_ref.1) | copy-start | bytes 1376260
  134.4 39.2 %all-to-all-start.2 = ((bf16[2,224,2048]{2,0,1:T(2,128)(2,1)}), bf16[2,224,2048]{2,0,1:T(2,128)(2,1)S(1)}, u32[]{:S(2)}, u32[]{:S(2)}) async-start(bf16[2,224,2048]{2,0,1:T(2,128)(2,1)} %copy.112), calls=%async_computation.2 | async-start | bytes 3670016 | tf_op jit(solution)/shard_map/all_to_all | solution.py:99
  142.4 45.6 %collective-permute-start = (bf16[224,1024]{1,0:T(8,128)(2,1)S(1)}, bf16[224,1024]{1,0:T(8,128)(2,1)S(1)}, u32[]{:S(2)}, u32[]{:S(2)}) collective-permute-start(bf16[224,1024]{1,0:T(8,128)(2,1)S(1)} %copy-done.1), channel_id=1, source_target_pairs={{32,0},{64,32},{96,64},{33,1},{65,33},{97,65},{34,2},{66,34},{98,6... | collective-permute-start | bytes 1376264 | tf_op jit(solution)/shard_map/ppermute | solution.py:214
  143.7 44.3 %collective-permute-start.1 = (bf16[224,1024]{1,0:T(8,128)(2,1)S(1)}, bf16[224,1024]{1,0:T(8,128)(2,1)S(1)}, u32[]{:S(2)}, u32[]{:S(2)}) collective-permute-start(bf16[224,1024]{1,0:T(8,128)(2,1)S(1)} %copy-done.1), channel_id=1, source_target_pairs={{64,0},{96,32},{65,1},{97,33},{66,2},{98,34},{67,3},{99,35},{68,4}... | collective-permute-start | bytes 1376264 | tf_op jit(solution)/shard_map/ppermute | solution.py:214
  145.0 43.0 %collective-permute-start.2 = (bf16[224,1024]{1,0:T(8,128)(2,1)S(1)}, bf16[224,1024]{1,0:T(8,128)(2,1)}, u32[]{:S(2)}, u32[]{:S(2)}) collective-permute-start(bf16[224,1024]{1,0:T(8,128)(2,1)S(1)} %copy-done.1), channel_id=1, source_target_pairs={{96,0},{97,1},{98,2},{99,3},{100,4},{101,5},{102,6},{103,7},{104,8... | collective-permute-start | bytes 1376264 | tf_op jit(solution)/shard_map/ppermute | solution.py:214
  183.4 16.1 %all-to-all-start.3 = ((bf16[32,7,1024]{2,1,0:T(8,128)(2,1)}), bf16[32,7,1024]{2,1,0:T(8,128)(2,1)S(1)}, u32[]{:S(2)}, u32[]{:S(2)}) async-start(bf16[32,7,1024]{2,1,0:T(8,128)(2,1)} %copy.114), calls=%async_computation.3 | async-start | bytes 1048576 | tf_op jit(solution)/shard_map/all_to_all | solution.py:108
  187.9 141.3 %reduce-scatter.2.cloned.1.call-start = ((), (), s32[]{:S(2)}) async-start(), calls=%async_computation.7 | async-start | bytes 2293760 | tf_op jit(solution)/shard_map/reduce_scatter | solution.py:258
  188.0 12.5 %copy-start.2 = (s32[2]{0:T(128)S(1)}, s32[2]{0:T(128)}, u32[]{:S(2)}) copy-start(s32[2]{0:T(128)} %constant.98.clone.1.info_ref) | copy-start | bytes 28
  200.5 1.3 copy-start
  236.6 4.8 %copy-start.9 = (f32[224,1024]{1,0:T(8,128)S(1)}, f32[224,1024]{1,0:T(8,128)}, u32[]{:S(2)}) copy-start(f32[224,1024]{1,0:T(8,128)} %get-tuple-element.33) | copy-start | bytes 2752516
  236.6 8.7 %copy-start.8 = (f32[224,1024]{1,0:T(8,128)S(1)}, f32[224,1024]{1,0:T(8,128)}, u32[]{:S(2)}) copy-start(f32[224,1024]{1,0:T(8,128)} %get-tuple-element.31) | copy-start | bytes 2752516
  237.6 44.7 %collective-permute-start.5 = (f32[224,1040]{1,0:T(8,128)}, f32[224,1040]{1,0:T(8,128)}, u32[]{:S(2)}, u32[]{:S(2)}) collective-permute-start(f32[224,1040]{1,0:T(8,128)} %pad_maximum_fusion.4), channel_id=1, source_target_pairs={{0,96},{1,97},{2,98},{3,99},{4,100},{5,101},{6,102},{7,103},{8,104... | collective-permute-start | bytes 2795528 | tf_op jit(solution)/shard_map/ppermute | solution.py:224
  241.4 7.2 %copy-start.7 = (f32[224,1024]{1,0:T(8,128)S(1)}, f32[224,1024]{1,0:T(8,128)}, u32[]{:S(2)}) copy-start(f32[224,1024]{1,0:T(8,128)} %reshape.173) | copy-start | bytes 2752516
  242.4 6.1 %copy-start.10 = (bf16[224,1024]{1,0:T(8,128)(2,1)S(1)}, bf16[224,1024]{1,0:T(8,128)(2,1)}, u32[]{:S(2)}) copy-start(bf16[224,1024]{1,0:T(8,128)(2,1)} %param.9) | copy-start | bytes 1376260
  242.4 40.8 %collective-permute-start.4 = (f32[224,1040]{1,0:T(8,128)}, f32[224,1040]{1,0:T(8,128)}, u32[]{:S(2)}, u32[]{:S(2)}) collective-permute-start(f32[224,1040]{1,0:T(8,128)} %pad_maximum_fusion.3), channel_id=1, source_target_pairs={{0,64},{32,96},{1,65},{33,97},{2,66},{34,98},{3,67},{35,99},{4,68}... | collective-permute-start | bytes 2795528 | tf_op jit(solution)/shard_map/ppermute | solution.py:224
  246.3 39.7 %collective-permute-start.3 = (f32[224,1040]{1,0:T(8,128)}, f32[224,1040]{1,0:T(8,128)}, u32[]{:S(2)}, u32[]{:S(2)}) collective-permute-start(f32[224,1040]{1,0:T(8,128)} %pad_maximum_fusion.2), channel_id=1, source_target_pairs={{0,32},{32,64},{64,96},{1,33},{33,65},{65,97},{2,34},{34,66},{66,9... | collective-permute-start | bytes 2795528 | tf_op jit(solution)/shard_map/ppermute | solution.py:224
  287.5 2.0 copy-start.3
Sparse Core Ops, SparseCore 0:
  9.6 94.3 all-gather.2
  106.3 88.1 all-gather.4
  298.3 30.7 reduce-scatter.1

commit v12 on v11

--- a/solution.py
+++ b/solution.py
@@ -213,6 +213,12 @@
     visiting = jnp.concatenate(
         [lax.ppermute(q_attn, "z", [(k, k - shift) for k in range(shift, quarters)]) for shift in shifts]
     )
+    needed = ((local_index + 1) * tok_rows + key_block - 1) // key_block
+    own_acc, own_max, own_total = flash_partial(
+        q_attn, key_part, value_part, local_index * tok_rows, needed, key_block
+    )
+    own_out, visiting = lax.optimization_barrier(((own_acc, own_max, own_total), visiting))
+    own_acc, own_max, own_total = own_out
     cross = flash_partial(
         visiting, key_part, value_part, jnp.int32(part_rows), jnp.int32(part_rows // key_block), key_block
     )
@@ -227,10 +233,6 @@
         back_stats = back[:, width:].T
         back_max = jnp.where(quarter >= shift, back_stats[:heads], neg_large)
         states.append((back[:, :width], back_max, back_stats[heads:]))
-    needed = ((local_index + 1) * tok_rows + key_block - 1) // key_block
-    own_acc, own_max, own_total = flash_partial(
-        q_attn, key_part, value_part, local_index * tok_rows, needed, key_block
-    )
     states.append((own_acc, own_max.reshape(heads, tok_rows), own_total.reshape(heads, tok_rows)))
     top = states[0][1]
     for state in states[1:]:

time: 342 us -> 352 us (1.029)
  Pallas kernels: 37.1 us -> 41.5 us
    ppermute x3, waiting for transfers between devices: 17.1 us -> 25.7 us  [attention(): lax.ppermute(jnp.concatenate([cross[0][rows], stats.T], axis=1), 'z', [(k...]
    pallas_call x2, Pallas kernels: 37.1 us -> 41.5 us  [flash_partial(): pl.pallas_call(kernel, out_shape=(jax.ShapeDtypeStruct((tok_rows, width),...]
    reduce_scatter x1, waiting for transfers between devices: 30.9 us -> 26.8 us  [local(): lax.psum_scatter((conv_part + jnp.dot(attended, w_attn_out, preferred_ele...]
    unnamed x28 -> x40, local copies, waits for them, and re-layouts: 7.76 us -> 9.45 us
  transfers between devices with their start and end apart: 13 -> 13, of which waited for: 7 -> 6; matrix products, arithmetic and copies ran while one was open for 25% -> 24% of each run, Pallas kernels for 2% -> 0%
where the time goes in v12:
time: 352 us; the launch traced here: 346 us
  waiting for transfers between devices  137 us (39%)
  local copies, waits for them, and re-layouts  52.4 us (15%)
  matrix products  46.8 us (13%)
  starting transfers between devices  42.6 us (12%)
  Pallas kernels  41.5 us (12%)
  between operations  14.1 us (4%)
  other arithmetic  11.5 us (3%)
    pallas_call x2, Pallas kernels, flash_partial(): pl.pallas_call(kernel, out_shape=(jax.ShapeDtypeStruct((tok_rows, width),...  41.5 us
    all_to_all x1, waiting for transfers between devices, spectral_conv(): lax.all_to_all(jnp.concatenate([source_re, source_im, filter_re, filter_i...  32.7 us
    reduce_scatter x1, waiting for transfers between devices, local(): lax.psum_scatter((conv_part + jnp.dot(attended, w_attn_out, preferred_ele...  26.8 us
    all_to_all x1, waiting for transfers between devices, spectral_conv(): lax.all_to_all(jnp.concatenate([turned_re, turned_im], axis=2).astype(jnp...  26.7 us
    ppermute x3, waiting for transfers between devices, attention(): lax.ppermute(jnp.concatenate([cross[0][rows], stats.T], axis=1), 'z', [(k...  25.7 us
    all_to_all x1, waiting for transfers between devices, spectral_conv(): lax.all_to_all(jnp.concatenate([gated, filters], axis=1).reshape(1, tok_r...  15.7 us
    all_to_all x1, starting transfers between devices, spectral_conv(): lax.all_to_all(jnp.concatenate([gated, filters], axis=1).reshape(1, tok_r...  11.5 us
    unnamed x40, local copies, waits for them, and re-layouts  9.45 us
  transfers between devices with their start and end apart: 13, of which 6 were waited for; matrix products, arithmetic and copies ran while one was open for 24% of the time, Pallas kernels for 0%

profile of v12, /device:TPU:1, one launch (start us, length us, event | category | flops | bytes accessed | tf_op | source)
XLA Modules:
  0.0 346.0 jit_solution(14363339840611634176)
XLA Ops:
  10.8 3.9 %reduce.14 = bf16[224,1088]{1,0:T(8,128)(2,1)S(1)} reduce(bf16[224,1,1088]{2,1,0:T(2,128)(2,1)S(1)} %bitcast.177, bf16[]{:T(256)} %broadcast.214), dimensions={1}, to_apply=%bitcast.170.reduce_sub_computation | reduce | bytes 974850
  16.4 11.5 %all-to-all-start = ((bf16[32,2,3808]{2,1,0:T(2,128)(2,1)}), bf16[32,2,3808]{2,1,0:T(2,128)(2,1)S(1)}, u32[]{:S(2)}, u32[]{:S(2)}) async-start(bf16[32,2,3808]{2,1,0:T(2,128)(2,1)} %reshape.185), calls=%async_computation | async-start | bytes 983040 | tf_op jit(solution)/shard_map/all_to_all | solution.py:49
  28.1 15.7 %all-to-all-done = bf16[32,2,3808]{2,1,0:T(2,128)(2,1)S(1)} async-done(((bf16[32,2,3808]{2,1,0:T(2,128)(2,1)}), bf16[32,2,3808]{2,1,0:T(2,128)(2,1)S(1)}, u32[]{:S(2)}, u32[]{:S(2)}) %all-to-all-start) | async-done | bytes 487456 | tf_op jit(solution)/shard_map/all_to_all | solution.py:49
  44.7 2.9 bitcast_reduce_fusion
  57.6 4.6 %all-to-all-start.1 = ((bf16[64,7,2176]{2,1,0:T(8,128)(2,1)}), bf16[64,7,2176]{2,1,0:T(8,128)(2,1)S(1)}, u32[]{:S(2)}, u32[]{:S(2)}) async-start(bf16[64,7,2176]{2,1,0:T(8,128)(2,1)} %copy.117), calls=%async_computation.1 | async-start | bytes 4456448 | tf_op jit(solution)/shard_map/all_to_all | solution.py:68
  63.1 32.7 %all-to-all-done.1 = bf16[64,7,2176]{2,1,0:T(8,128)(2,1)S(1)} async-done(((bf16[64,7,2176]{2,1,0:T(8,128)(2,1)}), bf16[64,7,2176]{2,1,0:T(8,128)(2,1)S(1)}, u32[]{:S(2)}, u32[]{:S(2)}) %all-to-all-start.1) | async-done | bytes 1949728 | tf_op jit(solution)/shard_map/all_to_all | solution.py:68
  108.4 2.7 fusion.206
  122.1 2.8 fusion.40
  127.6 3.8 %fusion.9 = (bf16[2,224,1024]{2,1,0:T(8,128)(2,1)S(1)}, bf16[2,224,1024]{2,1,0:T(8,128)(2,1)S(1)}) fusion(f32[2,1024,224]{1,2,0:T(8,128)S(1)} %convolution_add_fusion.1, f32[2,224]{1,0:T(2,128)S(1)} %get-tuple-element.53, f32[2,224]{1,0:T(2,128)S(1)} %get-tuple-element.52, f32[2,1024,224]{1,2,0:T(8,128)S(1)} %fusion.40, ...), kind=kOutput, calls=%fused_computation.31 | convolution fusion | flops 1237705728 | bytes 7343616 | tf_op jit(solution)/shard_map/kn,anc->akc/dot_general | solution.py:39
  131.6 3.2 copy.127
  134.8 7.8 %all-to-all-start.2 = ((bf16[2,224,2048]{2,0,1:T(2,128)(2,1)}), bf16[2,224,2048]{2,0,1:T(2,128)(2,1)S(1)}, u32[]{:S(2)}, u32[]{:S(2)}) async-start(bf16[2,224,2048]{2,0,1:T(2,128)(2,1)} %copy.127), calls=%async_computation.2 | async-start | bytes 3670016 | tf_op jit(solution)/shard_map/all_to_all | solution.py:99
  146.5 26.7 %all-to-all-done.2 = bf16[2,224,2048]{2,0,1:T(2,128)(2,1)S(1)} async-done(((bf16[2,224,2048]{2,0,1:T(2,128)(2,1)}), bf16[2,224,2048]{2,0,1:T(2,128)(2,1)S(1)}, u32[]{:S(2)}, u32[]{:S(2)}) %all-to-all-start.2) | async-done | bytes 1835040 | tf_op jit(solution)/shard_map/all_to_all | solution.py:99
  173.2 2.8 copy.128
  176.0 4.1 %all_to_all.51 = bf16[64,7,2048]{2,0,1:T(8,128)(2,1)S(1)} reshape(bf16[32,2,7,2048]{3,1,0,2:T(2,128)(2,1)} %copy.128) | data formatting | bytes 3670016 | tf_op jit(solution)/shard_map/all_to_all | solution.py:99
  182.4 5.6 %all-to-all-start.3 = ((bf16[32,7,1024]{2,1,0:T(8,128)(2,1)}), bf16[32,7,1024]{2,1,0:T(8,128)(2,1)S(1)}, u32[]{:S(2)}, u32[]{:S(2)}) async-start(bf16[32,7,1024]{2,1,0:T(8,128)(2,1)} %copy.129), calls=%async_computation.3 | async-start | bytes 1048576 | tf_op jit(solution)/shard_map/all_to_all | solution.py:108
  190.4 8.4 %all-to-all-done.3 = bf16[32,7,1024]{2,1,0:T(8,128)(2,1)S(1)} async-done(((bf16[32,7,1024]{2,1,0:T(8,128)(2,1)}), bf16[32,7,1024]{2,1,0:T(8,128)(2,1)S(1)}, u32[]{:S(2)}, u32[]{:S(2)}) %all-to-all-start.3) | async-done | bytes 458784 | tf_op jit(solution)/shard_map/all_to_all | solution.py:108
  199.9 8.3 %shard_map.91 = (f32[224,1024]{1,0:T(8,128)S(1)}, f32[8,224,1]{2,1,0:T(8,128)S(1)}, f32[8,224,1]{2,1,0:T(8,128)S(1)}) custom-call(s32[2]{0:T(128)S(1)} %pad_add_fusion.info_ref, bf16[224,1024]{1,0:T(8,128)(2,1)S(1)} %copy-done.7, bf16[1792,1024]{1,0:T(8,128)(2,1)} %all-gather.3.cloned.1.call-done.k_ref, bf16[1792,1024]{1,0:T(8,128)(2,1)} %all-gather.5.cloned.1.call-done.v_ref), custom_call_target="tpu_custom_call" | custom-call | flops 1644167168 | bytes 8716288 | tf_op jit(solution)/shard_map/pallas_call | solution.py:173
  211.2 33.3 %shard_map.92 = (f32[672,1024]{1,0:T(8,128)S(1)}, f32[8,672,1]{2,1,0:T(8,128)}, f32[8,672,1]{2,1,0:T(8,128)}) custom-call(s32[2]{0:T(128)S(1)} %copy-done.8, bf16[672,1024]{1,0:T(8,128)(2,1)S(1)} %copy-done, bf16[1792,1024]{1,0:T(8,128)(2,1)} %all-gather.3.cloned.1.call-done.k_ref, bf16[1792,1024]{1,0:T(8,128)(2,1)} %all-gather.5.cloned.1.call-done.v_ref), custom_call_target="tpu_custom_call" | custom-call | flops 4932501504 | bytes 11468800 | tf_op jit(solution)/shard_map/pallas_call | solution.py:173
  244.4 4.3 %slice_reduce_fusion.4 = (f32[8,224]{1,0:T(8,128)S(1)}, f32[8,224]{1,0:T(8,128)S(1)}, f32[8,224]{1,0:T(8,128)S(1)}, f32[8,224]{1,0:T(8,128)S(1)}, f32[8,224]{1,0:T(8,128)S(1)}, /*index=5*/f32[8,224]{1,0:T(8,128)S(1)}) fusion(f32[8,672,1]{2,1,0:T(8,128)} %get-tuple-element.21, f32[8,672,1]{2,1,0:T(8,128)} %get-tuple-element.20), kind=kLoop, calls=%fused_computation.49 | loop fusion | bytes 86016 | tf_op jit(solution)/shard_map/slice | solution.py:228
  251.3 4.0 %collective-permute-start.4 = (f32[224,1040]{1,0:T(8,128)}, f32[224,1040]{1,0:T(8,128)}, u32[]{:S(2)}, u32[]{:S(2)}) collective-permute-start(f32[224,1040]{1,0:T(8,128)} %pad_maximum_fusion.3), channel_id=1, source_target_pairs={{0,64},{32,96},{1,65},{33,97},{2,66},{34,98},{3,67},{35,99},{4,68}... | collective-permute-start | bytes 2795528 | tf_op jit(solution)/shard_map/ppermute | solution.py:230
  262.6 7.2 %fusion.24 = f32[224,4096]{1,0:T(8,128)} fusion(bf16[1024,4096]{1,0:T(8,128)(2,1)} %param.16, f32[224,1024]{1,0:T(8,128)S(1)} %copy-done.13, bf16[224,1024]{1,0:T(8,128)(2,1)S(1)} %copy-done.16), kind=kOutput, calls=%fused_computation.60 | convolution fusion | flops 1879736320 | bytes 13434880 | tf_op jit(solution)/shard_map/dot_general | solution.py:258
  273.5 25.7 %collective-permute-done.5 = f32[224,1040]{1,0:T(8,128)} collective-permute-done((f32[224,1040]{1,0:T(8,128)}, f32[224,1040]{1,0:T(8,128)}, u32[]{:S(2)}, u32[]{:S(2)}) %collective-permute-start.5) | collective-permute-done | bytes 931872 | tf_op jit(solution)/shard_map/ppermute | solution.py:230
  303.6 8.6 %fusion = bf16[224,4096]{1,0:T(8,128)(2,1)} fusion(f32[224,4096]{1,0:T(8,128)S(1)} %copy-done.9, bf16[1024,4096]{1,0:T(8,128)(2,1)} %param.17, f32[28,8,8,128]{3,2,1,0:T(8,128)S(1)} %bitcast.181, f32[224,1024]{1,0:T(8,128)S(1)} %copy-done.6, f32[28,8,8,128]{3,2,1,0:T(8,128)S(1)} %bitcast.180, f32[28,8,8,128]{3,2,1,0:T(8,128)S(1)} %bitcast.179, ...), kind=kOutput, calls=%fused_computation.1 | convolution fusion | flops 1882947584 | bytes 22151168 | tf_op jit(solution)/shard_map/dot_general | solution.py:261
  312.3 26.8 %reduce-scatter.2.cloned.1.call-done = bf16[56,4096]{1,0:T(8,128)(2,1)} async-done(((bf16[224,4096]{1,0:T(8,128)(2,1)}), bf16[56,4096]{1,0:T(8,128)(2,1)}) %reduce-scatter.2.cloned.1.call-update) | async-done | bytes 458768 | tf_op jit(solution)/shard_map/reduce_scatter | solution.py:260
  (119 shorter events, 74.4 us)
Async XLA Ops:
  6.5 193.4 %all-gather.3.cloned.1.call-start = ((), (), s32[]{:S(2)}) async-start(), calls=%async_computation.5 | async-start | bytes 4128768 | tf_op jit(solution)/shard_map/all_gather | solution.py:207
  16.4 27.4 %all-to-all-start = ((bf16[32,2,3808]{2,1,0:T(2,128)(2,1)}), bf16[32,2,3808]{2,1,0:T(2,128)(2,1)S(1)}, u32[]{:S(2)}, u32[]{:S(2)}) async-start(bf16[32,2,3808]{2,1,0:T(2,128)(2,1)} %reshape.185), calls=%async_computation | async-start | bytes 983040 | tf_op jit(solution)/shard_map/all_to_all | solution.py:49
  57.6 38.3 %all-to-all-start.1 = ((bf16[64,7,2176]{2,1,0:T(8,128)(2,1)}), bf16[64,7,2176]{2,1,0:T(8,128)(2,1)S(1)}, u32[]{:S(2)}, u32[]{:S(2)}) async-start(bf16[64,7,2176]{2,1,0:T(8,128)(2,1)} %copy.117), calls=%async_computation.1 | async-start | bytes 4456448 | tf_op jit(solution)/shard_map/all_to_all | solution.py:68
  62.2 137.7 %all-gather.5.cloned.1.call-start = ((), (), s32[]{:S(2)}) async-start(), calls=%async_computation.6 | async-start | bytes 4128768 | tf_op jit(solution)/shard_map/all_gather | solution.py:208
  114.8 2.1 copy-start.12
  134.8 7.9 %copy-start.7 = (bf16[224,1024]{1,0:T(8,128)(2,1)S(1)}, bf16[224,1024]{1,0:T(8,128)(2,1)}, u32[]{:S(2)}) copy-start(bf16[224,1024]{1,0:T(8,128)(2,1)} %q_ref.1) | copy-start | bytes 1376260
  134.8 38.4 %all-to-all-start.2 = ((bf16[2,224,2048]{2,0,1:T(2,128)(2,1)}), bf16[2,224,2048]{2,0,1:T(2,128)(2,1)S(1)}, u32[]{:S(2)}, u32[]{:S(2)}) async-start(bf16[2,224,2048]{2,0,1:T(2,128)(2,1)} %copy.127), calls=%async_computation.2 | async-start | bytes 3670016 | tf_op jit(solution)/shard_map/all_to_all | solution.py:99
  142.6 45.5 %collective-permute-start = (bf16[224,1024]{1,0:T(8,128)(2,1)S(1)}, bf16[224,1024]{1,0:T(8,128)(2,1)S(1)}, u32[]{:S(2)}, u32[]{:S(2)}) collective-permute-start(bf16[224,1024]{1,0:T(8,128)(2,1)S(1)} %copy-done.7), channel_id=1, source_target_pairs={{32,0},{64,32},{96,64},{33,1},{65,33},{97,65},{34,2},{66,34},{98,6... | collective-permute-start | bytes 1376264 | tf_op jit(solution)/shard_map/ppermute | solution.py:214
  143.9 44.2 %collective-permute-start.1 = (bf16[224,1024]{1,0:T(8,128)(2,1)S(1)}, bf16[224,1024]{1,0:T(8,128)(2,1)S(1)}, u32[]{:S(2)}, u32[]{:S(2)}) collective-permute-start(bf16[224,1024]{1,0:T(8,128)(2,1)S(1)} %copy-done.7), channel_id=1, source_target_pairs={{64,0},{96,32},{65,1},{97,33},{66,2},{98,34},{67,3},{99,35},{68,4}... | collective-permute-start | bytes 1376264 | tf_op jit(solution)/shard_map/ppermute | solution.py:214
  145.2 42.9 %collective-permute-start.2 = (bf16[224,1024]{1,0:T(8,128)(2,1)S(1)}, bf16[224,1024]{1,0:T(8,128)(2,1)}, u32[]{:S(2)}, u32[]{:S(2)}) collective-permute-start(bf16[224,1024]{1,0:T(8,128)(2,1)S(1)} %copy-done.7), channel_id=1, source_target_pairs={{96,0},{97,1},{98,2},{99,3},{100,4},{101,5},{102,6},{103,7},{104,8... | collective-permute-start | bytes 1376264 | tf_op jit(solution)/shard_map/ppermute | solution.py:214
  182.4 16.4 %all-to-all-start.3 = ((bf16[32,7,1024]{2,1,0:T(8,128)(2,1)}), bf16[32,7,1024]{2,1,0:T(8,128)(2,1)S(1)}, u32[]{:S(2)}, u32[]{:S(2)}) async-start(bf16[32,7,1024]{2,1,0:T(8,128)(2,1)} %copy.129), calls=%async_computation.3 | async-start | bytes 1048576 | tf_op jit(solution)/shard_map/all_to_all | solution.py:108
  188.0 151.1 %reduce-scatter.2.cloned.1.call-start = ((), (), s32[]{:S(2)}) async-start(), calls=%async_computation.7 | async-start | bytes 2293760 | tf_op jit(solution)/shard_map/reduce_scatter | solution.py:260
  199.9 9.2 %copy-start.8 = (s32[2]{0:T(128)S(1)}, s32[2]{0:T(128)}, u32[]{:S(2)}) copy-start(s32[2]{0:T(128)} %constant.98.clone.1.info_ref) | copy-start | bytes 28
  209.2 35.3 %copy-start.1 = (f32[8,224,1]{2,1,0:T(8,128)}, f32[8,224,1]{2,1,0:T(8,128)S(1)}, u32[]{:S(2)}) copy-start(f32[8,224,1]{2,1,0:T(8,128)S(1)} %get-tuple-element.24) | copy-start | bytes 21508
  209.2 35.3 %copy-start.3 = (f32[8,224,1]{2,1,0:T(8,128)}, f32[8,224,1]{2,1,0:T(8,128)S(1)}, u32[]{:S(2)}) copy-start(f32[8,224,1]{2,1,0:T(8,128)S(1)} %get-tuple-element.22) | copy-start | bytes 21508
  250.3 5.2 %copy-start.15 = (f32[224,1024]{1,0:T(8,128)S(1)}, f32[224,1024]{1,0:T(8,128)}, u32[]{:S(2)}) copy-start(f32[224,1024]{1,0:T(8,128)} %get-tuple-element.40) | copy-start | bytes 2752516
  250.3 8.7 %copy-start.14 = (f32[224,1024]{1,0:T(8,128)S(1)}, f32[224,1024]{1,0:T(8,128)}, u32[]{:S(2)}) copy-start(f32[224,1024]{1,0:T(8,128)} %get-tuple-element.39) | copy-start | bytes 2752516
  251.3 21.3 %collective-permute-start.4 = (f32[224,1040]{1,0:T(8,128)}, f32[224,1040]{1,0:T(8,128)}, u32[]{:S(2)}, u32[]{:S(2)}) collective-permute-start(f32[224,1040]{1,0:T(8,128)} %pad_maximum_fusion.3), channel_id=1, source_target_pairs={{0,64},{32,96},{1,65},{33,97},{2,66},{34,98},{3,67},{35,99},{4,68}... | collective-permute-start | bytes 2795528 | tf_op jit(solution)/shard_map/ppermute | solution.py:230
  255.5 7.1 %copy-start.13 = (f32[224,1024]{1,0:T(8,128)S(1)}, f32[224,1024]{1,0:T(8,128)}, u32[]{:S(2)}) copy-start(f32[224,1024]{1,0:T(8,128)} %reshape.173) | copy-start | bytes 2752516
  255.5 7.1 %copy-start.16 = (bf16[224,1024]{1,0:T(8,128)(2,1)S(1)}, bf16[224,1024]{1,0:T(8,128)(2,1)}, u32[]{:S(2)}) copy-start(bf16[224,1024]{1,0:T(8,128)(2,1)} %param.9) | copy-start | bytes 1376260
  256.6 42.6 %collective-permute-start.5 = (f32[224,1040]{1,0:T(8,128)}, f32[224,1040]{1,0:T(8,128)}, u32[]{:S(2)}, u32[]{:S(2)}) collective-permute-start(f32[224,1040]{1,0:T(8,128)} %pad_maximum_fusion.4), channel_id=1, source_target_pairs={{0,96},{1,97},{2,98},{3,99},{4,100},{5,101},{6,102},{7,103},{8,104... | collective-permute-start | bytes 2795528 | tf_op jit(solution)/shard_map/ppermute | solution.py:230
  260.0 9.8 %copy-start.4 = (f32[8,224,1]{2,1,0:T(8,128)S(1)}, f32[8,224,1]{2,1,0:T(8,128)}, u32[]{:S(2)}) copy-start(f32[8,224,1]{2,1,0:T(8,128)} %copy-done.3) | copy-start | bytes 21508
  260.0 11.2 %copy-start.2 = (f32[8,224,1]{2,1,0:T(8,128)S(1)}, f32[8,224,1]{2,1,0:T(8,128)}, u32[]{:S(2)}) copy-start(f32[8,224,1]{2,1,0:T(8,128)} %copy-done.1) | copy-start | bytes 21508
  260.0 40.1 %collective-permute-start.3 = (f32[224,1040]{1,0:T(8,128)}, f32[224,1040]{1,0:T(8,128)}, u32[]{:S(2)}, u32[]{:S(2)}) collective-permute-start(f32[224,1040]{1,0:T(8,128)} %pad_maximum_fusion.2), channel_id=1, source_target_pairs={{0,32},{32,64},{64,96},{1,33},{33,65},{65,97},{2,34},{34,66},{66,9... | collective-permute-start | bytes 2795528 | tf_op jit(solution)/shard_map/ppermute | solution.py:230
  (6 other events, 10.4 us)
Sparse Core Ops, SparseCore 0:
  9.6 95.2 all-gather.2
  107.3 86.2 all-gather.4
  312.4 26.6 reduce-scatter.1

commit v13 on v7

--- a/solution.py
+++ b/solution.py
@@ -246,14 +246,16 @@
     gated = (k_conv.astype(jnp.float32) * v_conv.astype(jnp.float32)).astype(jnp.bfloat16)
     conv = spectral_conv(gated, conv_filter, my_index, tok_rows, count_ctx)
     mixed = (q_conv.astype(jnp.float32) * conv.astype(jnp.float32)).astype(jnp.bfloat16)
-    conv_part = jnp.dot(mixed, w_conv_out, preferred_element_type=jnp.float32)
     attended = attention(q_attn, k_attn, v_attn, tok_rows)
-    return lax.psum_scatter(
-        (conv_part + jnp.dot(attended, w_attn_out, preferred_element_type=jnp.float32)).astype(jnp.bfloat16),
-        "ch",
-        scatter_dimension=0,
-        tiled=True,
-    )
+    half = w_conv_out.shape[1] // 2
+    outs = []
+    for cols in (slice(0, half), slice(half, 2 * half)):
+        part = (
+            jnp.dot(mixed, w_conv_out[:, cols], preferred_element_type=jnp.float32)
+            + jnp.dot(attended, w_attn_out[:, cols], preferred_element_type=jnp.float32)
+        ).astype(jnp.bfloat16)
+        outs.append(lax.psum_scatter(part, "ch", scatter_dimension=0, tiled=True))
+    return jnp.concatenate(outs, axis=1)
 
 
 def solution(mesh):

time: 333 us -> 379 us (1.14)
  waiting for transfers between devices: 90.6 us -> 160 us
  blocking collectives: 38.7 us -> 0 us
  starting transfers between devices: 39.8 us -> 50.8 us
  matrix products: 49.6 us -> 44.1 us
  other arithmetic: 9.69 us -> 14.7 us
  local copies, waits for them, and re-layouts: 37.6 us -> 41.6 us
    all_to_all x1 -> x0, blocking collectives: 38.7 us -> none  [spectral_conv(): lax.all_to_all(jnp.concatenate([turned_re, turned_im], axis=2).astype(jnp...]
    all_to_all x0 -> x1, waiting for transfers between devices: none -> 28.3 us  [spectral_conv(): lax.all_to_all(jnp.concatenate([turned_re, turned_im], axis=2).astype(jnp...]
    ppermute x6, waiting for transfers between devices: 5.3 us -> 30.7 us  [attention(): lax.ppermute((cross[0], stats), 'z', [(k - shift, k) for k in range(shift...]
    reduce_scatter x1 -> x2, waiting for transfers between devices: 27.7 us -> 38.3 us  [local(): outs.append(lax.psum_scatter(part, 'ch', scatter_dimension=0, tiled=True))]
    all_to_all x0 -> x1, starting transfers between devices: none -> 7.73 us  [spectral_conv(): lax.all_to_all(jnp.concatenate([turned_re, turned_im], axis=2).astype(jnp...]
    ppermute x3, waiting for transfers between devices: 0.01 us -> 4.67 us  [attention(): lax.ppermute(q_attn, 'z', [(k, k - shift) for k in range(shift, quarters)])]
    dot_general x2 -> x4, matrix products: 16 us -> 13.2 us  [the longest x2 6.71 us: local(): jnp.dot(attended, w_attn_out[:, cols], preferred_element_type=jnp.float32)]
    unnamed x30 -> x28, local copies, waits for them, and re-layouts: 8.92 us -> 7.24 us
  transfers between devices with their start and end apart: 15 -> 17, of which waited for: 5 -> 8; matrix products, arithmetic and copies ran while one was open for 24% -> 22% of each run, Pallas kernels for 14% -> 13%
where the time goes in v13:
time: 379 us; the launch traced here: 373 us
  waiting for transfers between devices  160 us (42%)
  starting transfers between devices  50.8 us (13%)
  Pallas kernels  48.1 us (13%)
  matrix products  44.1 us (12%)
  local copies, waits for them, and re-layouts  41.6 us (11%)
  other arithmetic  14.7 us (4%)
  between operations  14.1 us (4%)
    pallas_call x4, Pallas kernels, flash_partial(): pl.pallas_call(kernel, out_shape=(jax.ShapeDtypeStruct((tok_rows, width),...  48.1 us
    reduce_scatter x2, waiting for transfers between devices, local(): outs.append(lax.psum_scatter(part, 'ch', scatter_dimension=0, tiled=True))  38.3 us
    all_to_all x1, waiting for transfers between devices, spectral_conv(): lax.all_to_all(jnp.concatenate([source_re, source_im, filter_re, filter_i...  32.7 us
    ppermute x6, waiting for transfers between devices, attention(): lax.ppermute((cross[0], stats), 'z', [(k - shift, k) for k in range(shift...  30.7 us
    all_to_all x1, waiting for transfers between devices, spectral_conv(): lax.all_to_all(jnp.concatenate([turned_re, turned_im], axis=2).astype(jnp...  28.3 us
    ppermute x6, starting transfers between devices, attention(): lax.ppermute((cross[0], stats), 'z', [(k - shift, k) for k in range(shift...  16.1 us
    all_to_all x1, waiting for transfers between devices, spectral_conv(): lax.all_to_all(jnp.concatenate([gated, filters], axis=1).reshape(1, tok_r...  15.7 us
    all_to_all x1, starting transfers between devices, spectral_conv(): lax.all_to_all(jnp.concatenate([gated, filters], axis=1).reshape(1, tok_r...  11.5 us
  transfers between devices with their start and end apart: 17, of which 8 were waited for; matrix products, arithmetic and copies ran while one was open for 22% of the time, Pallas kernels for 13%

profile of v13, /device:TPU:1, one launch (start us, length us, event | category | flops | bytes accessed | tf_op | source)
XLA Modules:
  0.0 373.0 jit_solution(5522706810410347288)
XLA Ops:
  10.8 3.9 %reduce.10 = bf16[224,1088]{1,0:T(8,128)(2,1)S(1)} reduce(bf16[224,1,1088]{2,1,0:T(2,128)(2,1)S(1)} %bitcast.147, bf16[]{:T(256)} %broadcast.216), dimensions={1}, to_apply=%bitcast.140.reduce_sub_computation | reduce | bytes 974850
  16.4 11.5 %all-to-all-start = ((bf16[32,2,3808]{2,1,0:T(2,128)(2,1)}), bf16[32,2,3808]{2,1,0:T(2,128)(2,1)S(1)}, u32[]{:S(2)}, u32[]{:S(2)}) async-start(bf16[32,2,3808]{2,1,0:T(2,128)(2,1)} %reshape.187), calls=%async_computation | async-start | bytes 983040 | tf_op jit(solution)/shard_map/all_to_all | solution.py:49
  28.1 15.7 %all-to-all-done = bf16[32,2,3808]{2,1,0:T(2,128)(2,1)S(1)} async-done(((bf16[32,2,3808]{2,1,0:T(2,128)(2,1)}), bf16[32,2,3808]{2,1,0:T(2,128)(2,1)S(1)}, u32[]{:S(2)}, u32[]{:S(2)}) %all-to-all-start) | async-done | bytes 487456 | tf_op jit(solution)/shard_map/all_to_all | solution.py:49
  57.6 4.6 %all-to-all-start.1 = ((bf16[64,7,2176]{2,1,0:T(8,128)(2,1)}), bf16[64,7,2176]{2,1,0:T(8,128)(2,1)S(1)}, u32[]{:S(2)}, u32[]{:S(2)}) async-start(bf16[64,7,2176]{2,1,0:T(8,128)(2,1)} %copy.69), calls=%async_computation.1 | async-start | bytes 4456448 | tf_op jit(solution)/shard_map/all_to_all | solution.py:68
  63.1 32.7 %all-to-all-done.1 = bf16[64,7,2176]{2,1,0:T(8,128)(2,1)S(1)} async-done(((bf16[64,7,2176]{2,1,0:T(8,128)(2,1)}), bf16[64,7,2176]{2,1,0:T(8,128)(2,1)S(1)}, u32[]{:S(2)}, u32[]{:S(2)}) %all-to-all-start.1) | async-done | bytes 1949728 | tf_op jit(solution)/shard_map/all_to_all | solution.py:68
  128.6 3.8 %fusion.28 = (bf16[2,224,1024]{2,1,0:T(8,128)(2,1)S(1)}, bf16[2,224,1024]{2,1,0:T(8,128)(2,1)S(1)}) fusion(f32[2,1024,224]{1,2,0:T(8,128)S(1)} %convolution_add_fusion, f32[2,224]{1,0:T(2,128)S(1)} %get-tuple-element.48, f32[2,224]{1,0:T(2,128)S(1)} %get-tuple-element.47, f32[2,1024,224]{1,2,0:T(8,128)S(1)} %fusion.57, ...), kind=kOutput, calls=%fused_computation.37 | convolution fusion | flops 1237705728 | bytes 7343616 | tf_op jit(solution)/shard_map/kn,anc->akc/dot_general | solution.py:39
  132.6 3.2 copy.79
  135.8 7.7 %all-to-all-start.2 = ((bf16[2,224,2048]{2,0,1:T(2,128)(2,1)}), bf16[2,224,2048]{2,0,1:T(2,128)(2,1)S(1)}, u32[]{:S(2)}, u32[]{:S(2)}) async-start(bf16[2,224,2048]{2,0,1:T(2,128)(2,1)} %copy.79), calls=%async_computation.2 | async-start | bytes 3670016 | tf_op jit(solution)/shard_map/all_to_all | solution.py:99
  144.8 28.3 %all-to-all-done.2 = bf16[2,224,2048]{2,0,1:T(2,128)(2,1)S(1)} async-done(((bf16[2,224,2048]{2,0,1:T(2,128)(2,1)}), bf16[2,224,2048]{2,0,1:T(2,128)(2,1)S(1)}, u32[]{:S(2)}, u32[]{:S(2)}) %all-to-all-start.2) | async-done | bytes 1835040 | tf_op jit(solution)/shard_map/all_to_all | solution.py:99
  175.9 4.3 %all_to_all.51 = bf16[64,7,2048]{2,0,1:T(8,128)(2,1)S(1)} reshape(bf16[32,2,7,2048]{3,1,0,2:T(2,128)(2,1)} %copy.80) | data formatting | bytes 3670016 | tf_op jit(solution)/shard_map/all_to_all | solution.py:99
  182.5 6.6 %all-to-all-start.3 = ((bf16[32,7,1024]{2,1,0:T(8,128)(2,1)}), bf16[32,7,1024]{2,1,0:T(8,128)(2,1)S(1)}, u32[]{:S(2)}, u32[]{:S(2)}) async-start(bf16[32,7,1024]{2,1,0:T(8,128)(2,1)} %copy.81), calls=%async_computation.3 | async-start | bytes 1048576 | tf_op jit(solution)/shard_map/all_to_all | solution.py:108
  191.9 8.0 %all-to-all-done.3 = bf16[32,7,1024]{2,1,0:T(8,128)(2,1)S(1)} async-done(((bf16[32,7,1024]{2,1,0:T(8,128)(2,1)}), bf16[32,7,1024]{2,1,0:T(8,128)(2,1)S(1)}, u32[]{:S(2)}, u32[]{:S(2)}) %all-to-all-start.3) | async-done | bytes 458784 | tf_op jit(solution)/shard_map/all_to_all | solution.py:108
  201.0 13.1 %shard_map.91 = (f32[224,1024]{1,0:T(8,128)}, f32[8,224,1]{2,1,0:T(8,128)S(1)}, f32[8,224,1]{2,1,0:T(8,128)S(1)}) custom-call(s32[2]{0:T(128)S(1)} %copy-done.4, bf16[224,1024]{1,0:T(8,128)(2,1)S(1)} %collective-permute-done.q_ref, bf16[1792,1024]{1,0:T(8,128)(2,1)} %all-gather.3.cloned.1.call-done.k_ref, bf16[1792,1024]{1,0:T(8,128)(2,1)} %all-gather.5.cloned.1.call-done.v_ref), custom_call_target="tpu_custom_call" | custom-call | flops 1644167168 | bytes 8716288 | tf_op jit(solution)/shard_map/pallas_call | solution.py:173
  214.8 4.7 %collective-permute-done.5.q_ref = bf16[224,1024]{1,0:T(8,128)(2,1)S(1)} collective-permute-done((bf16[224,1024]{1,0:T(8,128)(2,1)S(1)}, bf16[224,1024]{1,0:T(8,128)(2,1)S(1)}, u32[]{:S(2)}, u32[]{:S(2)}) %collective-permute-start.5) | collective-permute-done | bytes 458784 | tf_op jit(solution)/shard_map/ppermute | solution.py:213
  221.2 13.4 %shard_map.93 = (f32[224,1024]{1,0:T(8,128)}, f32[8,224,1]{2,1,0:T(8,128)S(1)}, f32[8,224,1]{2,1,0:T(8,128)S(1)}) custom-call(s32[2]{0:T(128)S(1)} %copy-done.4, bf16[224,1024]{1,0:T(8,128)(2,1)S(1)} %copy-done.3, bf16[1792,1024]{1,0:T(8,128)(2,1)} %all-gather.3.cloned.1.call-done.k_ref, bf16[1792,1024]{1,0:T(8,128)(2,1)} %all-gather.5.cloned.1.call-done.v_ref), custom_call_target="tpu_custom_call" | custom-call | flops 1644167168 | bytes 8716288 | tf_op jit(solution)/shard_map/pallas_call | solution.py:173
  236.9 13.3 %shard_map.92 = (f32[224,1024]{1,0:T(8,128)}, f32[8,224,1]{2,1,0:T(8,128)S(1)}, f32[8,224,1]{2,1,0:T(8,128)S(1)}) custom-call(s32[2]{0:T(128)S(1)} %copy-done.4, bf16[224,1024]{1,0:T(8,128)(2,1)} %collective-permute-done.3.q_ref, bf16[1792,1024]{1,0:T(8,128)(2,1)} %all-gather.3.cloned.1.call-done.k_ref, bf16[1792,1024]{1,0:T(8,128)(2,1)} %all-gather.5.cloned.1.call-done.v_ref), custom_call_target="tpu_custom_call" | custom-call | flops 1644167168 | bytes 8716288 | tf_op jit(solution)/shard_map/pallas_call | solution.py:173
  260.9 30.7 %collective-permute-done.2 = f32[16,224]{1,0:T(8,128)S(1)} collective-permute-done((f32[16,224]{1,0:T(8,128)S(1)}, f32[16,224]{1,0:T(8,128)S(1)}, u32[]{:S(2)}, u32[]{:S(2)}) %collective-permute-start.2) | collective-permute-done | bytes 14368 | tf_op jit(solution)/shard_map/ppermute | solution.py:218
  291.6 6.7 %collective-permute-start.4 = (f32[16,224]{1,0:T(8,128)S(1)}, f32[16,224]{1,0:T(8,128)S(1)}, u32[]{:S(2)}, u32[]{:S(2)}) collective-permute-start(f32[16,224]{1,0:T(8,128)S(1)} %pad_maximum_fusion.3), channel_id=1, source_target_pairs={{0,64},{32,96},{1,65},{33,97},{2,66},{34,98},{3,67},{35,99},{4,68}... | collective-permute-start | bytes 43016 | tf_op jit(solution)/shard_map/ppermute | solution.py:218
  298.3 8.3 %shard_map.94 = (f32[224,1024]{1,0:T(8,128)S(1)}, f32[8,224,1]{2,1,0:T(8,128)S(1)}, f32[8,224,1]{2,1,0:T(8,128)S(1)}) custom-call(s32[2]{0:T(128)S(1)} %pad_add_fusion.info_ref, bf16[224,1024]{1,0:T(8,128)(2,1)S(1)} %copy-done.1, bf16[1792,1024]{1,0:T(8,128)(2,1)} %all-gather.3.cloned.1.call-done.k_ref, bf16[1792,1024]{1,0:T(8,128)(2,1)} %all-gather.5.cloned.1.call-done.v_ref), custom_call_target="tpu_custom_call" | custom-call | flops 1644167168 | bytes 8716288 | tf_op jit(solution)/shard_map/pallas_call | solution.py:173
  312.7 3.4 fusion
  318.4 3.3 fusion.4
  321.7 4.3 %fusion.17 = bf16[224,2048]{1,0:T(8,128)(2,1)} fusion(f32[224,2048]{1,0:T(8,128)S(1)} %fusion.4, bf16[1024,4096]{1,0:T(8,128)(2,1)} %param.16, f32[224,1024]{1,0:T(8,128)S(1)} %copy-done.5, bf16[224,1024]{1,0:T(8,128)(2,1)S(1)} %copy-done.8), kind=kOutput, calls=%fused_computation.11 | convolution fusion | flops 941129728 | bytes 8323072 | tf_op jit(solution)/shard_map/dot_general | solution.py:254
  326.0 15.2 %reduce-scatter.5.cloned.1.call-done = bf16[56,2048]{1,0:T(8,128)(2,1)} async-done(((bf16[224,2048]{1,0:T(8,128)(2,1)}), bf16[56,2048]{1,0:T(8,128)(2,1)}) %reduce-scatter.5.cloned.1.call-update) | async-done | bytes 229392 | tf_op jit(solution)/shard_map/reduce_scatter | solution.py:257
  341.2 23.1 %reduce-scatter.3.cloned.1.call-done = bf16[56,2048]{1,0:T(8,128)(2,1)} async-done(((bf16[224,2048]{1,0:T(8,128)(2,1)}), bf16[56,2048]{1,0:T(8,128)(2,1)}) %reduce-scatter.3.cloned.1.call-update) | async-done | bytes 229392 | tf_op jit(solution)/shard_map/reduce_scatter | solution.py:257
  (122 shorter events, 89.0 us)
Async XLA Ops:
  6.5 194.5 %all-gather.3.cloned.1.call-start = ((), (), s32[]{:S(2)}) async-start(), calls=%async_computation.6 | async-start | bytes 4128768 | tf_op jit(solution)/shard_map/all_gather | solution.py:207
  16.4 27.4 %all-to-all-start = ((bf16[32,2,3808]{2,1,0:T(2,128)(2,1)}), bf16[32,2,3808]{2,1,0:T(2,128)(2,1)S(1)}, u32[]{:S(2)}, u32[]{:S(2)}) async-start(bf16[32,2,3808]{2,1,0:T(2,128)(2,1)} %reshape.187), calls=%async_computation | async-start | bytes 983040 | tf_op jit(solution)/shard_map/all_to_all | solution.py:49
  57.6 38.3 %all-to-all-start.1 = ((bf16[64,7,2176]{2,1,0:T(8,128)(2,1)}), bf16[64,7,2176]{2,1,0:T(8,128)(2,1)S(1)}, u32[]{:S(2)}, u32[]{:S(2)}) async-start(bf16[64,7,2176]{2,1,0:T(8,128)(2,1)} %copy.69), calls=%async_computation.1 | async-start | bytes 4456448 | tf_op jit(solution)/shard_map/all_to_all | solution.py:68
  62.2 138.8 %all-gather.5.cloned.1.call-start = ((), (), s32[]{:S(2)}) async-start(), calls=%async_computation.7 | async-start | bytes 4128768 | tf_op jit(solution)/shard_map/all_gather | solution.py:208
  115.6 2.3 copy-start.7
  135.8 7.7 %copy-start.1 = (bf16[224,1024]{1,0:T(8,128)(2,1)S(1)}, bf16[224,1024]{1,0:T(8,128)(2,1)}, u32[]{:S(2)}) copy-start(bf16[224,1024]{1,0:T(8,128)(2,1)} %q_ref.1) | copy-start | bytes 1376260
  135.8 37.4 %all-to-all-start.2 = ((bf16[2,224,2048]{2,0,1:T(2,128)(2,1)}), bf16[2,224,2048]{2,0,1:T(2,128)(2,1)S(1)}, u32[]{:S(2)}, u32[]{:S(2)}) async-start(bf16[2,224,2048]{2,0,1:T(2,128)(2,1)} %copy.79), calls=%async_computation.2 | async-start | bytes 3670016 | tf_op jit(solution)/shard_map/all_to_all | solution.py:99
  143.5 57.5 %collective-permute-start = (bf16[224,1024]{1,0:T(8,128)(2,1)S(1)}, bf16[224,1024]{1,0:T(8,128)(2,1)S(1)}, u32[]{:S(2)}, u32[]{:S(2)}) collective-permute-start(bf16[224,1024]{1,0:T(8,128)(2,1)S(1)} %copy-done.1), channel_id=1, source_target_pairs={{32,0},{64,32},{96,64},{33,1},{65,33},{97,65},{34,2},{66,34},{98,6... | collective-permute-start | bytes 1376264 | tf_op jit(solution)/shard_map/ppermute | solution.py:213
  181.4 19.6 %copy-start.4 = (s32[2]{0:T(128)S(1)}, s32[2]{0:T(128)}, u32[]{:S(2)}) copy-start(s32[2]{0:T(128)} %constant.98.clone.1.info_ref) | copy-start | bytes 28
  182.5 17.4 %all-to-all-start.3 = ((bf16[32,7,1024]{2,1,0:T(8,128)(2,1)}), bf16[32,7,1024]{2,1,0:T(8,128)(2,1)S(1)}, u32[]{:S(2)}, u32[]{:S(2)}) async-start(bf16[32,7,1024]{2,1,0:T(8,128)(2,1)} %copy.81), calls=%async_computation.3 | async-start | bytes 1048576 | tf_op jit(solution)/shard_map/all_to_all | solution.py:108
  189.2 152.1 %reduce-scatter.5.cloned.1.call-start = ((), (), s32[]{:S(2)}) async-start(), calls=%async_computation.9 | async-start | bytes 1146880 | tf_op jit(solution)/shard_map/reduce_scatter | solution.py:257
  189.2 30.3 %collective-permute-start.5 = (bf16[224,1024]{1,0:T(8,128)(2,1)S(1)}, bf16[224,1024]{1,0:T(8,128)(2,1)S(1)}, u32[]{:S(2)}, u32[]{:S(2)}) collective-permute-start(bf16[224,1024]{1,0:T(8,128)(2,1)S(1)} %copy-done.1), channel_id=1, source_target_pairs={{96,0},{97,1},{98,2},{99,3},{100,4},{101,5},{102,6},{103,7},{104,8... | collective-permute-start | bytes 1376264 | tf_op jit(solution)/shard_map/ppermute | solution.py:213
  190.5 46.4 %collective-permute-start.3 = (bf16[224,1024]{1,0:T(8,128)(2,1)S(1)}, bf16[224,1024]{1,0:T(8,128)(2,1)}, u32[]{:S(2)}, u32[]{:S(2)}) collective-permute-start(bf16[224,1024]{1,0:T(8,128)(2,1)S(1)} %copy-done.1), channel_id=1, source_target_pairs={{64,0},{96,32},{65,1},{97,33},{66,2},{98,34},{67,3},{99,35},{68,4}... | collective-permute-start | bytes 1376264 | tf_op jit(solution)/shard_map/ppermute | solution.py:213
  234.7 73.3 %collective-permute-start.8 = (f32[224,1024]{1,0:T(8,128)}, f32[224,1024]{1,0:T(8,128)}, u32[]{:S(2)}, u32[]{:S(2)}) collective-permute-start(f32[224,1024]{1,0:T(8,128)} %get-tuple-element.26), channel_id=1, source_target_pairs={{0,96},{1,97},{2,98},{3,99},{4,100},{5,101},{6,102},{7,103},{8,104... | collective-permute-start | bytes 2752520 | tf_op jit(solution)/shard_map/ppermute | solution.py:218
  251.1 56.9 %collective-permute-start.7 = (f32[224,1024]{1,0:T(8,128)}, f32[224,1024]{1,0:T(8,128)}, u32[]{:S(2)}, u32[]{:S(2)}) collective-permute-start(f32[224,1024]{1,0:T(8,128)} %get-tuple-element.25), channel_id=1, source_target_pairs={{0,64},{32,96},{1,65},{33,97},{2,66},{34,98},{3,67},{35,99},{4,68}... | collective-permute-start | bytes 2752520 | tf_op jit(solution)/shard_map/ppermute | solution.py:218
  253.4 54.6 %collective-permute-start.1 = (f32[224,1024]{1,0:T(8,128)}, f32[224,1024]{1,0:T(8,128)}, u32[]{:S(2)}, u32[]{:S(2)}) collective-permute-start(f32[224,1024]{1,0:T(8,128)} %get-tuple-element.17), channel_id=1, source_target_pairs={{0,32},{32,64},{64,96},{1,33},{33,65},{65,97},{2,34},{34,66},{66,9... | collective-permute-start | bytes 2752520 | tf_op jit(solution)/shard_map/ppermute | solution.py:218
  255.8 35.8 %collective-permute-start.2 = (f32[16,224]{1,0:T(8,128)S(1)}, f32[16,224]{1,0:T(8,128)S(1)}, u32[]{:S(2)}, u32[]{:S(2)}) collective-permute-start(f32[16,224]{1,0:T(8,128)S(1)} %pad_maximum_fusion.2), channel_id=1, source_target_pairs={{0,32},{32,64},{64,96},{1,33},{33,65},{65,97},{2,34},{34,66},{66,9... | collective-permute-start | bytes 43016 | tf_op jit(solution)/shard_map/ppermute | solution.py:218
  257.8 49.5 %collective-permute-start.6 = (f32[16,224]{1,0:T(8,128)S(1)}, f32[16,224]{1,0:T(8,128)S(1)}, u32[]{:S(2)}, u32[]{:S(2)}) collective-permute-start(f32[16,224]{1,0:T(8,128)S(1)} %pad_maximum_fusion.4), channel_id=1, source_target_pairs={{0,96},{1,97},{2,98},{3,99},{4,100},{5,101},{6,102},{7,103},{8,104... | collective-permute-start | bytes 43016 | tf_op jit(solution)/shard_map/ppermute | solution.py:218
  291.6 15.7 %collective-permute-start.4 = (f32[16,224]{1,0:T(8,128)S(1)}, f32[16,224]{1,0:T(8,128)S(1)}, u32[]{:S(2)}, u32[]{:S(2)}) collective-permute-start(f32[16,224]{1,0:T(8,128)S(1)} %pad_maximum_fusion.3), channel_id=1, source_target_pairs={{0,64},{32,96},{1,65},{33,97},{2,66},{34,98},{3,67},{35,99},{4,68}... | collective-permute-start | bytes 43016 | tf_op jit(solution)/shard_map/ppermute | solution.py:218
  308.9 7.2 %slice-start = ((s8[8388608]{0:T(1024)(128)(4,1)}), s8[4194304]{0:T(1024)(128)(4,1)S(1)}, s32[]{:S(2)}) async-start(s8[8388608]{0:T(1024)(128)(4,1)} %bitcast.142), calls=%async_computation.10 | async-start | bytes 8388608
  309.5 6.6 %slice-start.1 = ((s8[8388608]{0:T(1024)(128)(4,1)}), s8[4194304]{0:T(1024)(128)(4,1)S(1)}, s32[]{:S(2)}) async-start(s8[8388608]{0:T(1024)(128)(4,1)} %bitcast.142), calls=%async_computation.11 | async-start | bytes 8388608
  312.7 3.5 copy-start.5
  312.7 3.5 copy-start.8
  318.3 46.1 %reduce-scatter.3.cloned.1.call-start = ((), (), s32[]{:S(2)}) async-start(), calls=%async_computation.8 | async-start | bytes 1146880 | tf_op jit(solution)/shard_map/reduce_scatter | solution.py:257
  (4 other events, 4.8 us)
Sparse Core Ops, SparseCore 0:
  9.6 95.1 all-gather.2
  107.1 85.7 all-gather.4
  318.4 22.7 reduce-scatter.4
  343.5 20.7 reduce-scatter.2
